TPU v7x, 32 devices: a whole 2x2x4 slice. The times are simulated.
32 devices in a mesh: group: 2 (over y), head: 4 (over z), req: 4 (over x, core).
Axes of the slice: x: 2, y: 2, z: 4, core: 2. Of those that a mesh axis runs over, the one named last changes fastest.
Arguments:
- x_input: bfloat16 [128, 8, 16384], P(('group', 'req'), None, 'head'), parts along dimension 0, may hold values from -6 to 6
- z_input: bfloat16 [128, 8, 16384], P(('group', 'req'), None, 'head'), parts along dimension 0, may hold values from -6 to 6
- bc_input: bfloat16 [128, 8, 4096], P(('group', 'req')), parts along dimension 0, may hold values from -6 to 6
- dt_input: float32 [128, 8, 256], P(('group', 'req'), None, 'head'), parts along dimension 0, may hold values from -6 to 6
- conv_x_state: bfloat16 [128, 3, 16384], P(('group', 'req'), None, 'head'), parts along dimension 0, may hold values from -6 to 6
- conv_bc_state: bfloat16 [128, 3, 4096], P(('group', 'req')), parts along dimension 0, may hold values from -6 to 6
- ssm_state: bfloat16 [128, 256, 64, 256], P(('group', 'req'), 'head'), parts along dimension 0, may hold values from -6 to 6
- accepted: int32 [128], P(('group', 'req')), parts along dimension 0, may hold values from 0 to 8
- next_owner: int32 [128], P('group'), parts along dimension 0, may hold values from 0 to 3, as said below
- conv_x_weight: float32 [4, 16384], P(None, 'head'), may hold values from -3 to 3
- conv_x_bias: float32 [16384], P('head'), may hold values from -3 to 3
- conv_bc_weight: float32 [4, 4096], replicated, may hold values from -3 to 3
- conv_bc_bias: float32 [4096], replicated, may hold values from -3 to 3
- dt_bias: float32 [256], P('head'), may hold values from -3 to 0
- a_log: float32 [256], P('head'), may hold values from -4 to 1
- d_skip: float32 [256], P('head'), may hold values from 0.5 to 1.5
- norm_gain: float32 [16384], P('head'), may hold values from 0.5 to 1.5
- out_weight: bfloat16 [16384, 8192], P('head'), may hold values from -0.0625 to 0.0625
Outputs:
- mixed: bfloat16 [128, 8, 8192], P(('group', 'req'), None, 'head'), parts along dimension 0
- new_ssm_state: bfloat16 [128, 256, 64, 256], P(('group', 'req'), 'head'), parts along dimension 0
- new_conv_x_state: bfloat16 [128, 3, 16384], P(('group', 'req'), None, 'head'), parts along dimension 0
- new_conv_bc_state: bfloat16 [128, 3, 4096], P(('group', 'req')), parts along dimension 0
There are 2 independent parts, one for each index of `group`. A program takes and returns all parts, laid end to end along the dimension named above; an argument that names none is the same for every part. Nothing has to cross between parts.
Inputs may be any that keep to these rules, and one draw needn't show every extreme that they name: Every index of req is next_owner of exactly 16 requests, and at most 8 of the requests of one index of req (requests i * 16 .. i * 16 + 15) share one next_owner.
All inputs are finite; a program needn't handle non-finite values.
Results may differ from a plain program's by a relative error of at most 0.0049.
Values may be sent and summed in bfloat16 or wider, within the bound.
No kernel may reach another device: no remote copies, remote signals or barrier semaphores. Data moves between devices by JAX's collectives and lax.ppermute only.
A program may use at most 576 MiB of HBM per device.

v0:
```python
import jax
import jax.numpy as jnp
from jax import lax
from jax.sharding import PartitionSpec as P

D = 8192
H = 256
P_SIZE = 64
N = 256
G = 8
K = 4
L = 8


epsilon = 1e-05
highest = lax.Precision.HIGHEST


def conv_window(history, inputs, weight, bias_vector):
    joined = jnp.concatenate([history, inputs], axis=1)
    widened = joined.astype(jnp.float32)
    accumulated = bias_vector[None, None, :] + weight[0][None, None, :] * widened[:, 0:L, :]
    for offset in range(1, K):
        accumulated = (
            accumulated + weight[offset][None, None, :] * widened[:, offset : offset + L, :]
        )
    return (jax.nn.silu(accumulated), joined)


def on_device(
    x_input,
    z_input,
    bc_input,
    dt_input,
    conv_x_state,
    conv_bc_state,
    ssm_state,
    accepted,
    next_owner,
    conv_x_weight,
    conv_x_bias,
    conv_bc_weight,
    conv_bc_bias,
    dt_bias,
    a_log,
    d_skip,
    norm_gain,
    out_weight,
):
    local_requests = x_input.shape[0]
    local_heads = dt_input.shape[2]
    head_index = lax.axis_index("head")
    req_index = lax.axis_index("req")
    all_requests = next_owner.shape[0]
    heads_group = H // G
    x_conv, x_joined = conv_window(conv_x_state, x_input, conv_x_weight, conv_x_bias)
    bc_conv, bc_joined = conv_window(conv_bc_state, bc_input, conv_bc_weight, conv_bc_bias)
    step_size = jax.nn.softplus(dt_input + dt_bias[None, None, :])
    log_decay = -jnp.exp(a_log)[None, None, :] * step_size
    global_heads = head_index * local_heads + jnp.arange(local_heads, dtype=jnp.int32)
    group_pick = (
        global_heads[:, None] // heads_group == jnp.arange(G, dtype=jnp.int32)[None, :]
    ).astype(jnp.float32)
    b_groups = bc_conv[:, :, : G * N].reshape(local_requests, L, G, N)
    c_groups = bc_conv[:, :, G * N :].reshape(local_requests, L, G, N)
    b_heads = jnp.einsum("rlgn,hg->rlhn", b_groups, group_pick, precision=highest)
    c_heads = jnp.einsum("rlgn,hg->rlhn", c_groups, group_pick, precision=highest)
    x_heads = x_conv.reshape(local_requests, L, local_heads, P_SIZE)
    initial = ssm_state.astype(jnp.float32)
    inclusive = jnp.cumsum(log_decay, axis=1)
    before = jnp.concatenate(
        [jnp.zeros((local_requests, 1, local_heads), jnp.float32), inclusive], axis=1
    )
    positions = jnp.arange(L, dtype=jnp.int32)
    causal = positions[:, None] >= positions[None, :]
    by_head = inclusive.transpose(0, 2, 1)
    differences = by_head[:, :, :, None] - by_head[:, :, None, :]
    pair_decay = jnp.exp(jnp.where(causal[None, None], differences, -jnp.inf))
    scores = jnp.einsum("rthn,rshn->rhts", c_heads, b_heads, precision=highest)
    weights = scores * pair_decay * step_size.transpose(0, 2, 1)[:, :, None, :]
    within = jnp.einsum("rhts,rshp->rthp", weights, x_heads, precision=highest)
    carried = jnp.exp(inclusive)[:, :, :, None] * jnp.einsum(
        "rhpn,rthn->rthp", initial, c_heads, precision=highest
    )
    y_values = within + carried + d_skip[None, None, :, None] * x_heads
    count_pick = (jnp.arange(L + 1, dtype=jnp.int32)[None, :] == accepted[:, None]).astype(
        jnp.float32
    )
    reached = jnp.einsum("ra,rah->rh", count_pick, before, precision=highest)
    valid = positions[None, :] < accepted[:, None]
    exponent = jnp.where(valid[:, :, None], reached[:, None, :] - inclusive, -jnp.inf)
    token_weight = jnp.exp(exponent) * step_size
    retained = jnp.exp(reached)[:, :, None, None] * initial + jnp.einsum(
        "rsh,rshp,rshn->rhpn", token_weight, x_heads, b_heads, precision=highest
    )
    retained = retained.astype(jnp.bfloat16)
    gated = y_values.reshape(local_requests, L, local_heads * P_SIZE) * jax.nn.silu(
        z_input.astype(jnp.float32)
    )
    blocks = gated.reshape(local_requests, L, local_heads, P_SIZE)
    inverse_rms = lax.rsqrt(jnp.mean(blocks * blocks, axis=3, keepdims=True) + epsilon)
    normed = (
        (blocks * inverse_rms).reshape(local_requests, L, local_heads * P_SIZE)
        * norm_gain[None, None, :]
    ).astype(jnp.bfloat16)
    partial_terms = jnp.dot(
        normed.reshape(local_requests * L, local_heads * P_SIZE),
        out_weight,
        preferred_element_type=jnp.float32,
    )
    share_width = D // lax.axis_size("head")
    summed = lax.psum(partial_terms, "head")
    share = lax.dynamic_slice_in_dim(summed, head_index * share_width, share_width, 1)
    mixed = share.astype(jnp.bfloat16).reshape(local_requests, L, share_width)
    window_rows = jnp.arange(K - 1 + L, dtype=jnp.int32)
    row_pick = (
        window_rows[None, None, :]
        == accepted[:, None, None] + jnp.arange(K - 1, dtype=jnp.int32)[None, :, None]
    ).astype(jnp.bfloat16)
    kept_x = jnp.einsum(
        "rkt,rtc->rkc", row_pick, x_joined, preferred_element_type=jnp.float32
    ).astype(jnp.bfloat16)
    kept_bc = jnp.einsum(
        "rkt,rtc->rkc", row_pick, bc_joined, preferred_element_type=jnp.float32
    ).astype(jnp.bfloat16)
    state_flat = retained.reshape(local_requests, -1)
    conv_x_flat = kept_x.reshape(local_requests, -1)
    conv_bc_flat = kept_bc.reshape(local_requests, -1)
    request_ids = jnp.arange(all_requests, dtype=jnp.int32)
    same_owner = next_owner[:, None] == next_owner[None, :]
    earlier = request_ids[None, :] < request_ids[:, None]
    position = jnp.sum((same_owner & earlier).astype(jnp.int32), axis=1)
    slot_rows = jnp.arange(local_requests, dtype=jnp.int32)
    arrive = (
        (next_owner[None, :] == req_index) & (position[None, :] == slot_rows[:, None])
    ).astype(jnp.bfloat16)
    new_state_flat = jnp.dot(
        arrive,
        lax.all_gather(state_flat, "req", axis=0, tiled=True),
        preferred_element_type=jnp.float32,
    ).astype(jnp.bfloat16)
    new_conv_x_flat = jnp.dot(
        arrive,
        lax.all_gather(conv_x_flat, "req", axis=0, tiled=True),
        preferred_element_type=jnp.float32,
    ).astype(jnp.bfloat16)
    new_conv_bc_flat = jnp.dot(
        arrive,
        lax.all_gather(conv_bc_flat, "req", axis=0, tiled=True),
        preferred_element_type=jnp.float32,
    ).astype(jnp.bfloat16)
    new_ssm_state = new_state_flat.reshape(retained.shape)
    new_conv_x_state = new_conv_x_flat.reshape(kept_x.shape)
    new_conv_bc_state = new_conv_bc_flat.reshape(kept_bc.shape)
    return (mixed, new_ssm_state, new_conv_x_state, new_conv_bc_state)


def solution(mesh):
    placed = (
        P(("group", "req"), None, "head"),
        P(("group", "req"), None, "head"),
        P(("group", "req"), None, None),
        P(("group", "req"), None, "head"),
        P(("group", "req"), None, "head"),
        P(("group", "req"), None, None),
        P(("group", "req"), "head", None, None),
        P(("group", "req")),
        P("group"),
        P(None, "head"),
        P("head"),
        P(),
        P(),
        P("head"),
        P("head"),
        P("head"),
        P("head"),
        P("head", None),
    )
    return jax.shard_map(
        on_device,
        mesh=mesh,
        in_specs=placed,
        out_specs=(
            P(("group", "req"), None, "head"),
            P(("group", "req"), "head", None, None),
            P(("group", "req"), None, "head"),
            P(("group", "req"), None, None),
        ),
        check_vma=False,
    )
```

profile of v0, /device:TPU:0, one launch (start us, length us, event | category | flops | bytes accessed | tf_op | source)
XLA Modules:
  0.0 1015.5 jit_solution(1302443822829279630)
XLA Ops:
  7.2 0.0 copy-start.6
  7.2 0.0 copy-start.4
  7.2 0.0 all-gather.8.cloned.1.call-start
  7.2 0.8 iota_add_fusion
  8.1 1.3 copy.48
  9.4 2.0 convolution_convert_fusion.3
  11.4 0.0 copy-start.13
  11.4 1.0 copy.73
  12.5 0.0 all-gather.8.cloned.1.call-update
  12.5 0.0 all-gather.6.cloned.1.call-start
  12.6 0.0 copy-done.6
  12.6 0.3 copy.47
  12.9 0.8 convolution_convert_fusion.4
  13.7 0.0 copy-start.5
  13.7 1.0 copy.72
  14.8 0.0 all-gather.6.cloned.1.call-update
  14.8 0.0 all-gather.4.cloned.1.call-start
  14.9 0.1 fusion.56
  14.9 0.1 iota_compare_fusion.4
  15.0 2.6 fusion.36
  17.7 0.0 copy-start.9
  17.7 0.0 copy-start.10
  17.7 0.0 copy-start.11
  17.7 2.7 fusion.35
  20.4 0.1 broadcast_multiply_fusion.1
  20.5 0.1 reduce_window_sum.11
  20.6 0.2 fusion.46
  20.9 0.1 exponential_multiply_fusion
  21.0 7.4 divide_multiply_fusion.1
  28.4 0.0 copy-start.12
  28.4 3.0 reshape.178
  31.4 7.0 divide_multiply_fusion
  38.5 1.2 fusion.75
  39.6 1.4 copy-done.2
  41.0 2.6 broadcast_multiply_fusion
  43.7 5.8 convolution_bitcast_fusion
  49.4 72.6 %add_convert_fusion = bf16[16,64,64,256]{3,2,1,0:T(8,128)(2,1)} fusion(bf16[16,64,64,256]{3,2,1,0:T(8,128)(2,1)} %param.24, f32[16,64]{1,0:T(8,128)S(1)} %exp.40, f32[16,8,64,256]{3,2,1,0:T(8,128)} %convolution_bitcast_fusion, f32[16,8,64,64]{3,2,1,0:T(8,128)} %broadcast_multiply_fusion), kind=kOutput, calls=%fused_computation.1 | convolution fusion | flops 1677721600 | bytes 77598720 | tf_op jit(solution)/shard_map/rsh,rshp,rshn->rhpn/dot_general | solution.py:93
  122.1 31.2 %copy.70 = bf16[2,8,4096,256]{3,1,2,0:T(8,128)(2,1)} copy(bf16[2,8,4096,256]{3,2,1,0:T(8,128)(2,1)} %bitcast.78) | data formatting | bytes 67108864
  153.3 0.0 all-gather.4.cloned.1.call-update
  153.3 1.0 copy.53
  154.3 0.2 copy.55
  154.5 0.2 copy.51
  154.7 8.9 convolution_bitcast_fusion.1
  163.6 21.0 %fusion.1 = f32[16,64,8,8]{3,2,1,0:T(8,128)} fusion(f32[16,8,64,256]{3,2,1,0:T(8,128)S(1)} %copy-done, f32[16,8,64,256]{3,2,1,0:T(8,128)} %convolution_bitcast_fusion.1), kind=kOutput, calls=%fused_computation.5 | convolution fusion | flops 201326592 | bytes 17039360 | tf_op jit(solution)/shard_map/rthn,rshn->rhts/dot_general | solution.py:79
  184.6 16.2 %fusion.9 = f32[16,64,64,8]{2,3,1,0:T(8,128)} fusion(f32[16,64,8,8]{3,2,1,0:T(8,128)} %fusion.1, f32[16,8,64,64]{3,2,1,0:T(8,128)} %reshape.178, f32[16,64,8]{2,1,0:T(8,128)} %copy.53, f32[16,64,8]{2,1,0:T(8,128)S(1)} %copy.51, pred[8,8]{1,0:T(8,128)(4,1)S(1)} %iota_compare_fusion.7), kind=kOutput, calls=%fused_computation.16 | convolution fusion | flops 50593792 | bytes 4522048 | tf_op jit(solution)/shard_map/rhts,rshp->rthp/dot_general | solution.py:81
  200.9 35.1 %fusion.7 = f32[16,8,64,64]{3,1,2,0:T(8,128)} fusion(f32[16,64,64,8]{2,3,1,0:T(8,128)} %fusion.9, f32[16,8,64,64]{3,2,1,0:T(8,128)} %reshape.178, bf16[16,64,64,256]{3,2,1,0:T(8,128)(2,1)} %param.24, f32[16,8,64,256]{3,2,1,0:T(8,128)S(1)} %copy-done.1, f32[64]{0:T(128)S(1)} %copy-done.14, f32[16,8,64]{1,2,0:T(8,128)S(1)} %copy.55), kind=kOutput, calls=%fused_computation.14 | convolution fusion | flops 1612709888 | bytes 48267520 | tf_op jit(solution)/shard_map/rhpn,rthn->rthp/dot_general | solution.py:82
  236.0 5.4 copy.58
  241.5 4.2 reshape.181
  245.7 1.9 fusion.74
  247.6 4.7 mul.209
  252.2 3.3 reduce_sum.18
  255.6 2.6 mul.210
  258.3 4.8 mul.211
  263.0 26.6 %fusion.38 = f32[128,8192]{1,0:T(8,128)} fusion(bf16[4096,8192]{1,0:T(8,128)(2,1)} %param.35, f32[16,8,4096]{2,1,0:T(8,128)} %mul.211, f32[4096]{0:T(1024)S(1)} %copy-done.8, f32[16,8,4096]{2,1,0:T(8,128)S(1)} %reshape.181, bf16[16,8,4096]{2,1,0:T(8,128)(2,1)S(1)} %copy-done.3), kind=kOutput, calls=%fused_computation.61 | convolution fusion | flops 8594653184 | bytes 76562432 | tf_op jit(solution)/shard_map/dot_general | solution.py:106
  289.7 0.2 convert_reduce_fusion
  289.9 150.2 %all-reduce.2 = bf16[128,8192]{1,0:T(8,128)(2,1)S(1)} all-reduce(f32[128,8192]{1,0:T(8,128)} %fusion.38), channel_id=1, replica_groups=mesh['group'=2,'head'=4,'req'=4] {'head'}, use_global_device_ids=true, to_apply=%region_2.3 | all-reduce | flops 1048576 | bytes 6291456 | tf_op jit(solution)/shard_map/psum | solution.py:112
  440.1 0.8 fusion.45
  440.9 1.7 convolution_convert_fusion.1
  442.6 0.8 copy.101
  443.4 1.7 convolution_convert_fusion.2
  445.1 0.8 copy.102
  445.9 485.2 %all-gather.4.cloned.1.call-done = bf16[64,1048576]{1,0:T(8,128)(2,1)} async-done(((bf16[16,1048576]{1,0:T(8,128)(2,1)}), bf16[64,1048576]{1,0:T(8,128)(2,1)}) %all-gather.4.cloned.1.call-update) | async-done | bytes 134217744 | tf_op jit(solution)/shard_map/all_gather | solution.py:139
  931.1 54.6 %convolution_convert_fusion = bf16[16,1048576]{1,0:T(8,128)(2,1)} fusion(bf16[64,1048576]{1,0:T(8,128)(2,1)} %all-gather.4.cloned.1.call-done, s32[64]{0:T(128)S(1)} %convert_reduce_fusion, pred[64]{0:T(512)(128)(4,1)S(1)} %broadcast_compare_fusion), kind=kOutput, calls=%fused_computation | convolution fusion | flops 2164262912 | bytes 167772480 | tf_op jit(solution)/shard_map/dot_general | solution.py:137
  985.7 23.1 %copy.71 = bf16[2,8,4096,256]{3,2,1,0:T(8,128)(2,1)} copy(bf16[2,8,4096,256]{3,1,2,0:T(8,128)(2,1)} %bitcast.79) | data formatting | bytes 67108864
  (36 shorter events, 0.2 us)
Async XLA Ops:
  7.2 5.4 copy-start.6
  7.2 5.7 copy-start.4
  7.2 433.7 %all-gather.8.cloned.1.call-start = ((), (), s32[]{:S(2)}) async-start(), calls=%async_computation.2 | async-start | bytes 1966080 | tf_op jit(solution)/shard_map/all_gather | solution.py:149
  11.4 3.4 copy-start.13
  12.5 430.9 %all-gather.6.cloned.1.call-start = ((), (), s32[]{:S(2)}) async-start(), calls=%async_computation.1 | async-start | bytes 1966080 | tf_op jit(solution)/shard_map/all_gather | solution.py:144
  13.7 3.9 copy-start.5
  14.8 916.3 %all-gather.4.cloned.1.call-start = ((), (), s32[]{:S(2)}) async-start(), calls=%async_computation | async-start | bytes 167772160 | tf_op jit(solution)/shard_map/all_gather | solution.py:139
  17.7 2.8 copy-start.16
  17.7 2.8 copy-start.7
  17.7 2.8 copy-start.15
  17.7 3.1 copy-start.9
  17.7 3.2 copy-start.10
  17.7 3.4 copy-start.11
  28.4 3.0 copy-start.12
  38.5 2.6 copy-start.2
  154.7 8.9 copy-start
  184.6 16.2 %copy-start.1 = (f32[16,8,64,256]{3,2,1,0:T(8,128)S(1)}, f32[16,8,64,256]{3,2,1,0:T(8,128)}, u32[]{:S(2)}) copy-start(f32[16,8,64,256]{3,2,1,0:T(8,128)} %convolution_bitcast_fusion.1) | copy-start | bytes 25165828
  184.6 16.2 %copy-start.14 = (f32[64]{0:T(128)S(1)}, f32[64]{0:T(128)}, u32[]{:S(2)}) copy-start(f32[64]{0:T(128)} %param.33) | copy-start | bytes 772
  241.5 4.2 copy-start.3
  258.3 4.8 copy-start.8
  263.0 26.6 %copy-start.17 = (s32[64]{0:T(128)S(1)}, s32[64]{0:T(128)}, u32[]{:S(2)}) copy-start(s32[64]{0:T(128)} %param.26) | copy-start | bytes 772
Sparse Core Ops, SparseCore 0:
  12.6 22.3 all-gather.7
  37.1 19.6 all-gather.5
  153.4 777.6 all-gather.3
where the time goes:
time: 1020 us
  waiting for transfers between devices  485 us (48%)
  matrix products  247 us (24%)
  blocking collectives  150 us (15%)
  local copies, waits for them, and re-layouts  89.3 us (9%)
  other arithmetic  29 us (3%)
  between operations  14.3 us (1%)
    all_gather x1, waiting for transfers between devices, on_device(): lax.all_gather(state_flat, 'req', axis=0, tiled=True)  485 us
    psum x1, blocking collectives, on_device(): summed = lax.psum(partial_terms, 'head')  150 us
    dot_general x1, matrix products, on_device(): jnp.einsum('rsh,rshp,rshn->rhpn', token_weight, x_heads, b_heads, precisi...  72.6 us
    unnamed x42, local copies, waits for them, and re-layouts  59.5 us
    dot_general x1, matrix products, on_device(): jnp.dot(arrive, lax.all_gather(state_flat, 'req', axis=0, tiled=True), pr...  54.6 us
    dot_general x1, matrix products, on_device(): jnp.einsum('rhpn,rthn->rthp', initial, c_heads, precision=highest)  35.1 us
    dot_general x1, matrix products, on_device(): jnp.dot(normed.reshape(local_requests * L, local_heads * P_SIZE), out_wei...  26.6 us
    dot_general x1, matrix products, on_device(): scores = jnp.einsum('rthn,rshn->rhts', c_heads, b_heads, precision=highest)  21 us
  transfers between devices with their start and end apart: 3, of which 1 were waited for; matrix products, arithmetic and copies ran while one was open for 28% of the time, Pallas kernels for 0%

commit v1 on v0

--- a/solution.py
+++ b/solution.py
@@ -10,6 +10,7 @@
 G = 8
 K = 4
 L = 8
+CAP = 8
 
 
 epsilon = 1e-05
@@ -109,8 +110,7 @@
         preferred_element_type=jnp.float32,
     )
     share_width = D // lax.axis_size("head")
-    summed = lax.psum(partial_terms, "head")
-    share = lax.dynamic_slice_in_dim(summed, head_index * share_width, share_width, 1)
+    share = lax.psum_scatter(partial_terms, "head", scatter_dimension=1, tiled=True)
     mixed = share.astype(jnp.bfloat16).reshape(local_requests, L, share_width)
     window_rows = jnp.arange(K - 1 + L, dtype=jnp.int32)
     row_pick = (
@@ -123,35 +123,36 @@
     kept_bc = jnp.einsum(
         "rkt,rtc->rkc", row_pick, bc_joined, preferred_element_type=jnp.float32
     ).astype(jnp.bfloat16)
-    state_flat = retained.reshape(local_requests, -1)
-    conv_x_flat = kept_x.reshape(local_requests, -1)
-    conv_bc_flat = kept_bc.reshape(local_requests, -1)
+    requests_per_owner = local_requests
+    owners = lax.axis_size("req")
+    cap = min(CAP, local_requests)
     request_ids = jnp.arange(all_requests, dtype=jnp.int32)
+    source = request_ids // requests_per_owner
     same_owner = next_owner[:, None] == next_owner[None, :]
     earlier = request_ids[None, :] < request_ids[:, None]
-    position = jnp.sum((same_owner & earlier).astype(jnp.int32), axis=1)
+    rank_at_owner = jnp.sum((same_owner & earlier).astype(jnp.int32), axis=1)
+    same_source = source[:, None] == source[None, :]
+    rank_in_pair = jnp.sum((same_owner & earlier & same_source).astype(jnp.int32), axis=1)
+    local_owner = lax.dynamic_slice_in_dim(next_owner, req_index * local_requests, local_requests)
+    local_rank = lax.dynamic_slice_in_dim(rank_in_pair, req_index * local_requests, local_requests)
     slot_rows = jnp.arange(local_requests, dtype=jnp.int32)
-    arrive = (
-        (next_owner[None, :] == req_index) & (position[None, :] == slot_rows[:, None])
-    ).astype(jnp.bfloat16)
-    new_state_flat = jnp.dot(
-        arrive,
-        lax.all_gather(state_flat, "req", axis=0, tiled=True),
-        preferred_element_type=jnp.float32,
-    ).astype(jnp.bfloat16)
-    new_conv_x_flat = jnp.dot(
-        arrive,
-        lax.all_gather(conv_x_flat, "req", axis=0, tiled=True),
-        preferred_element_type=jnp.float32,
-    ).astype(jnp.bfloat16)
-    new_conv_bc_flat = jnp.dot(
-        arrive,
-        lax.all_gather(conv_bc_flat, "req", axis=0, tiled=True),
-        preferred_element_type=jnp.float32,
-    ).astype(jnp.bfloat16)
-    new_ssm_state = new_state_flat.reshape(retained.shape)
-    new_conv_x_state = new_conv_x_flat.reshape(kept_x.shape)
-    new_conv_bc_state = new_conv_bc_flat.reshape(kept_bc.shape)
+    chosen = (local_owner[None, None, :] == jnp.arange(owners, dtype=jnp.int32)[:, None, None]) & (
+        local_rank[None, None, :] == jnp.arange(cap, dtype=jnp.int32)[None, :, None]
+    )
+    send_index = jnp.sum(jnp.where(chosen, slot_rows[None, None, :], 0), axis=2).reshape(-1)
+    arriving = (next_owner[None, :] == req_index) & (rank_at_owner[None, :] == slot_rows[:, None])
+    receive_index = jnp.sum(
+        jnp.where(arriving, source[None, :] * cap + rank_in_pair[None, :], 0), axis=1
+    )
+
+    def hand_over(values):
+        outgoing = jnp.take(values, send_index, axis=0, mode="clip")
+        incoming = lax.all_to_all(outgoing, "req", 0, 0, tiled=True)
+        return jnp.take(incoming, receive_index, axis=0, mode="clip")
+
+    new_ssm_state = hand_over(retained)
+    new_conv_x_state = hand_over(kept_x)
+    new_conv_bc_state = hand_over(kept_bc)
     return (mixed, new_ssm_state, new_conv_x_state, new_conv_bc_state)
 
 

time: 1020 us -> 1090 us (1.069); the launches traced: 1020 us -> 1070 us
  blocking collectives: 150 us -> 0 us
  waiting for transfers between devices: 485 us -> 591 us
  local copies, waits for them, and re-layouts: 89.3 us -> 173 us
  matrix products: 247 us -> 178 us
  other arithmetic: 29 us -> 93.8 us
  starting transfers between devices: 0.12 us -> 21.1 us
    all_to_all x0 -> x3, waiting for transfers between devices: none -> 517 us  [hand_over(): incoming = lax.all_to_all(outgoing, 'req', 0, 0, tiled=True)]
    all_gather x3 -> x0, waiting for transfers between devices: 485 us -> none  [the longest x1 485 us: on_device(): lax.all_gather(state_flat, 'req', axis=0, tiled=True)]
    psum x1 -> x0, blocking collectives: 150 us -> none  [on_device(): summed = lax.psum(partial_terms, 'head')]
    gather x0 -> x10, local copies, waits for them, and re-layouts: none -> 136 us  [the longest x5 69 us: hand_over(): return jnp.take(incoming, receive_index, axis=0, mode='clip')]
    reduce_scatter x0 -> x1, waiting for transfers between devices: none -> 74.1 us  [on_device(): lax.psum_scatter(partial_terms, 'head', scatter_dimension=1, tiled=True)]
    dot_general x3 -> x0, matrix products: 58.1 us -> none  [the longest x1 54.6 us: on_device(): jnp.dot(arrive, lax.all_gather(state_flat, 'req', axis=0, tiled=True), pr...]
    unnamed x42 -> x64, local copies, waits for them, and re-layouts: 59.5 us -> 8.81 us
    unnamed x0 -> x1, other arithmetic: none -> 44.5 us
  transfers between devices with their start and end apart: 3 -> 4, of which waited for: 1 -> 2; matrix products, arithmetic and copies ran while one was open for 28% -> 32% of each run, Pallas kernels for 0% -> 0%
where the time goes in v1:
time: 1090 us; the launch traced here: 1070 us
  waiting for transfers between devices  591 us (54%)
  matrix products  178 us (16%)
  local copies, waits for them, and re-layouts  173 us (16%)
  other arithmetic  93.8 us (9%)
  starting transfers between devices  21.1 us (2%)
  between operations  14.7 us (1%)
    all_to_all x3, waiting for transfers between devices, hand_over(): incoming = lax.all_to_all(outgoing, 'req', 0, 0, tiled=True)  517 us
    reduce_scatter x1, waiting for transfers between devices, on_device(): lax.psum_scatter(partial_terms, 'head', scatter_dimension=1, tiled=True)  74.1 us
    dot_general x1, matrix products, on_device(): jnp.einsum('rsh,rshp,rshn->rhpn', token_weight, x_heads, b_heads, precisi...  72.5 us
    gather x5, local copies, waits for them, and re-layouts, hand_over(): return jnp.take(incoming, receive_index, axis=0, mode='clip')  69 us
    gather x5, local copies, waits for them, and re-layouts, hand_over(): outgoing = jnp.take(values, send_index, axis=0, mode='clip')  67.4 us
    unnamed x1, other arithmetic  44.5 us
    dot_general x1, matrix products, on_device(): jnp.einsum('rhpn,rthn->rthp', initial, c_heads, precision=highest)  31.9 us
    dot_general x1, matrix products, on_device(): jnp.dot(normed.reshape(local_requests * L, local_heads * P_SIZE), out_wei...  26.6 us
  transfers between devices with their start and end apart: 4, of which 2 were waited for; matrix products, arithmetic and copies ran while one was open for 32% of the time, Pallas kernels for 0%

profile of v1, /device:TPU:0, one launch (start us, length us, event | category | flops | bytes accessed | tf_op | source)
XLA Modules:
  0.0 1070.8 jit_solution(5732053786943494728)
XLA Ops:
  7.2 0.7 dynamic_slice.6
  7.9 1.4 convert_reduce_fusion
  9.4 0.6 copy-done.27
  9.9 0.1 dynamic_slice.7
  10.0 0.2 select_reduce_fusion
  10.2 0.1 reshape.282
  10.3 0.7 iota_add_fusion
  11.0 1.4 copy.47
  12.4 2.0 convolution_convert_fusion.1
  14.5 2.4 gather_fusion
  16.9 4.3 all-to-all-start.1
  21.3 0.1 fusion.51
  21.4 0.1 iota_compare_fusion.5
  21.4 2.7 fusion.36
  24.3 0.2 fusion.45
  24.7 0.7 exponential_multiply_fusion
  25.4 1.1 copy.48
  26.5 7.0 divide_multiply_fusion.1
  33.6 3.0 reshape.242
  36.6 2.1 fusion.35
  38.7 1.3 divide_multiply_fusion
  40.0 1.1 fusion.67
  41.1 1.4 copy-done
  42.6 2.6 broadcast_multiply_fusion
  45.1 5.7 convolution_bitcast_fusion
  50.9 72.5 %add_convert_fusion = bf16[16,64,64,256]{3,2,1,0:T(8,128)(2,1)} fusion(bf16[16,64,64,256]{3,2,1,0:T(8,128)(2,1)} %param.24, f32[16,64]{1,0:T(8,128)S(1)} %exp.40, f32[16,8,64,256]{3,2,1,0:T(8,128)} %convolution_bitcast_fusion, f32[16,8,64,64]{3,2,1,0:T(8,128)} %broadcast_multiply_fusion), kind=kOutput, calls=%fused_computation.9 | convolution fusion | flops 1677721600 | bytes 77598720 | tf_op jit(solution)/shard_map/rsh,rshp,rshn->rhpn/dot_general | solution.py:94
  123.4 25.2 %fusion.66 = (bf16[16,64,64,128]{3,2,1,0:T(8,128)(2,1)}, bf16[16,64,64,128]{3,2,1,0:T(8,128)(2,1)}) fusion(bf16[16,64,64,256]{3,2,1,0:T(8,128)(2,1)} %add_convert_fusion), kind=kLoop, calls=%fused_computation.124 | loop fusion | bytes 67108864 | tf_op jit(solution)/shard_map/jit(_take)/gather | solution.py:149
  148.6 0.8 convolution_convert_fusion
  149.4 2.4 gather_fusion.2
  151.8 18.7 %gather_fusion.4 = bf16[32,64,64,128]{3,2,1,0:T(8,128)(2,1)} fusion(bf16[16,64,64,128]{3,2,1,0:T(8,128)(2,1)} %get-tuple-element.20, s32[1024]{0:T(1024)S(1)} %pad_clamp_fusion.1), kind=kCustom, calls=%fused_computation.4 | custom fusion | bytes 67108992 | tf_op jit(solution)/shard_map/jit(_take)/gather | solution.py:149
  170.5 18.7 %gather_fusion.5 = bf16[32,64,64,128]{3,2,1,0:T(8,128)(2,1)} fusion(bf16[16,64,64,128]{3,2,1,0:T(8,128)(2,1)} %get-tuple-element.21, s32[1024]{0:T(1024)S(1)} %pad_clamp_fusion.1), kind=kCustom, calls=%fused_computation.5 | custom fusion | bytes 67108992 | tf_op jit(solution)/shard_map/jit(_take)/gather | solution.py:149
  189.2 3.6 all-to-all-start.2
  192.8 44.5 %pad_maximum_fusion = bf16[32,64,64,256]{3,2,1,0:T(8,128)(2,1)} fusion(bf16[32,64,64,128]{3,2,1,0:T(8,128)(2,1)} %gather_fusion.5, bf16[32,64,64,128]{3,2,1,0:T(8,128)(2,1)} %gather_fusion.4), kind=kLoop, calls=%fused_computation.8 | loop fusion | flops 134217728 | bytes 134217728
  237.4 1.0 copy-done.4
  238.4 13.1 %all-to-all-start = ((bf16[32,64,64,256]{3,2,1,0:T(8,128)(2,1)}), bf16[32,64,64,256]{3,2,1,0:T(8,128)(2,1)}, u32[]{:S(2)}, u32[]{:S(2)}) async-start(bf16[32,64,64,256]{3,2,1,0:T(8,128)(2,1)} %pad_maximum_fusion), calls=%async_computation.1 | async-start | bytes 134217728 | tf_op jit(solution)/shard_map/all_to_all | solution.py:150
  251.6 1.0 copy.53
  252.6 0.2 copy.55
  252.8 0.2 copy.51
  253.0 4.7 convolution_bitcast_fusion.1
  257.7 19.7 %fusion.1 = f32[16,64,8,8]{3,2,1,0:T(8,128)} fusion(f32[16,8,64,256]{3,2,1,0:T(8,128)} %convolution_bitcast_fusion, f32[16,8,64,256]{3,2,1,0:T(8,128)S(1)} %convolution_bitcast_fusion.1), kind=kOutput, calls=%fused_computation.12 | convolution fusion | flops 201326592 | bytes 17039360 | tf_op jit(solution)/shard_map/rthn,rshn->rhts/dot_general | solution.py:80
  277.4 13.9 %fusion.9 = f32[16,64,64,8]{2,3,1,0:T(8,128)} fusion(f32[16,64,8,8]{3,2,1,0:T(8,128)} %fusion.1, f32[16,8,64,64]{3,2,1,0:T(8,128)} %reshape.242, f32[16,64,8]{2,1,0:T(8,128)} %copy.53, f32[16,64,8]{2,1,0:T(8,128)S(1)} %copy.51, pred[8,8]{1,0:T(8,128)(4,1)S(1)} %iota_compare_fusion.8), kind=kOutput, calls=%fused_computation.23 | convolution fusion | flops 50593792 | bytes 4522048 | tf_op jit(solution)/shard_map/rhts,rshp->rthp/dot_general | solution.py:82
  291.4 31.9 %fusion.7 = f32[16,8,64,64]{3,1,2,0:T(8,128)} fusion(f32[16,64,64,8]{2,3,1,0:T(8,128)} %fusion.9, f32[16,8,64,64]{3,2,1,0:T(8,128)} %reshape.242, bf16[16,64,64,256]{3,2,1,0:T(8,128)(2,1)} %param.24, f32[16,8,64,256]{3,2,1,0:T(8,128)S(1)} %convolution_bitcast_fusion.1, f32[64]{0:T(128)S(1)} %copy-done.21, f32[16,8,64]{1,2,0:T(8,128)S(1)} %copy.55), kind=kOutput, calls=%fused_computation.21 | convolution fusion | flops 1612709888 | bytes 48267520 | tf_op jit(solution)/shard_map/rhpn,rthn->rthp/dot_general | solution.py:83
  323.3 4.9 copy.58
  328.1 3.8 reshape.245
  332.0 1.9 fusion.64
  333.9 4.6 mul.221
  338.5 3.3 reduce_sum.45
  341.9 2.6 mul.222
  344.5 4.8 mul.223
  349.3 26.6 %fusion.38 = f32[128,8192]{1,0:T(8,128)} fusion(bf16[4096,8192]{1,0:T(8,128)(2,1)} %param.35, f32[16,8,4096]{2,1,0:T(8,128)} %mul.223, f32[4096]{0:T(1024)S(1)} %copy-done.15, f32[16,8,4096]{2,1,0:T(8,128)S(1)} %reshape.245, bf16[16,8,4096]{2,1,0:T(8,128)(2,1)S(1)} %copy-done.1), kind=kOutput, calls=%fused_computation.68 | convolution fusion | flops 8594653184 | bytes 76562432 | tf_op jit(solution)/shard_map/dot_general | solution.py:107
  375.9 0.6 copy-done.25
  376.6 0.1 select_reduce_fusion.1
  376.7 0.4 copy-done.3
  377.1 1.0 gather_fusion.1
  378.1 1.0 copy.61
  379.2 1.0 gather_fusion.3
  380.2 1.0 copy.62
  381.2 74.1 %reduce-scatter.2.cloned.1.call-done = f32[128,2048]{1,0:T(8,128)} async-done(((f32[128,8192]{1,0:T(8,128)}), f32[128,2048]{1,0:T(8,128)}) %reduce-scatter.2.cloned.1.call-update) | async-done | bytes 1048592 | tf_op jit(solution)/shard_map/reduce_scatter | solution.py:113
  455.3 2.1 convert_bitcast_fusion
  457.4 516.5 %all-to-all-done = bf16[32,64,64,256]{3,2,1,0:T(8,128)(2,1)} async-done(((bf16[32,64,64,256]{3,2,1,0:T(8,128)(2,1)}), bf16[32,64,64,256]{3,2,1,0:T(8,128)(2,1)}, u32[]{:S(2)}, u32[]{:S(2)}) %all-to-all-start) | async-done | bytes 67108896 | tf_op jit(solution)/shard_map/all_to_all | solution.py:150
  973.9 43.5 %fusion.65 = (bf16[32,64,64,128]{3,2,1,0:T(8,128)(2,1)}, bf16[32,64,64,128]{3,2,1,0:T(8,128)(2,1)}) fusion(bf16[32,64,64,256]{3,2,1,0:T(8,128)(2,1)} %all-to-all-done), kind=kLoop, calls=%fused_computation.123 | loop fusion | bytes 134217728 | tf_op jit(solution)/shard_map/jit(_take)/gather | solution.py:151
  1017.3 11.8 %gather_fusion.6 = bf16[16,64,64,128]{3,2,1,0:T(8,128)(2,1)} fusion(bf16[32,64,64,128]{3,2,1,0:T(8,128)(2,1)} %get-tuple-element.18, s32[1024]{0:T(1024)S(1)} %pad_clamp_fusion), kind=kCustom, calls=%fused_computation.6 | custom fusion | bytes 33554496 | tf_op jit(solution)/shard_map/jit(_take)/gather | solution.py:151
  1029.1 11.8 %gather_fusion.7 = bf16[16,64,64,128]{3,2,1,0:T(8,128)(2,1)} fusion(bf16[32,64,64,128]{3,2,1,0:T(8,128)(2,1)} %get-tuple-element.19, s32[1024]{0:T(1024)S(1)} %pad_clamp_fusion), kind=kCustom, calls=%fused_computation.7 | custom fusion | bytes 33554496 | tf_op jit(solution)/shard_map/jit(_take)/gather | solution.py:151
  1040.9 22.9 %pad_maximum_fusion.1 = bf16[16,64,64,256]{3,2,1,0:T(8,128)(2,1)} fusion(bf16[16,64,64,128]{3,2,1,0:T(8,128)(2,1)} %gather_fusion.7, bf16[16,64,64,128]{3,2,1,0:T(8,128)(2,1)} %gather_fusion.6), kind=kLoop, calls=%fused_computation.10 | loop fusion | flops 67108864 | bytes 67108864 | tf_op jit(solution)/shard_map
  (75 shorter events, 0.5 us)
Async XLA Ops:
  9.4 0.6 copy-start.27
  11.0 10.3 copy-start.20
  11.0 10.4 copy-start.7
  16.9 7.3 copy-start.29
  16.9 7.3 copy-start.14
  16.9 7.3 copy-start.22
  16.9 7.7 copy-start.16
  16.9 7.7 copy-start.17
  16.9 8.5 copy-start.11
  16.9 172.3 %all-to-all-start.1 = ((bf16[32,3,4096]{2,1,0:T(4,128)(2,1)}), bf16[32,3,4096]{2,1,0:T(4,128)(2,1)S(1)}, u32[]{:S(2)}, u32[]{:S(2)}) async-start(bf16[32,3,4096]{2,1,0:T(4,128)(2,1)} %gather_fusion), calls=%async_computation.2 | async-start | bytes 2097152 | tf_op jit(solution)/shard_map/all_to_all | solution.py:150
  21.3 5.3 copy-start.18
  24.1 21.0 %copy-start.23 = (s32[64]{0:T(128)}, s32[64]{0:T(128)S(1)}, u32[]{:S(2)}) copy-start(s32[64]{0:T(128)S(1)} %and_select_fusion.1) | copy-start | bytes 772
  24.3 2.2 copy-start.9
  36.6 2.1 copy-start.19
  40.0 2.6 copy-start
  123.4 25.2 %copy-start.6 = (bf16[16,3,4096]{2,1,0:T(4,128)(2,1)S(1)}, bf16[16,3,4096]{2,1,0:T(4,128)(2,1)}, u32[]{:S(2)}) copy-start(bf16[16,3,4096]{2,1,0:T(4,128)(2,1)} %copy.48) | copy-start | bytes 1179652
  123.4 25.2 %copy-start.8 = (bf16[16,8,4096]{2,1,0:T(8,128)(2,1)S(1)}, bf16[16,8,4096]{2,1,0:T(8,128)(2,1)}, u32[]{:S(2)}) copy-start(bf16[16,8,4096]{2,1,0:T(8,128)(2,1)} %param.20) | copy-start | bytes 3145732
  189.2 48.1 %copy-start.2 = (bf16[32,3,4096]{2,1,0:T(4,128)(2,1)}, bf16[32,3,4096]{2,1,0:T(4,128)(2,1)S(1)}, u32[]{:S(2)}) copy-start(bf16[32,3,4096]{2,1,0:T(4,128)(2,1)S(1)} %all-to-all-done.1) | copy-start | bytes 2359300
  189.2 48.2 %all-to-all-start.2 = ((bf16[32,3,4096]{2,1,0:T(4,128)(2,1)}), bf16[32,3,4096]{2,1,0:T(4,128)(2,1)S(1)}, u32[]{:S(2)}, u32[]{:S(2)}) async-start(bf16[32,3,4096]{2,1,0:T(4,128)(2,1)} %gather_fusion.2), calls=%async_computation.3 | async-start | bytes 2097152 | tf_op jit(solution)/shard_map/all_to_all | solution.py:150
  237.4 14.2 %copy-start.13 = (f32[16,64,8]{1,2,0:T(8,128)S(1)}, f32[16,64,8]{1,2,0:T(8,128)}, u32[]{:S(2)}) copy-start(f32[16,64,8]{1,2,0:T(8,128)} %get-tuple-element.25) | copy-start | bytes 98308
  237.4 15.2 %copy-start.12 = (f32[16,8,64]{2,1,0:T(8,128)S(1)}, f32[16,8,64]{2,1,0:T(8,128)}, u32[]{:S(2)}) copy-start(f32[16,8,64]{2,1,0:T(8,128)} %get-tuple-element.26) | copy-start | bytes 98308
  237.4 15.4 %copy-start.10 = (f32[16,8,64]{2,1,0:T(8,128)S(1)}, f32[16,8,64]{2,1,0:T(8,128)}, u32[]{:S(2)}) copy-start(f32[16,8,64]{2,1,0:T(8,128)} %copy-done.9) | copy-start | bytes 98308
  237.4 15.6 %copy-start.24 = (s32[64]{0:T(128)S(1)}, s32[64]{0:T(128)}, u32[]{:S(2)}) copy-start(s32[64]{0:T(128)} %copy-done.23) | copy-start | bytes 772
  237.4 1.0 copy-start.4
  238.4 735.4 %all-to-all-start = ((bf16[32,64,64,256]{3,2,1,0:T(8,128)(2,1)}), bf16[32,64,64,256]{3,2,1,0:T(8,128)(2,1)}, u32[]{:S(2)}, u32[]{:S(2)}) async-start(bf16[32,64,64,256]{3,2,1,0:T(8,128)(2,1)} %pad_maximum_fusion), calls=%async_computation.1 | async-start | bytes 134217728 | tf_op jit(solution)/shard_map/all_to_all | solution.py:150
  251.5 203.8 %reduce-scatter.2.cloned.1.call-start = ((), (), s32[]{:S(2)}) async-start(), calls=%async_computation.4 | async-start | bytes 5242880 | tf_op jit(solution)/shard_map/reduce_scatter | solution.py:113
  277.4 13.9 %copy-start.21 = (f32[64]{0:T(128)S(1)}, f32[64]{0:T(128)}, u32[]{:S(2)}) copy-start(f32[64]{0:T(128)} %param.33) | copy-start | bytes 772
  328.1 3.8 copy-start.1
  344.5 4.8 copy-start.15
  375.9 0.7 copy-start.25
  375.9 0.7 copy-start.28
  375.9 0.7 copy-start.26
  375.9 1.2 copy-start.3
  375.9 3.3 copy-start.5
Sparse Core Ops, SparseCore 0:
  376.1 79.1 reduce-scatter.1

commit v2 on v1

--- a/solution.py
+++ b/solution.py
@@ -2,6 +2,8 @@
 import jax.numpy as jnp
 from jax import lax
 from jax.sharding import PartitionSpec as P
+from jax.experimental import pallas as pl
+from jax.experimental.pallas import tpu as pltpu
 
 D = 8192
 H = 256
@@ -14,7 +16,7 @@
 
 
 epsilon = 1e-05
-highest = lax.Precision.HIGHEST
+highest = lax.Precision.HIGH
 
 
 def conv_window(history, inputs, weight, bias_vector):
@@ -26,6 +28,45 @@
             accumulated + weight[offset][None, None, :] * widened[:, offset : offset + L, :]
         )
     return (jax.nn.silu(accumulated), joined)
+
+
+def assemble(piece_of, slot_of, pieces):
+    rows = piece_of.shape[0]
+    count = len(pieces)
+
+    def kernel(piece_ref, slot_ref, *refs):
+        sources = refs[:count]
+        out_ref = refs[count]
+        sem = refs[count + 1]
+
+        def start(row, carry):
+            piece = piece_ref[row]
+            slot = slot_ref[row]
+            for which, ref in enumerate(sources):
+
+                @pl.when(piece == which)
+                def _():
+                    pltpu.make_async_copy(ref.at[slot], out_ref.at[row], sem.at[row]).start()
+
+            return carry
+
+        lax.fori_loop(0, rows, start, 0)
+
+        def finish(row, carry):
+            pltpu.make_async_copy(sources[0].at[0], out_ref.at[row], sem.at[row]).wait()
+            return carry
+
+        lax.fori_loop(0, rows, finish, 0)
+
+    smem = pl.BlockSpec(memory_space=pltpu.SMEM)
+    anywhere = pl.BlockSpec(memory_space=pl.ANY)
+    return pl.pallas_call(
+        kernel,
+        out_shape=jax.ShapeDtypeStruct((rows,) + pieces[0].shape[1:], pieces[0].dtype),
+        in_specs=[smem, smem] + [anywhere] * count,
+        out_specs=anywhere,
+        scratch_shapes=[pltpu.SemaphoreType.DMA((rows,))],
+    )(piece_of, slot_of, *pieces)
 
 
 def on_device(
@@ -91,8 +132,9 @@
     valid = positions[None, :] < accepted[:, None]
     exponent = jnp.where(valid[:, :, None], reached[:, None, :] - inclusive, -jnp.inf)
     token_weight = jnp.exp(exponent) * step_size
+    weighted_x = token_weight[:, :, :, None] * x_heads
     retained = jnp.exp(reached)[:, :, None, None] * initial + jnp.einsum(
-        "rsh,rshp,rshn->rhpn", token_weight, x_heads, b_heads, precision=highest
+        "rshp,rshn->rhpn", weighted_x, b_heads, precision=highest
     )
     retained = retained.astype(jnp.bfloat16)
     gated = y_values.reshape(local_requests, L, local_heads * P_SIZE) * jax.nn.silu(
@@ -145,12 +187,31 @@
         jnp.where(arriving, source[None, :] * cap + rank_in_pair[None, :], 0), axis=1
     )
 
+    partner_bits = range(1, owners)
+    own_index = jnp.take(send_index.reshape(owners, cap), req_index, axis=0)
+    pair_index = [
+        jnp.take(send_index.reshape(owners, cap), req_index ^ bits, axis=0) for bits in partner_bits
+    ]
+    arriving_source = jnp.sum(jnp.where(arriving, source[None, :], 0), axis=1)
+    arriving_rank = jnp.sum(jnp.where(arriving, rank_in_pair[None, :], 0), axis=1)
+    gather_index = (arriving_source ^ req_index) * cap + arriving_rank
+
+    piece_of = jnp.clip(arriving_source ^ req_index, 0, owners - 1)
+    slot_of = jnp.clip(arriving_rank, 0, cap - 1)
+
+    def send_pieces(values):
+        pieces = [jnp.take(values, own_index, axis=0, mode="clip")]
+        for bits, index in zip(partner_bits, pair_index):
+            outgoing = jnp.take(values, index, axis=0, mode="clip")
+            pairs = [(i, i ^ bits) for i in range(owners)]
+            pieces.append(lax.ppermute(outgoing, "req", pairs))
+        return pieces
+
     def hand_over(values):
-        outgoing = jnp.take(values, send_index, axis=0, mode="clip")
-        incoming = lax.all_to_all(outgoing, "req", 0, 0, tiled=True)
-        return jnp.take(incoming, receive_index, axis=0, mode="clip")
-
-    new_ssm_state = hand_over(retained)
+        pieces = send_pieces(values)
+        return jnp.take(jnp.concatenate(pieces, axis=0), gather_index, axis=0, mode="clip")
+
+    new_ssm_state = assemble(piece_of, slot_of, send_pieces(retained))
     new_conv_x_state = hand_over(kept_x)
     new_conv_bc_state = hand_over(kept_bc)
     return (mixed, new_ssm_state, new_conv_x_state, new_conv_bc_state)

time: 1090 us -> 1970 us (1.81)
  Pallas kernels: 0 us -> 1020 us
  waiting for transfers between devices: 591 us -> 545 us
  matrix products: 178 us -> 135 us
    pallas_call x0 -> x1, Pallas kernels: none -> 1020 us  [assemble(): pl.pallas_call(kernel, out_shape=jax.ShapeDtypeStruct((rows,) + pieces[0]...]
    ppermute x0 -> x9, waiting for transfers between devices: none -> 545 us  [send_pieces(): pieces.append(lax.ppermute(outgoing, 'req', pairs))]
    all_to_all x3 -> x0, waiting for transfers between devices: 517 us -> none  [hand_over(): incoming = lax.all_to_all(outgoing, 'req', 0, 0, tiled=True)]
    reduce_scatter x1, waiting for transfers between devices: 74.1 us -> 0.01 us  [on_device(): lax.psum_scatter(partial_terms, 'head', scatter_dimension=1, tiled=True)]
    dot_general x1, matrix products: 72.5 us -> 44.9 us  [on_device(): jnp.einsum('rshp,rshn->rhpn', weighted_x, b_heads, precision=highest)]
    another operation x1 -> x0, other arithmetic: 22.9 us -> none
    all_to_all x3 -> x0, starting transfers between devices: 21.1 us -> none  [hand_over(): incoming = lax.all_to_all(outgoing, 'req', 0, 0, tiled=True)]
    gather x10 -> x19, local copies, waits for them, and re-layouts: 136 us -> 118 us  [the longest x12 67.1 us: send_pieces(): outgoing = jnp.take(values, index, axis=0, mode='clip')]
  transfers between devices with their start and end apart: 4 -> 10, of which waited for: 2 -> 4; matrix products, arithmetic and copies ran while one was open for 32% -> 12% of each run, Pallas kernels for 0% -> 0%
where the time goes in v2:
time: 1970 us; the launch traced here: 1960 us
  Pallas kernels  1020 us (52%)
  waiting for transfers between devices  545 us (28%)
  local copies, waits for them, and re-layouts  154 us (8%)
  matrix products  135 us (7%)
  other arithmetic  84.7 us (4%)
    pallas_call x1, Pallas kernels, assemble(): pl.pallas_call(kernel, out_shape=jax.ShapeDtypeStruct((rows,) + pieces[0]...  1020 us
    ppermute x9, waiting for transfers between devices, send_pieces(): pieces.append(lax.ppermute(outgoing, 'req', pairs))  545 us
    gather x12, local copies, waits for them, and re-layouts, send_pieces(): outgoing = jnp.take(values, index, axis=0, mode='clip')  67.1 us
    unnamed x4, other arithmetic  57.4 us
    gather x5, local copies, waits for them, and re-layouts, send_pieces(): pieces = [jnp.take(values, own_index, axis=0, mode='clip')]  48.5 us
    dot_general x1, matrix products, on_device(): jnp.einsum('rshp,rshn->rhpn', weighted_x, b_heads, precision=highest)  44.9 us
  transfers between devices with their start and end apart: 10, of which 4 were waited for; matrix products, arithmetic and copies ran while one was open for 12% of the time, Pallas kernels for 0%

profile of v2, /device:TPU:0, one launch (start us, length us, event | category | flops | bytes accessed | tf_op | source)
XLA Modules:
  0.0 1959.2 jit_solution(15985122464328176502)
XLA Ops:
  10.6 1.4 convert_reduce_fusion
  12.9 0.9 broadcast_multiply_fusion.1
  14.0 1.1 fusion.71
  15.1 1.1 fusion.72
  16.2 0.9 exponential_multiply_fusion
  17.1 1.3 copy.47
  18.5 1.5 copy.48
  20.0 2.1 fusion.35
  22.1 1.3 divide_multiply_fusion
  23.5 1.2 fusion.70
  25.6 1.3 divide_multiply_fusion.1
  26.9 3.0 reshape.257
  30.0 4.2 broadcast_multiply_fusion
  34.1 5.7 convolution_bitcast_fusion
  39.8 44.9 %add_convert_fusion = bf16[16,64,64,256]{3,2,1,0:T(8,128)(2,1)} fusion(bf16[16,64,64,256]{3,2,1,0:T(8,128)(2,1)} %param.26, f32[16,64]{1,0:T(8,128)S(1)} %exp.40, f32[16,8,64,256]{3,2,1,0:T(8,128)} %convolution_bitcast_fusion, f32[16,8,64,64]{3,2,1,0:T(8,128)} %broadcast_multiply_fusion), kind=kOutput, calls=%fused_computation.18 | convolution fusion | flops 872415232 | bytes 77598720 | tf_op jit(solution)/shard_map/rshp,rshn->rhpn/dot_general | solution.py:136
  84.7 25.1 %fusion.69 = (bf16[16,64,64,128]{3,2,1,0:T(8,128)(2,1)}, bf16[16,64,64,128]{3,2,1,0:T(8,128)(2,1)}) fusion(bf16[16,64,64,256]{3,2,1,0:T(8,128)(2,1)} %add_convert_fusion), kind=kLoop, calls=%fused_computation.155 | loop fusion | bytes 67108864 | tf_op jit(solution)/shard_map/jit(_take)/gather | solution.py:203
  109.8 10.5 gather_fusion.12
  120.3 10.4 gather_fusion.13
  130.7 14.3 pad_maximum_fusion.1
  145.2 10.4 gather_fusion.14
  155.7 10.4 gather_fusion.15
  166.1 14.2 pad_maximum_fusion.2
  180.3 2.6 collective-permute-start.1
  183.0 10.4 gather_fusion.16
  193.4 10.3 gather_fusion.17
  203.7 14.4 pad_maximum_fusion.3
  218.5 1.0 copy.53
  219.9 3.6 convolution_bitcast_fusion.1
  223.5 18.9 fusion.1
  242.5 10.3 fusion.9
  252.7 23.3 %fusion.7 = f32[16,8,64,64]{3,1,2,0:T(8,128)} fusion(f32[16,64,64,8]{2,3,1,0:T(8,128)} %fusion.9, f32[16,8,64,64]{3,2,1,0:T(8,128)} %reshape.257, bf16[16,64,64,256]{3,2,1,0:T(8,128)(2,1)} %param.26, f32[16,8,64,256]{3,2,1,0:T(8,128)S(1)} %convolution_bitcast_fusion.1, f32[64]{0:T(128)S(1)} %copy-done.14, f32[16,8,64]{1,2,0:T(8,128)S(1)} %copy.55), kind=kOutput, calls=%fused_computation.33 | convolution fusion | flops 807403520 | bytes 48267520 | tf_op jit(solution)/shard_map/rhpn,rthn->rthp/dot_general | solution.py:124
  276.1 5.0 copy.58
  281.1 3.6 reshape.260
  284.7 1.9 fusion.68
  286.6 4.6 mul.229
  291.2 3.3 reduce_sum.54
  294.5 2.6 mul.230
  297.1 4.8 mul.231
  301.9 26.8 %fusion.38 = f32[128,8192]{1,0:T(8,128)} fusion(bf16[4096,8192]{1,0:T(8,128)(2,1)} %param.37, f32[16,8,4096]{2,1,0:T(8,128)} %mul.231, f32[4096]{0:T(1024)S(1)} %copy-done.8, f32[16,8,4096]{2,1,0:T(8,128)S(1)} %reshape.260, bf16[16,8,4096]{2,1,0:T(8,128)(2,1)S(1)} %copy-done), kind=kOutput, calls=%fused_computation.80 | convolution fusion | flops 8594653184 | bytes 76562432 | tf_op jit(solution)/shard_map/dot_general | solution.py:149
  330.2 0.8 convolution_convert_fusion.1
  331.0 0.8 gather_fusion.1
  332.7 1.8 collective-permute-start.4
  334.6 11.3 gather_fusion.10
  345.8 10.6 gather_fusion.11
  356.5 0.8 convolution_convert_fusion
  357.3 14.5 pad_maximum_fusion.refs_0_
  371.9 0.8 gather_fusion.3
  372.6 0.8 gather_fusion.6
  373.6 535.9 %collective-permute-done.4 = bf16[8,3,4096]{2,1,0:T(4,128)(2,1)} collective-permute-done((bf16[8,3,4096]{2,1,0:T(4,128)(2,1)S(1)}, bf16[8,3,4096]{2,1,0:T(4,128)(2,1)}, u32[]{:S(2)}, u32[]{:S(2)}) %collective-permute-start.4) | collective-permute-done | bytes 196640 | tf_op jit(solution)/shard_map/ppermute | solution.py:207
  910.9 0.8 gather_fusion.8
  911.7 0.8 gather_fusion.7
  912.4 0.8 gather_fusion.5
  913.2 1.4 collective-permute-done.5
  914.7 1.5 collective-permute-start.7
  916.2 1.7 pad_maximum_fusion.8
  917.9 1.0 gather_fusion.4
  918.9 1.0 copy.61
  920.0 3.9 collective-permute-done.7
  923.8 4.1 collective-permute-done.8
  927.9 1.7 pad_maximum_fusion.9
  929.6 1.0 gather_fusion.9
  930.6 1.0 copy.62
  931.6 2.1 convert_bitcast_fusion
  933.7 1018.4 %shard_map.201 = bf16[16,64,64,256]{3,2,1,0:T(8,128)(2,1)} custom-call(s32[16]{0:T(128)} %get-tuple-element.52.piece_ref, s32[16]{0:T(128)} %get-tuple-element.53.slot_ref, bf16[8,64,64,256]{3,2,1,0:T(8,128)(2,1)} %pad_maximum_fusion.refs_0_, bf16[8,64,64,256]{3,2,1,0:T(8,128)(2,1)} %collective-permute-done.refs_1_, ...), custom_call_target="tpu_custom_call" | custom-call | tf_op jit(solution)/shard_map/pallas_call | solution.py:63
  (83 shorter events, 10.5 us)
Async XLA Ops:
  7.2 924.5 %reduce-scatter.2.cloned.1.call-start = ((), (), s32[]{:S(2)}) async-start(), calls=%async_computation.1 | async-start | bytes 5242880 | tf_op jit(solution)/shard_map/reduce_scatter | solution.py:155
  10.1 0.5 copy-start.12
  12.1 3.0 copy-start.17
  13.8 8.3 copy-start.9
  18.4 6.2 copy-start.3
  20.0 2.1 copy-start.1
  23.4 1.5 copy-start.5
  23.5 2.1 copy-start.10
  144.9 788.8 %collective-permute-start = (bf16[8,64,64,256]{3,2,1,0:T(8,128)(2,1)}, bf16[8,64,64,256]{3,2,1,0:T(8,128)(2,1)}, u32[]{:S(2)}, u32[]{:S(2)}) collective-permute-start(bf16[8,64,64,256]{3,2,1,0:T(8,128)(2,1)} %pad_maximum_fusion.1), channel_id=1, source_target_pairs={{0,1},{1,0},{2,3},{3,2},{4,5},{5,4},{6,7},{7,6},{8,9},{9,8},{10,11... | collective-permute-start | bytes 50331656 | tf_op jit(solution)/shard_map/ppermute | solution.py:207
  180.3 753.4 %collective-permute-start.1 = (bf16[8,64,64,256]{3,2,1,0:T(8,128)(2,1)}, bf16[8,64,64,256]{3,2,1,0:T(8,128)(2,1)}, u32[]{:S(2)}, u32[]{:S(2)}) collective-permute-start(bf16[8,64,64,256]{3,2,1,0:T(8,128)(2,1)} %pad_maximum_fusion.2), channel_id=1, source_target_pairs={{0,2},{1,3},{2,0},{3,1},{4,6},{5,7},{6,4},{7,5},{8,10},{9,11},{10,... | collective-permute-start | bytes 50331656 | tf_op jit(solution)/shard_map/ppermute | solution.py:207
  218.1 715.6 %collective-permute-start.2 = (bf16[8,64,64,256]{3,2,1,0:T(8,128)(2,1)}, bf16[8,64,64,256]{3,2,1,0:T(8,128)(2,1)}, u32[]{:S(2)}, u32[]{:S(2)}) collective-permute-start(bf16[8,64,64,256]{3,2,1,0:T(8,128)(2,1)} %pad_maximum_fusion.3), channel_id=1, source_target_pairs={{0,3},{1,2},{2,1},{3,0},{4,7},{5,6},{6,5},{7,4},{8,11},{9,10},{10,... | collective-permute-start | bytes 50331656 | tf_op jit(solution)/shard_map/ppermute | solution.py:207
  242.5 10.3 copy-start.14
  281.1 3.6 copy-start
  297.1 4.8 copy-start.8
  328.8 0.7 copy-start.11
  328.8 1.1 copy-start.4
  328.8 1.4 copy-start.6
  328.8 5.8 copy-start.16
  331.7 41.8 %collective-permute-start.3 = (bf16[8,3,4096]{2,1,0:T(4,128)(2,1)S(1)}, bf16[8,3,4096]{2,1,0:T(4,128)(2,1)S(1)}, u32[]{:S(2)}, u32[]{:S(2)}) collective-permute-start(bf16[8,3,4096]{2,1,0:T(4,128)(2,1)S(1)} %gather_fusion.1), channel_id=1, source_target_pairs={{0,1},{1,0},{2,3},{3,2},{4,5},{5,4},{6,7},{7,6},{8,9},{9,8},{10,11... | collective-permute-start | bytes 589832 | tf_op jit(solution)/shard_map/ppermute | solution.py:207
  332.7 576.8 %collective-permute-start.4 = (bf16[8,3,4096]{2,1,0:T(4,128)(2,1)S(1)}, bf16[8,3,4096]{2,1,0:T(4,128)(2,1)}, u32[]{:S(2)}, u32[]{:S(2)}) collective-permute-start(bf16[8,3,4096]{2,1,0:T(4,128)(2,1)S(1)} %gather_fusion.2), channel_id=1, source_target_pairs={{0,2},{1,3},{2,0},{3,1},{4,6},{5,7},{6,4},{7,5},{8,10},{9,11},{10,... | collective-permute-start | bytes 589832 | tf_op jit(solution)/shard_map/ppermute | solution.py:207
  345.8 10.6 copy-start.2
  345.8 10.6 copy-start.7
  357.3 14.6 copy-start.15
  357.3 16.1 copy-start.13
  357.3 16.1 copy-start.18
  357.3 16.1 copy-start.19
  373.6 541.1 %collective-permute-start.5 = (bf16[8,3,4096]{2,1,0:T(4,128)(2,1)S(1)}, bf16[8,3,4096]{2,1,0:T(4,128)(2,1)S(1)}, u32[]{:S(2)}, u32[]{:S(2)}) collective-permute-start(bf16[8,3,4096]{2,1,0:T(4,128)(2,1)S(1)} %gather_fusion.3), channel_id=1, source_target_pairs={{0,3},{1,2},{2,1},{3,0},{4,7},{5,6},{6,5},{7,4},{8,11},{9,10},{10,... | collective-permute-start | bytes 589832 | tf_op jit(solution)/shard_map/ppermute | solution.py:207
  909.5 6.7 collective-permute-start.6
  914.7 9.2 collective-permute-start.7
  916.2 11.7 collective-permute-start.8
Sparse Core Ops, SparseCore 0:
  328.9 78.2 reduce-scatter.1

commit v3 on v1

--- a/solution.py
+++ b/solution.py
@@ -14,7 +14,7 @@
 
 
 epsilon = 1e-05
-highest = lax.Precision.HIGHEST
+highest = lax.Precision.HIGH
 
 
 def conv_window(history, inputs, weight, bias_vector):
@@ -91,8 +91,9 @@
     valid = positions[None, :] < accepted[:, None]
     exponent = jnp.where(valid[:, :, None], reached[:, None, :] - inclusive, -jnp.inf)
     token_weight = jnp.exp(exponent) * step_size
+    weighted_x = token_weight[:, :, :, None] * x_heads
     retained = jnp.exp(reached)[:, :, None, None] * initial + jnp.einsum(
-        "rsh,rshp,rshn->rhpn", token_weight, x_heads, b_heads, precision=highest
+        "rshp,rshn->rhpn", weighted_x, b_heads, precision=highest
     )
     retained = retained.astype(jnp.bfloat16)
     gated = y_values.reshape(local_requests, L, local_heads * P_SIZE) * jax.nn.silu(
@@ -145,12 +146,60 @@
         jnp.where(arriving, source[None, :] * cap + rank_in_pair[None, :], 0), axis=1
     )
 
+    partner_bits = range(1, owners)
+    own_index = jnp.take(send_index.reshape(owners, cap), req_index, axis=0)
+    pair_index = [
+        jnp.take(send_index.reshape(owners, cap), req_index ^ bits, axis=0) for bits in partner_bits
+    ]
+    arriving_source = jnp.sum(jnp.where(arriving, source[None, :], 0), axis=1)
+    arriving_rank = jnp.sum(jnp.where(arriving, rank_in_pair[None, :], 0), axis=1)
+    gather_index = (arriving_source ^ req_index) * cap + arriving_rank
+
+    def send_pieces(values):
+        pieces = [jnp.take(values, own_index, axis=0, mode="clip")]
+        for bits, index in zip(partner_bits, pair_index):
+            outgoing = jnp.take(values, index, axis=0, mode="clip")
+            pairs = [(i, i ^ bits) for i in range(owners)]
+            pieces.append(lax.ppermute(outgoing, "req", pairs))
+        return pieces
+
     def hand_over(values):
-        outgoing = jnp.take(values, send_index, axis=0, mode="clip")
-        incoming = lax.all_to_all(outgoing, "req", 0, 0, tiled=True)
-        return jnp.take(incoming, receive_index, axis=0, mode="clip")
-
-    new_ssm_state = hand_over(retained)
+        pieces = send_pieces(values)
+        return jnp.take(jnp.concatenate(pieces, axis=0), gather_index, axis=0, mode="clip")
+
+    owner_ids = jnp.arange(owners, dtype=jnp.int32)
+    pair_count = jnp.sum(
+        (
+            (source[None, None, :] == owner_ids[:, None, None])
+            & (next_owner[None, None, :] == owner_ids[None, :, None])
+        ).astype(jnp.int32),
+        axis=2,
+    )
+    first_slots = min(3, cap)
+    state_pieces = [jnp.take(retained, own_index, axis=0, mode="clip")]
+    for bits, index in zip(partner_bits, pair_index):
+        pairs = [(i, i ^ bits) for i in range(owners)]
+        if bits == 1:
+            outgoing = jnp.take(retained, index, axis=0, mode="clip")
+            state_pieces.append(lax.ppermute(outgoing, "req", pairs))
+            continue
+        outgoing = jnp.take(retained, index[:first_slots], axis=0, mode="clip")
+        arrived = lax.ppermute(outgoing, "req", pairs)
+        buffer = jnp.concatenate(
+            [arrived, jnp.zeros((cap - first_slots,) + arrived.shape[1:], arrived.dtype)], axis=0
+        )
+        needed = jnp.max(pair_count[owner_ids, owner_ids ^ bits])
+        needed = jnp.clip(lax.pmax(needed, "group"), first_slots, cap)
+
+        def one_slot(slot, held, index=index, pairs=pairs):
+            row = lax.dynamic_index_in_dim(retained, index[slot], 0, keepdims=True)
+            got = lax.ppermute(row, "req", pairs)
+            return lax.dynamic_update_index_in_dim(held, got, slot, 0)
+
+        state_pieces.append(lax.fori_loop(first_slots, needed, one_slot, buffer))
+    new_ssm_state = jnp.take(
+        jnp.concatenate(state_pieces, axis=0), gather_index, axis=0, mode="clip"
+    )
     new_conv_x_state = hand_over(kept_x)
     new_conv_bc_state = hand_over(kept_bc)
     return (mixed, new_ssm_state, new_conv_x_state, new_conv_bc_state)

time: 1090 us -> 1040 us (0.954); the launches traced: 1070 us -> 1030 us
  waiting for transfers between devices: 591 us -> 479 us
  local copies, waits for them, and re-layouts: 173 us -> 253 us
  matrix products: 178 us -> 137 us
  other arithmetic: 93.8 us -> 121 us
    all_to_all x3 -> x0, waiting for transfers between devices: 517 us -> none  [hand_over(): incoming = lax.all_to_all(outgoing, 'req', 0, 0, tiled=True)]
    ppermute x0 -> x14, waiting for transfers between devices: none -> 479 us  [the longest x6 246 us: send_pieces(): pieces.append(lax.ppermute(outgoing, 'req', pairs))]
    reduce_scatter x1, waiting for transfers between devices: 74.1 us -> 0.01 us  [on_device(): lax.psum_scatter(partial_terms, 'head', scatter_dimension=1, tiled=True)]
    concatenate x0 -> x4, other arithmetic: none -> 46.9 us  [the longest x1 44.4 us: on_device(): jnp.concatenate(state_pieces, axis=0)]
    gather x10 -> x24, local copies, waits for them, and re-layouts: 136 us -> 175 us  [the longest x3 67 us: on_device(): jnp.take(jnp.concatenate(state_pieces, axis=0), gather_index, axis=0, mod...]
    dot_general x1, matrix products: 72.5 us -> 44.9 us  [on_device(): jnp.einsum('rshp,rshn->rhpn', weighted_x, b_heads, precision=highest)]
    all_to_all x3 -> x0, starting transfers between devices: 21.1 us -> none  [hand_over(): incoming = lax.all_to_all(outgoing, 'req', 0, 0, tiled=True)]
    dynamic_slice x0 -> x10, local copies, waits for them, and re-layouts: none -> 18.9 us  [one_slot(): row = lax.dynamic_index_in_dim(retained, index[slot], 0, keepdims=True)]
  transfers between devices with their start and end apart: 4 -> 15, of which waited for: 2 -> 8; matrix products, arithmetic and copies ran while one was open for 32% -> 23% of each run, Pallas kernels for 0% -> 0%
where the time goes in v3:
time: 1040 us; the launch traced here: 1030 us
  waiting for transfers between devices  479 us (46%)
  local copies, waits for them, and re-layouts  253 us (24%)
  matrix products  137 us (13%)
  other arithmetic  121 us (12%)
  between operations  16.2 us (2%)
  starting transfers between devices  13.1 us (1%)
    ppermute x6, waiting for transfers between devices, send_pieces(): pieces.append(lax.ppermute(outgoing, 'req', pairs))  246 us
    ppermute x5, waiting for transfers between devices, one_slot(): got = lax.ppermute(row, 'req', pairs)  233 us
    gather x3, local copies, waits for them, and re-layouts, on_device(): jnp.take(jnp.concatenate(state_pieces, axis=0), gather_index, axis=0, mod...  67 us
    gather x3, local copies, waits for them, and re-layouts, on_device(): state_pieces = [jnp.take(retained, own_index, axis=0, mode='clip')]  45.9 us
    dot_general x1, matrix products, on_device(): jnp.einsum('rshp,rshn->rhpn', weighted_x, b_heads, precision=highest)  44.9 us
    concatenate x1, other arithmetic, on_device(): jnp.concatenate(state_pieces, axis=0)  44.4 us
    gather x4, local copies, waits for them, and re-layouts, on_device(): outgoing = jnp.take(retained, index[:first_slots], axis=0, mode='clip')  31.7 us
    dot_general x1, matrix products, on_device(): jnp.dot(normed.reshape(local_requests * L, local_heads * P_SIZE), out_wei...  26.9 us
  transfers between devices with their start and end apart: 15, of which 8 were waited for; matrix products, arithmetic and copies ran while one was open for 23% of the time, Pallas kernels for 0%

profile of v3, /device:TPU:0, one launch (start us, length us, event | category | flops | bytes accessed | tf_op | source)
XLA Modules:
  0.0 1033.0 jit_solution(2109051206131003059)
XLA Ops:
  10.6 1.4 convert_reduce_fusion
  18.9 1.5 copy.48
  20.4 2.1 fusion.35
  27.4 3.1 reshape.349
  30.4 4.2 broadcast_multiply_fusion
  34.6 5.6 convolution_bitcast_fusion
  40.2 44.9 %add_convert_fusion = bf16[16,64,64,256]{3,2,1,0:T(8,128)(2,1)} fusion(bf16[16,64,64,256]{3,2,1,0:T(8,128)(2,1)} %param.30, f32[16,64]{1,0:T(8,128)S(1)} %exp.40, f32[16,8,64,256]{3,2,1,0:T(8,128)} %convolution_bitcast_fusion, f32[16,8,64,64]{3,2,1,0:T(8,128)} %broadcast_multiply_fusion), kind=kOutput, calls=%fused_computation.27 | convolution fusion | flops 872415232 | bytes 77598720 | tf_op jit(solution)/shard_map/rshp,rshn->rhpn/dot_general | solution.py:95
  85.1 25.1 %fusion.78 = (bf16[16,64,64,128]{3,2,1,0:T(8,128)(2,1)}, bf16[16,64,64,128]{3,2,1,0:T(8,128)(2,1)}) fusion(bf16[16,64,64,256]{3,2,1,0:T(8,128)(2,1)} %add_convert_fusion), kind=kLoop, calls=%fused_computation.179 | loop fusion | bytes 67108864 | tf_op jit(solution)/shard_map/jit(_take)/gather | solution.py:179
  110.2 10.4 %gather_fusion.14 = bf16[8,64,64,128]{3,2,1,0:T(8,128)(2,1)} fusion(bf16[16,64,64,128]{3,2,1,0:T(8,128)(2,1)} %get-tuple-element.114, s32[1024]{0:T(1024)S(1)} %pad_clamp_fusion.5), kind=kCustom, calls=%fused_computation.14 | custom fusion | bytes 16777248 | tf_op jit(solution)/shard_map/jit(_take)/gather | solution.py:183
  120.6 10.4 %gather_fusion.15 = bf16[8,64,64,128]{3,2,1,0:T(8,128)(2,1)} fusion(bf16[16,64,64,128]{3,2,1,0:T(8,128)(2,1)} %get-tuple-element.115, s32[1024]{0:T(1024)S(1)} %pad_clamp_fusion.5), kind=kCustom, calls=%fused_computation.15 | custom fusion | bytes 16777248 | tf_op jit(solution)/shard_map/jit(_take)/gather | solution.py:183
  131.1 14.4 %pad_maximum_fusion.2 = bf16[8,64,64,256]{3,2,1,0:T(8,128)(2,1)} fusion(bf16[8,64,64,128]{3,2,1,0:T(8,128)(2,1)} %gather_fusion.15, bf16[8,64,64,128]{3,2,1,0:T(8,128)(2,1)} %gather_fusion.14), kind=kLoop, calls=%fused_computation.29 | loop fusion | flops 33554432 | bytes 33554432
  147.3 3.6 convolution_bitcast_fusion.1
  150.9 18.9 %fusion.1 = f32[16,64,8,8]{3,2,1,0:T(8,128)} fusion(f32[16,8,64,256]{3,2,1,0:T(8,128)} %convolution_bitcast_fusion, f32[16,8,64,256]{3,2,1,0:T(8,128)S(1)} %convolution_bitcast_fusion.1), kind=kOutput, calls=%fused_computation.31 | convolution fusion | flops 100663296 | bytes 17039360 | tf_op jit(solution)/shard_map/rthn,rshn->rhts/dot_general | solution.py:80
  169.9 10.3 fusion.9
  180.2 23.3 %fusion.7 = f32[16,8,64,64]{3,1,2,0:T(8,128)} fusion(f32[16,64,64,8]{2,3,1,0:T(8,128)} %fusion.9, f32[16,8,64,64]{3,2,1,0:T(8,128)} %reshape.349, bf16[16,64,64,256]{3,2,1,0:T(8,128)(2,1)} %param.30, f32[16,8,64,256]{3,2,1,0:T(8,128)S(1)} %convolution_bitcast_fusion.1, f32[64]{0:T(128)S(1)} %copy-done.13, f32[16,8,64]{1,2,0:T(8,128)S(1)} %copy.55), kind=kOutput, calls=%fused_computation.42 | convolution fusion | flops 807403520 | bytes 48267520 | tf_op jit(solution)/shard_map/rhpn,rthn->rthp/dot_general | solution.py:83
  203.5 5.0 copy.58
  208.5 3.6 reshape.352
  212.1 1.9 fusion.76
  214.0 4.7 mul.229
  218.6 3.3 reduce_sum.63
  222.0 2.7 mul.230
  224.7 4.7 mul.231
  229.4 26.9 %fusion.38 = f32[128,8192]{1,0:T(8,128)} fusion(bf16[4096,8192]{1,0:T(8,128)(2,1)} %param.41, f32[16,8,4096]{2,1,0:T(8,128)} %mul.231, f32[4096]{0:T(1024)S(1)} %copy-done.6, f32[16,8,4096]{2,1,0:T(8,128)S(1)} %reshape.352, bf16[16,8,4096]{2,1,0:T(8,128)(2,1)S(1)} %copy-done), kind=kOutput, calls=%fused_computation.89 | convolution fusion | flops 8594653184 | bytes 76562432 | tf_op jit(solution)/shard_map/dot_general | solution.py:108
  256.3 6.9 gather_fusion.18
  263.3 9.3 gather_fusion.19
  272.5 5.9 pad_maximum_fusion.4
  278.5 2.4 collective-permute-start.4
  280.8 7.0 gather_fusion.16
  287.9 8.5 gather_fusion.17
  296.4 6.0 pad_maximum_fusion.3
  305.3 2.2 convolution_convert_fusion.1
  308.5 5.1 all-reduce.3
  318.6 1.9 collective-permute-start.6
  320.5 237.4 %collective-permute-done.6 = bf16[8,3,4096]{2,1,0:T(4,128)(2,1)S(1)} collective-permute-done((bf16[8,3,4096]{2,1,0:T(4,128)(2,1)S(1)}, bf16[8,3,4096]{2,1,0:T(4,128)(2,1)S(1)}, u32[]{:S(2)}, u32[]{:S(2)}) %collective-permute-start.6) | collective-permute-done | bytes 196640 | tf_op jit(solution)/shard_map/ppermute | solution.py:163
  559.4 10.5 %gather_fusion.12 = bf16[8,64,64,128]{3,2,1,0:T(8,128)(2,1)} fusion(bf16[16,64,64,128]{3,2,1,0:T(8,128)(2,1)} %get-tuple-element.114, s32[1024]{0:T(1024)S(1)} %pad_clamp_fusion.6), kind=kCustom, calls=%fused_computation.12 | custom fusion | bytes 16777248 | tf_op jit(solution)/shard_map/jit(_take)/gather | solution.py:179
  569.9 10.4 %gather_fusion.13 = bf16[8,64,64,128]{3,2,1,0:T(8,128)(2,1)} fusion(bf16[16,64,64,128]{3,2,1,0:T(8,128)(2,1)} %get-tuple-element.115, s32[1024]{0:T(1024)S(1)} %pad_clamp_fusion.6), kind=kCustom, calls=%fused_computation.13 | custom fusion | bytes 16777248 | tf_op jit(solution)/shard_map/jit(_take)/gather | solution.py:179
  581.6 2.0 collective-permute-start.9
  583.6 1.8 pad_maximum_fusion.9
  587.5 3.3 collective-permute-done.9
  590.7 5.0 collective-permute-done.10
  598.5 8.0 concatenate.35
  606.5 8.0 concatenate.33
  614.5 2.1 convert_bitcast_fusion
  616.6 274.9 %while.22 = (s32[]{:T(128)}, bf16[8,64,64,256]{3,2,1,0:T(8,128)(2,1)}, s32[]{:T(128)}, s32[8]{0:T(128)S(1)}, bf16[16,64,64,256]{3,2,1,0:T(8,128)(2,1)}, /*index=5*/s32[]{:T(128)}, s32[]{:T(128)}, s32[]{:T(128)}, s32[]{:T(128)}) while((s32[]{:T(128)}, bf16[8,64,64,256]{3,2,1,0:T(8,128)(2,1)}, s32[]{:T(128)}, s32[8]{0:T(128)S(1)}, ...), condition=%wide.region_13.15_spmd, body=%wide.region_12.14_spmd.sunk | while | flops 8 | bytes 16777436 | solution.py:199
  619.1 3.2 constant_dynamic-slice_fusion.9
  622.3 1.5 collective-permute-start.1
  623.8 46.3 %collective-permute-done.1 = bf16[1,64,64,256]{3,2,1,0:T(8,128)(2,1)S(1)} collective-permute-done((bf16[1,64,64,256]{3,2,1,0:T(8,128)(2,1)}, bf16[1,64,64,256]{3,2,1,0:T(8,128)(2,1)S(1)}, u32[]{:S(2)}, u32[]{:S(2)}) %collective-permute-start.1) | collective-permute-done | bytes 2097184 | tf_op jit(solution)/shard_map/while/body/ppermute | solution.py:196
  670.1 1.5 constant_dynamic-update-slice_fusion.5
  674.1 3.2 constant_dynamic-slice_fusion.9
  678.6 46.5 %collective-permute-done.1 = bf16[1,64,64,256]{3,2,1,0:T(8,128)(2,1)S(1)} collective-permute-done((bf16[1,64,64,256]{3,2,1,0:T(8,128)(2,1)}, bf16[1,64,64,256]{3,2,1,0:T(8,128)(2,1)S(1)}, u32[]{:S(2)}, u32[]{:S(2)}) %collective-permute-start.1) | collective-permute-done | bytes 2097184 | tf_op jit(solution)/shard_map/while/body/ppermute | solution.py:196
  725.1 1.5 constant_dynamic-update-slice_fusion.5
  729.1 3.2 constant_dynamic-slice_fusion.9
  733.4 46.7 %collective-permute-done.1 = bf16[1,64,64,256]{3,2,1,0:T(8,128)(2,1)S(1)} collective-permute-done((bf16[1,64,64,256]{3,2,1,0:T(8,128)(2,1)}, bf16[1,64,64,256]{3,2,1,0:T(8,128)(2,1)S(1)}, u32[]{:S(2)}, u32[]{:S(2)}) %collective-permute-start.1) | collective-permute-done | bytes 2097184 | tf_op jit(solution)/shard_map/while/body/ppermute | solution.py:196
  780.1 1.5 constant_dynamic-update-slice_fusion.5
  784.1 3.2 constant_dynamic-slice_fusion.9
  788.3 46.7 %collective-permute-done.1 = bf16[1,64,64,256]{3,2,1,0:T(8,128)(2,1)S(1)} collective-permute-done((bf16[1,64,64,256]{3,2,1,0:T(8,128)(2,1)}, bf16[1,64,64,256]{3,2,1,0:T(8,128)(2,1)S(1)}, u32[]{:S(2)}, u32[]{:S(2)}) %collective-permute-start.1) | collective-permute-done | bytes 2097184 | tf_op jit(solution)/shard_map/while/body/ppermute | solution.py:196
  835.0 1.5 constant_dynamic-update-slice_fusion.5
  839.1 3.2 constant_dynamic-slice_fusion.9
  843.3 46.7 %collective-permute-done.1 = bf16[1,64,64,256]{3,2,1,0:T(8,128)(2,1)S(1)} collective-permute-done((bf16[1,64,64,256]{3,2,1,0:T(8,128)(2,1)}, bf16[1,64,64,256]{3,2,1,0:T(8,128)(2,1)S(1)}, u32[]{:S(2)}, u32[]{:S(2)}) %collective-permute-start.1) | collective-permute-done | bytes 2097184 | tf_op jit(solution)/shard_map/while/body/ppermute | solution.py:196
  891.5 44.4 %pad_maximum_fusion = bf16[32,64,64,256]{3,2,1,0:T(8,128)(2,1)} fusion(bf16[8,64,64,256]{3,2,1,0:T(8,128)(2,1)} %get-tuple-element.62, bf16[8,64,64,256]{3,2,1,0:T(8,128)(2,1)} %get-tuple-element.61, bf16[8,64,64,256]{3,2,1,0:T(8,128)(2,1)} %collective-permute-done.2, bf16[8,64,64,128]{3,2,1,0:T(8,128)(2,1)} %gather_fusion.13, ...), kind=kLoop, calls=%fused_computation.26 | loop fusion | flops 335544320 | bytes 134217728 | tf_op jit(solution)/shard_map/concatenate | solution.py:201
  935.8 43.4 %fusion.77 = (bf16[32,64,64,128]{3,2,1,0:T(8,128)(2,1)}, bf16[32,64,64,128]{3,2,1,0:T(8,128)(2,1)}) fusion(bf16[32,64,64,256]{3,2,1,0:T(8,128)(2,1)} %pad_maximum_fusion), kind=kLoop, calls=%fused_computation.178 | loop fusion | bytes 134217728 | tf_op jit(solution)/shard_map/jit(_take)/gather | solution.py:200
  979.3 11.8 %gather_fusion.20 = bf16[16,64,64,128]{3,2,1,0:T(8,128)(2,1)} fusion(bf16[32,64,64,128]{3,2,1,0:T(8,128)(2,1)} %get-tuple-element.112, s32[1024]{0:T(1024)S(1)} %pad_clamp_fusion.2), kind=kCustom, calls=%fused_computation.20 | custom fusion | bytes 33554496 | tf_op jit(solution)/shard_map/jit(_take)/gather | solution.py:200
  991.1 11.8 %gather_fusion.21 = bf16[16,64,64,128]{3,2,1,0:T(8,128)(2,1)} fusion(bf16[32,64,64,128]{3,2,1,0:T(8,128)(2,1)} %get-tuple-element.113, s32[1024]{0:T(1024)S(1)} %pad_clamp_fusion.2), kind=kCustom, calls=%fused_computation.21 | custom fusion | bytes 33554496 | tf_op jit(solution)/shard_map/jit(_take)/gather | solution.py:200
  1002.9 22.9 %pad_maximum_fusion.1 = bf16[16,64,64,256]{3,2,1,0:T(8,128)(2,1)} fusion(bf16[16,64,64,128]{3,2,1,0:T(8,128)(2,1)} %gather_fusion.21, bf16[16,64,64,128]{3,2,1,0:T(8,128)(2,1)} %gather_fusion.20), kind=kLoop, calls=%fused_computation.28 | loop fusion | flops 67108864 | bytes 67108864 | tf_op jit(solution)/shard_map
  (124 shorter events, 41.0 us)
Async XLA Ops:
  7.2 607.4 %reduce-scatter.2.cloned.1.call-start = ((), (), s32[]{:S(2)}) async-start(), calls=%async_computation.1 | async-start | bytes 5242880 | tf_op jit(solution)/shard_map/reduce_scatter | solution.py:114
  10.1 0.5 copy-start.11
  12.1 0.5 copy-start.17
  14.3 8.3 copy-start.7
  18.9 6.2 copy-start.3
  20.4 2.1 copy-start.1
  23.9 1.5 copy-start.4
  23.9 2.1 copy-start.8
  145.5 746.0 %collective-permute-start.2 = (bf16[8,64,64,256]{3,2,1,0:T(8,128)(2,1)}, bf16[8,64,64,256]{3,2,1,0:T(8,128)(2,1)}, u32[]{:S(2)}, u32[]{:S(2)}) collective-permute-start(bf16[8,64,64,256]{3,2,1,0:T(8,128)(2,1)} %pad_maximum_fusion.2), channel_id=1, source_target_pairs={{0,1},{1,0},{2,3},{3,2},{4,5},{5,4},{6,7},{7,6},{8,9},{9,8},{10,11... | collective-permute-start | bytes 50331656 | tf_op jit(solution)/shard_map/ppermute | solution.py:184
  169.9 10.3 copy-start.13
  208.5 3.6 copy-start
  224.7 4.8 copy-start.6
  272.5 8.3 copy-start.10
  278.5 320.0 %collective-permute-start.4 = (bf16[3,64,64,256]{3,2,1,0:T(8,128)(2,1)}, bf16[3,64,64,256]{3,2,1,0:T(8,128)(2,1)}, u32[]{:S(2)}, u32[]{:S(2)}) collective-permute-start(bf16[3,64,64,256]{3,2,1,0:T(8,128)(2,1)} %pad_maximum_fusion.4), channel_id=1, source_target_pairs={{0,3},{1,2},{2,1},{3,0},{4,7},{5,6},{6,5},{7,4},{8,11},{9,10},{10,... | collective-permute-start | bytes 18874376 | tf_op jit(solution)/shard_map/ppermute | solution.py:187
  296.4 6.1 copy-start.14
  296.4 6.1 copy-start.12
  296.4 8.8 copy-start.9
  302.4 12.8 %copy-start.2 = (bf16[16,3,4096]{2,1,0:T(4,128)(2,1)S(1)}, bf16[16,3,4096]{2,1,0:T(4,128)(2,1)}, u32[]{:S(2)}) copy-start(bf16[16,3,4096]{2,1,0:T(4,128)(2,1)} %copy-done.1) | copy-start | bytes 1179652
  302.4 12.9 %copy-start.5 = (bf16[16,8,4096]{2,1,0:T(8,128)(2,1)S(1)}, bf16[16,8,4096]{2,1,0:T(8,128)(2,1)}, u32[]{:S(2)}) copy-start(bf16[16,8,4096]{2,1,0:T(8,128)(2,1)} %param.26) | copy-start | bytes 3145732
  302.4 304.1 %collective-permute-start.3 = (bf16[3,64,64,256]{3,2,1,0:T(8,128)(2,1)}, bf16[3,64,64,256]{3,2,1,0:T(8,128)(2,1)}, u32[]{:S(2)}, u32[]{:S(2)}) collective-permute-start(bf16[3,64,64,256]{3,2,1,0:T(8,128)(2,1)} %pad_maximum_fusion.3), channel_id=1, source_target_pairs={{0,2},{1,3},{2,0},{3,1},{4,6},{5,7},{6,4},{7,5},{8,10},{9,11},{10,... | collective-permute-start | bytes 18874376 | tf_op jit(solution)/shard_map/ppermute | solution.py:187
  305.3 13.1 %copy-start.16 = (s32[64]{0:T(128)S(1)}, s32[64]{0:T(128)}, u32[]{:S(2)}) copy-start(s32[64]{0:T(128)} %get-tuple-element.88) | copy-start | bytes 772
  305.3 13.1 %copy-start.18 = (s32[64]{0:T(128)S(1)}, s32[64]{0:T(128)}, u32[]{:S(2)}) copy-start(s32[64]{0:T(128)} %copy-done.17) | copy-start | bytes 772
  305.3 252.5 %copy-start.15 = (s32[8]{0:T(128)S(1)}, s32[8]{0:T(128)}, u32[]{:S(2)}) copy-start(s32[8]{0:T(128)} %get-tuple-element.129) | copy-start | bytes 100
  308.3 12.2 %collective-permute-start.5 = (bf16[8,3,4096]{2,1,0:T(4,128)(2,1)S(1)}, bf16[8,3,4096]{2,1,0:T(4,128)(2,1)}, u32[]{:S(2)}, u32[]{:S(2)}) collective-permute-start(bf16[8,3,4096]{2,1,0:T(4,128)(2,1)S(1)} %gather_fusion.3), channel_id=1, source_target_pairs={{0,1},{1,0},{2,3},{3,2},{4,5},{5,4},{6,7},{7,6},{8,9},{9,8},{10,11... | collective-permute-start | bytes 589832 | tf_op jit(solution)/shard_map/ppermute | solution.py:163
  318.6 239.3 %collective-permute-start.6 = (bf16[8,3,4096]{2,1,0:T(4,128)(2,1)S(1)}, bf16[8,3,4096]{2,1,0:T(4,128)(2,1)S(1)}, u32[]{:S(2)}, u32[]{:S(2)}) collective-permute-start(bf16[8,3,4096]{2,1,0:T(4,128)(2,1)S(1)} %gather_fusion.4), channel_id=1, source_target_pairs={{0,2},{1,3},{2,0},{3,1},{4,6},{5,7},{6,4},{7,5},{8,10},{9,11},{10,... | collective-permute-start | bytes 589832 | tf_op jit(solution)/shard_map/ppermute | solution.py:163
  320.5 261.1 %collective-permute-start.7 = (bf16[8,3,4096]{2,1,0:T(4,128)(2,1)S(1)}, bf16[8,3,4096]{2,1,0:T(4,128)(2,1)}, u32[]{:S(2)}, u32[]{:S(2)}) collective-permute-start(bf16[8,3,4096]{2,1,0:T(4,128)(2,1)S(1)} %gather_fusion.5), channel_id=1, source_target_pairs={{0,3},{1,2},{2,1},{3,0},{4,7},{5,6},{6,5},{7,4},{8,11},{9,10},{10,... | collective-permute-start | bytes 589832 | tf_op jit(solution)/shard_map/ppermute | solution.py:163
  557.9 25.7 %collective-permute-start.8 = (bf16[8,3,4096]{2,1,0:T(4,128)(2,1)S(1)}, bf16[8,3,4096]{2,1,0:T(4,128)(2,1)S(1)}, u32[]{:S(2)}, u32[]{:S(2)}) collective-permute-start(bf16[8,3,4096]{2,1,0:T(4,128)(2,1)S(1)} %gather_fusion.8), channel_id=1, source_target_pairs={{0,1},{1,0},{2,3},{3,2},{4,5},{5,4},{6,7},{7,6},{8,9},{9,8},{10,11... | collective-permute-start | bytes 589832 | tf_op jit(solution)/shard_map/ppermute | solution.py:163
  581.6 9.2 collective-permute-start.9
  583.6 12.1 %collective-permute-start.10 = (bf16[8,3,4096]{2,1,0:T(4,128)(2,1)S(1)}, bf16[8,3,4096]{2,1,0:T(4,128)(2,1)S(1)}, u32[]{:S(2)}, u32[]{:S(2)}) collective-permute-start(bf16[8,3,4096]{2,1,0:T(4,128)(2,1)S(1)} %gather_fusion.10), channel_id=1, source_target_pairs={{0,3},{1,2},{2,1},{3,0},{4,7},{5,6},{6,5},{7,4},{8,11},{9,10},{10,... | collective-permute-start | bytes 589832 | tf_op jit(solution)/shard_map/ppermute | solution.py:163
  622.3 47.8 %collective-permute-start.1 = (bf16[1,64,64,256]{3,2,1,0:T(8,128)(2,1)}, bf16[1,64,64,256]{3,2,1,0:T(8,128)(2,1)S(1)}, u32[]{:S(2)}, u32[]{:S(2)}) collective-permute-start(bf16[1,64,64,256]{3,2,1,0:T(8,128)(2,1)} %constant_dynamic-slice_fusion.9), channel_id=1, source_target_pairs={{0,3},{1,2},{2,1},{3,0},{4,7},{5,6},{6,5},{7,4},{8,11},{9,10},{10,... | collective-permute-start | bytes 6291464 | tf_op jit(solution)/shard_map/while/body/ppermute | solution.py:196
  677.3 47.8 %collective-permute-start.1 = (bf16[1,64,64,256]{3,2,1,0:T(8,128)(2,1)}, bf16[1,64,64,256]{3,2,1,0:T(8,128)(2,1)S(1)}, u32[]{:S(2)}, u32[]{:S(2)}) collective-permute-start(bf16[1,64,64,256]{3,2,1,0:T(8,128)(2,1)} %constant_dynamic-slice_fusion.9), channel_id=1, source_target_pairs={{0,3},{1,2},{2,1},{3,0},{4,7},{5,6},{6,5},{7,4},{8,11},{9,10},{10,... | collective-permute-start | bytes 6291464 | tf_op jit(solution)/shard_map/while/body/ppermute | solution.py:196
  732.3 47.8 %collective-permute-start.1 = (bf16[1,64,64,256]{3,2,1,0:T(8,128)(2,1)}, bf16[1,64,64,256]{3,2,1,0:T(8,128)(2,1)S(1)}, u32[]{:S(2)}, u32[]{:S(2)}) collective-permute-start(bf16[1,64,64,256]{3,2,1,0:T(8,128)(2,1)} %constant_dynamic-slice_fusion.9), channel_id=1, source_target_pairs={{0,3},{1,2},{2,1},{3,0},{4,7},{5,6},{6,5},{7,4},{8,11},{9,10},{10,... | collective-permute-start | bytes 6291464 | tf_op jit(solution)/shard_map/while/body/ppermute | solution.py:196
  787.2 47.8 %collective-permute-start.1 = (bf16[1,64,64,256]{3,2,1,0:T(8,128)(2,1)}, bf16[1,64,64,256]{3,2,1,0:T(8,128)(2,1)S(1)}, u32[]{:S(2)}, u32[]{:S(2)}) collective-permute-start(bf16[1,64,64,256]{3,2,1,0:T(8,128)(2,1)} %constant_dynamic-slice_fusion.9), channel_id=1, source_target_pairs={{0,3},{1,2},{2,1},{3,0},{4,7},{5,6},{6,5},{7,4},{8,11},{9,10},{10,... | collective-permute-start | bytes 6291464 | tf_op jit(solution)/shard_map/while/body/ppermute | solution.py:196
  842.2 47.8 %collective-permute-start.1 = (bf16[1,64,64,256]{3,2,1,0:T(8,128)(2,1)}, bf16[1,64,64,256]{3,2,1,0:T(8,128)(2,1)S(1)}, u32[]{:S(2)}, u32[]{:S(2)}) collective-permute-start(bf16[1,64,64,256]{3,2,1,0:T(8,128)(2,1)} %constant_dynamic-slice_fusion.9), channel_id=1, source_target_pairs={{0,3},{1,2},{2,1},{3,0},{4,7},{5,6},{6,5},{7,4},{8,11},{9,10},{10,... | collective-permute-start | bytes 6291464 | tf_op jit(solution)/shard_map/while/body/ppermute | solution.py:196
Sparse Core Ops, SparseCore 0:
  256.4 78.9 reduce-scatter.1

commit v4 on v3

--- a/solution.py
+++ b/solution.py
@@ -77,13 +77,6 @@
     by_head = inclusive.transpose(0, 2, 1)
     differences = by_head[:, :, :, None] - by_head[:, :, None, :]
     pair_decay = jnp.exp(jnp.where(causal[None, None], differences, -jnp.inf))
-    scores = jnp.einsum("rthn,rshn->rhts", c_heads, b_heads, precision=highest)
-    weights = scores * pair_decay * step_size.transpose(0, 2, 1)[:, :, None, :]
-    within = jnp.einsum("rhts,rshp->rthp", weights, x_heads, precision=highest)
-    carried = jnp.exp(inclusive)[:, :, :, None] * jnp.einsum(
-        "rhpn,rthn->rthp", initial, c_heads, precision=highest
-    )
-    y_values = within + carried + d_skip[None, None, :, None] * x_heads
     count_pick = (jnp.arange(L + 1, dtype=jnp.int32)[None, :] == accepted[:, None]).astype(
         jnp.float32
     )
@@ -96,23 +89,6 @@
         "rshp,rshn->rhpn", weighted_x, b_heads, precision=highest
     )
     retained = retained.astype(jnp.bfloat16)
-    gated = y_values.reshape(local_requests, L, local_heads * P_SIZE) * jax.nn.silu(
-        z_input.astype(jnp.float32)
-    )
-    blocks = gated.reshape(local_requests, L, local_heads, P_SIZE)
-    inverse_rms = lax.rsqrt(jnp.mean(blocks * blocks, axis=3, keepdims=True) + epsilon)
-    normed = (
-        (blocks * inverse_rms).reshape(local_requests, L, local_heads * P_SIZE)
-        * norm_gain[None, None, :]
-    ).astype(jnp.bfloat16)
-    partial_terms = jnp.dot(
-        normed.reshape(local_requests * L, local_heads * P_SIZE),
-        out_weight,
-        preferred_element_type=jnp.float32,
-    )
-    share_width = D // lax.axis_size("head")
-    share = lax.psum_scatter(partial_terms, "head", scatter_dimension=1, tiled=True)
-    mixed = share.astype(jnp.bfloat16).reshape(local_requests, L, share_width)
     window_rows = jnp.arange(K - 1 + L, dtype=jnp.int32)
     row_pick = (
         window_rows[None, None, :]
@@ -155,6 +131,9 @@
     arriving_rank = jnp.sum(jnp.where(arriving, rank_in_pair[None, :], 0), axis=1)
     gather_index = (arriving_source ^ req_index) * cap + arriving_rank
 
+    piece_of = jnp.clip(arriving_source ^ req_index, 0, owners - 1)
+    slot_of = jnp.clip(arriving_rank, 0, cap - 1)
+
     def send_pieces(values):
         pieces = [jnp.take(values, own_index, axis=0, mode="clip")]
         for bits, index in zip(partner_bits, pair_index):
@@ -163,6 +142,17 @@
             pieces.append(lax.ppermute(outgoing, "req", pairs))
         return pieces
 
+    def assemble_rows(pieces):
+        def pick(which):
+            return lambda slot: lax.dynamic_index_in_dim(pieces[which], slot, 0, keepdims=True)
+
+        def place(row, held):
+            chosen = lax.switch(piece_of[row], [pick(w) for w in range(len(pieces))], slot_of[row])
+            return lax.dynamic_update_index_in_dim(held, chosen, row, 0)
+
+        empty = jnp.zeros((local_requests,) + pieces[0].shape[1:], pieces[0].dtype)
+        return lax.fori_loop(0, local_requests, place, empty)
+
     def hand_over(values):
         pieces = send_pieces(values)
         return jnp.take(jnp.concatenate(pieces, axis=0), gather_index, axis=0, mode="clip")
@@ -176,14 +166,16 @@
         axis=2,
     )
     first_slots = min(3, cap)
+    cross_pieces = []
     state_pieces = [jnp.take(retained, own_index, axis=0, mode="clip")]
     for bits, index in zip(partner_bits, pair_index):
         pairs = [(i, i ^ bits) for i in range(owners)]
         if bits == 1:
-            outgoing = jnp.take(retained, index, axis=0, mode="clip")
-            state_pieces.append(lax.ppermute(outgoing, "req", pairs))
+            near_pairs, near_index = pairs, index
+            state_pieces.append(None)
             continue
         outgoing = jnp.take(retained, index[:first_slots], axis=0, mode="clip")
+        cross_pieces.append(outgoing)
         arrived = lax.ppermute(outgoing, "req", pairs)
         buffer = jnp.concatenate(
             [arrived, jnp.zeros((cap - first_slots,) + arrived.shape[1:], arrived.dtype)], axis=0
@@ -197,9 +189,36 @@
             return lax.dynamic_update_index_in_dim(held, got, slot, 0)
 
         state_pieces.append(lax.fori_loop(first_slots, needed, one_slot, buffer))
-    new_ssm_state = jnp.take(
-        jnp.concatenate(state_pieces, axis=0), gather_index, axis=0, mode="clip"
-    )
+    x_heads, c_heads, b_heads, cross_pieces, near_source = lax.optimization_barrier(
+        (x_heads, c_heads, b_heads, cross_pieces, retained)
+    )
+    near_outgoing = jnp.take(near_source, near_index, axis=0, mode="clip")
+    state_pieces[1] = lax.ppermute(near_outgoing, "req", near_pairs)
+    scores = jnp.einsum("rthn,rshn->rhts", c_heads, b_heads, precision=highest)
+    weights = scores * pair_decay * step_size.transpose(0, 2, 1)[:, :, None, :]
+    within = jnp.einsum("rhts,rshp->rthp", weights, x_heads, precision=highest)
+    carried = jnp.exp(inclusive)[:, :, :, None] * jnp.einsum(
+        "rhpn,rthn->rthp", initial, c_heads, precision=highest
+    )
+    y_values = within + carried + d_skip[None, None, :, None] * x_heads
+    gated = y_values.reshape(local_requests, L, local_heads * P_SIZE) * jax.nn.silu(
+        z_input.astype(jnp.float32)
+    )
+    blocks = gated.reshape(local_requests, L, local_heads, P_SIZE)
+    inverse_rms = lax.rsqrt(jnp.mean(blocks * blocks, axis=3, keepdims=True) + epsilon)
+    normed = (
+        (blocks * inverse_rms).reshape(local_requests, L, local_heads * P_SIZE)
+        * norm_gain[None, None, :]
+    ).astype(jnp.bfloat16)
+    partial_terms = jnp.dot(
+        normed.reshape(local_requests * L, local_heads * P_SIZE),
+        out_weight,
+        preferred_element_type=jnp.float32,
+    )
+    share_width = D // lax.axis_size("head")
+    share = lax.psum_scatter(partial_terms, "head", scatter_dimension=1, tiled=True)
+    mixed = share.astype(jnp.bfloat16).reshape(local_requests, L, share_width)
+    new_ssm_state = assemble_rows(state_pieces)
     new_conv_x_state = hand_over(kept_x)
     new_conv_bc_state = hand_over(kept_bc)
     return (mixed, new_ssm_state, new_conv_x_state, new_conv_bc_state)

time: 1040 us -> 1280 us (1.23)
  local copies, waits for them, and re-layouts: 253 us -> 517 us
  other arithmetic: 121 us -> 56.4 us
  loops' own time: 9.56 us -> 49.7 us
    cond x0 -> x16, local copies, waits for them, and re-layouts: none -> 226 us
    gather x5 -> x3, local copies, waits for them, and re-layouts: 87.9 us -> 34.1 us  [on_device(): near_outgoing = jnp.take(near_source, near_index, axis=0, mode='clip')]
    dynamic_update_slice x0 -> x16, local copies, waits for them, and re-layouts: none -> 50.7 us  [place(): return lax.dynamic_update_index_in_dim(held, chosen, row, 0)]
    concatenate x1 -> x0, other arithmetic: 44.4 us -> none  [on_device(): jnp.concatenate(state_pieces, axis=0)]
    another operation x0 -> x17, loops' own time: none -> 40.2 us  [the longest x1 40.2 us: assemble_rows(): return lax.fori_loop(0, local_requests, place, empty)]
    gather x4 -> x5, local copies, waits for them, and re-layouts: 31.7 us -> 59.1 us  [on_device(): outgoing = jnp.take(retained, index[:first_slots], axis=0, mode='clip')]
    gather x3 -> x2, local copies, waits for them, and re-layouts: 45.9 us -> 21.8 us  [on_device(): state_pieces = [jnp.take(retained, own_index, axis=0, mode='clip')]]
    another operation x1 -> x0, other arithmetic: 22.9 us -> none
  transfers between devices with their start and end apart: 15 -> 15, of which waited for: 8 -> 8; matrix products, arithmetic and copies ran while one was open for 23% -> 16% of each run, Pallas kernels for 0% -> 0%
where the time goes in v4:
time: 1280 us; the launch traced here: 1270 us
  local copies, waits for them, and re-layouts  517 us (40%)
  waiting for transfers between devices  474 us (37%)
  matrix products  138 us (11%)
  other arithmetic  56.4 us (4%)
  loops' own time  49.7 us (4%)
  between operations  16.4 us (1%)
    ppermute x6, waiting for transfers between devices, send_pieces(): pieces.append(lax.ppermute(outgoing, 'req', pairs))  238 us
    ppermute x5, waiting for transfers between devices, one_slot(): got = lax.ppermute(row, 'req', pairs)  236 us
    cond x16, local copies, waits for them, and re-layouts  226 us
    gather x5, local copies, waits for them, and re-layouts, on_device(): outgoing = jnp.take(retained, index[:first_slots], axis=0, mode='clip')  59.1 us
    dynamic_update_slice x16, local copies, waits for them, and re-layouts, place(): return lax.dynamic_update_index_in_dim(held, chosen, row, 0)  50.7 us
    dot_general x1, matrix products, on_device(): jnp.einsum('rshp,rshn->rhpn', weighted_x, b_heads, precision=highest)  44.8 us
    another operation x1, loops' own time, assemble_rows(): return lax.fori_loop(0, local_requests, place, empty)  40.2 us
    gather x3, local copies, waits for them, and re-layouts, on_device(): near_outgoing = jnp.take(near_source, near_index, axis=0, mode='clip')  34.1 us
  transfers between devices with their start and end apart: 15, of which 8 were waited for; matrix products, arithmetic and copies ran while one was open for 16% of the time, Pallas kernels for 0%

profile of v4, /device:TPU:0, one launch (start us, length us, event | category | flops | bytes accessed | tf_op | source)
XLA Modules:
  0.0 1267.6 jit_solution(3068066280757769341)
XLA Ops:
  34.4 5.6 convolution_bitcast_fusion
  40.0 44.8 %add_convert_fusion = bf16[16,64,64,256]{3,2,1,0:T(8,128)(2,1)} fusion(bf16[16,64,64,256]{3,2,1,0:T(8,128)(2,1)} %param.36, f32[16,64]{1,0:T(8,128)S(1)} %exp.37, f32[16,8,64,256]{3,2,1,0:T(8,128)} %convolution_bitcast_fusion, f32[16,8,64,64]{3,2,1,0:T(8,128)} %broadcast_multiply_fusion), kind=kOutput, calls=%fused_computation.25 | convolution fusion | flops 872415232 | bytes 77598720 | tf_op jit(solution)/shard_map/rshp,rshn->rhpn/dot_general | solution.py:88
  84.7 25.2 %fusion.78 = (bf16[16,64,64,128]{3,2,1,0:T(8,128)(2,1)}, bf16[16,64,64,128]{3,2,1,0:T(8,128)(2,1)}) fusion(bf16[16,64,64,256]{3,2,1,0:T(8,128)(2,1)} %add_convert_fusion), kind=kLoop, calls=%fused_computation.181 | loop fusion | bytes 67108864 | tf_op jit(solution)/shard_map/jit(_take)/gather | solution.py:177
  110.0 8.5 gather_fusion.15
  118.5 8.4 gather_fusion.14
  126.9 8.5 gather_fusion.13
  135.4 8.5 gather_fusion.12
  143.9 6.6 convolution_bitcast_fusion.1
  150.5 5.0 constant_dynamic-update-slice_fusion.5
  155.5 5.0 constant_dynamic-update-slice_fusion.3
  169.1 13.3 %fusion.77 = (bf16[16,64,64,128]{3,2,1,0:T(8,128)(2,1)}, bf16[16,64,64,128]{3,2,1,0:T(8,128)(2,1)}) fusion(bf16[16,64,64,256]{3,2,1,0:T(8,128)(2,1)S(1)} %copy-done), kind=kLoop, calls=%fused_computation.180 | loop fusion | bytes 67108864 | tf_op jit(solution)/shard_map/jit(_take)/gather | solution.py:195
  182.4 10.5 gather_fusion.18
  192.8 10.4 gather_fusion.19
  203.2 14.6 %pad_maximum_fusion.1 = bf16[8,64,64,256]{3,2,1,0:T(8,128)(2,1)} fusion(bf16[8,64,64,128]{3,2,1,0:T(8,128)(2,1)} %gather_fusion.19, bf16[8,64,64,128]{3,2,1,0:T(8,128)(2,1)} %gather_fusion.18), kind=kLoop, calls=%fused_computation.27 | loop fusion | flops 33554432 | bytes 33554432
  219.9 21.3 %fusion = f32[16,64,8,8]{3,2,1,0:T(8,128)} fusion(f32[16,8,64,256]{3,2,1,0:T(8,128)} %convolution_bitcast_fusion, f32[16,8,64,256]{3,2,1,0:T(8,128)} %convolution_bitcast_fusion.1), kind=kOutput, calls=%fused_computation.28 | convolution fusion | flops 100663296 | bytes 17039360 | tf_op jit(solution)/shard_map/rthn,rshn->rhts/dot_general | solution.py:197
  241.2 7.6 fusion.9
  248.8 24.2 %fusion.7 = f32[16,8,64,64]{3,1,2,0:T(8,128)} fusion(f32[16,64,64,8]{2,3,1,0:T(8,128)S(1)} %fusion.9, f32[16,8,64,64]{3,2,1,0:T(8,128)S(1)} %copy-done.1, bf16[16,64,64,256]{3,2,1,0:T(8,128)(2,1)} %param.36, f32[16,8,64,256]{3,2,1,0:T(8,128)} %convolution_bitcast_fusion.1, f32[64]{0:T(128)S(1)} %copy-done.22, f32[16,8,64]{1,2,0:T(8,128)S(1)} %copy.57), kind=kOutput, calls=%fused_computation.38 | convolution fusion | flops 807403520 | bytes 48267520 | tf_op jit(solution)/shard_map/rhpn,rthn->rthp/dot_general | solution.py:200
  298.9 26.7 %fusion.38 = f32[128,8192]{1,0:T(8,128)} fusion(bf16[4096,8192]{1,0:T(8,128)(2,1)} %param.47, f32[16,8,4096]{2,1,0:T(8,128)} %mul.237, f32[4096]{0:T(1024)S(1)} %copy-done.12, f32[16,8,4096]{2,1,0:T(8,128)S(1)} %reshape.355, bf16[16,8,4096]{2,1,0:T(8,128)(2,1)S(1)} %copy-done.2), kind=kOutput, calls=%fused_computation.85 | convolution fusion | flops 8594653184 | bytes 76562432 | tf_op jit(solution)/shard_map/dot_general | solution.py:213
  330.2 11.1 gather_fusion.17
  341.3 10.7 gather_fusion.16
  356.5 14.3 %pad_maximum_fusion = bf16[8,64,64,256]{3,2,1,0:T(8,128)(2,1)} fusion(bf16[8,64,64,128]{3,2,1,0:T(8,128)(2,1)} %gather_fusion.17, bf16[8,64,64,128]{3,2,1,0:T(8,128)(2,1)} %gather_fusion.16), kind=kLoop, calls=%fused_computation.26 | loop fusion | flops 33554432 | bytes 33554432
  374.5 230.7 %collective-permute-done.6 = bf16[8,3,4096]{2,1,0:T(4,128)(2,1)S(1)} collective-permute-done((bf16[8,3,4096]{2,1,0:T(4,128)(2,1)S(1)}, bf16[8,3,4096]{2,1,0:T(4,128)(2,1)S(1)}, u32[]{:S(2)}, u32[]{:S(2)}) %collective-permute-start.6) | collective-permute-done | bytes 196640 | tf_op jit(solution)/shard_map/ppermute | solution.py:142
  605.2 5.2 all-reduce.3
  630.9 8.0 concatenate.32
  638.9 8.0 concatenate.30
  649.0 274.7 %while.35 = (s32[]{:T(128)}, bf16[8,64,64,256]{3,2,1,0:T(8,128)(2,1)}, s32[]{:T(128)}, s32[8]{0:T(128)S(1)}, bf16[16,64,64,256]{3,2,1,0:T(8,128)(2,1)}, /*index=5*/s32[]{:T(128)}, s32[]{:T(128)}, s32[]{:T(128)}, s32[]{:T(128)}) while((s32[]{:T(128)}, bf16[8,64,64,256]{3,2,1,0:T(8,128)(2,1)}, s32[]{:T(128)}, s32[8]{0:T(128)S(1)}, ...), condition=%wide.region_16.18_spmd, body=%wide.region_15.17_spmd.sunk | while | flops 8 | bytes 16777436 | solution.py:191
  656.6 45.9 %collective-permute-done.1 = bf16[1,64,64,256]{3,2,1,0:T(8,128)(2,1)S(1)} collective-permute-done((bf16[1,64,64,256]{3,2,1,0:T(8,128)(2,1)}, bf16[1,64,64,256]{3,2,1,0:T(8,128)(2,1)S(1)}, u32[]{:S(2)}, u32[]{:S(2)}) %collective-permute-start.1) | collective-permute-done | bytes 2097184 | tf_op jit(solution)/shard_map/while/body/ppermute | solution.py:188
  710.6 46.7 %collective-permute-done.1 = bf16[1,64,64,256]{3,2,1,0:T(8,128)(2,1)S(1)} collective-permute-done((bf16[1,64,64,256]{3,2,1,0:T(8,128)(2,1)}, bf16[1,64,64,256]{3,2,1,0:T(8,128)(2,1)S(1)}, u32[]{:S(2)}, u32[]{:S(2)}) %collective-permute-start.1) | collective-permute-done | bytes 2097184 | tf_op jit(solution)/shard_map/while/body/ppermute | solution.py:188
  764.6 47.6 %collective-permute-done.1 = bf16[1,64,64,256]{3,2,1,0:T(8,128)(2,1)S(1)} collective-permute-done((bf16[1,64,64,256]{3,2,1,0:T(8,128)(2,1)}, bf16[1,64,64,256]{3,2,1,0:T(8,128)(2,1)S(1)}, u32[]{:S(2)}, u32[]{:S(2)}) %collective-permute-start.1) | collective-permute-done | bytes 2097184 | tf_op jit(solution)/shard_map/while/body/ppermute | solution.py:188
  819.3 47.9 %collective-permute-done.1 = bf16[1,64,64,256]{3,2,1,0:T(8,128)(2,1)S(1)} collective-permute-done((bf16[1,64,64,256]{3,2,1,0:T(8,128)(2,1)}, bf16[1,64,64,256]{3,2,1,0:T(8,128)(2,1)S(1)}, u32[]{:S(2)}, u32[]{:S(2)}) %collective-permute-start.1) | collective-permute-done | bytes 2097184 | tf_op jit(solution)/shard_map/while/body/ppermute | solution.py:188
  874.3 47.8 %collective-permute-done.1 = bf16[1,64,64,256]{3,2,1,0:T(8,128)(2,1)S(1)} collective-permute-done((bf16[1,64,64,256]{3,2,1,0:T(8,128)(2,1)}, bf16[1,64,64,256]{3,2,1,0:T(8,128)(2,1)S(1)}, u32[]{:S(2)}, u32[]{:S(2)}) %collective-permute-start.1) | collective-permute-done | bytes 2097184 | tf_op jit(solution)/shard_map/while/body/ppermute | solution.py:188
  923.7 336.6 %while.36 = (s32[]{:T(128)}, bf16[16,64,64,256]{3,2,1,0:T(8,128)(2,1)}, s32[16]{0:T(128)S(1)}, s32[16]{0:T(128)S(1)}, bf16[8,64,64,256]{3,2,1,0:T(8,128)(2,1)}, ...) while((s32[]{:T(128)}, ...), condition=%wide.region_22.24_spmd, body=%wide.region_17.23_spmd.sunk | while | flops 6 | bytes 37749036 | solution.py:154
  925.5 14.1 %conditional.2 = (bf16[8,64,64,256]{3,2,1,0:T(8,128)(2,1)}, s32[]{:T(128)}, s32[]{:T(128)}) conditional(s32[]{:T(128)} %bitcast.80, (bf16[8,64,64,256]{3,2,1,0:T(8,128)(2,1)}, s32[]{:T(128)}) %tuple.122, (bf16[8,64,64,256]{3,2,1,0:T(8,128)(2,1)}, s32[]{:T(128)}) %tuple.123, (bf16[8,64,64,256]{3,2,1,0:T(8,128)(2,1)}, ...), branch_computations={%region_18.19_spmd, %region_19.20_spmd, %region_20.21_spmd, %regio... | conditional | bytes 33554464 | solution.py:150
  925.5 14.1 %copy.95 = bf16[8,64,64,256]{3,2,1,0:T(8,128)(2,1)} copy(bf16[8,64,64,256]{3,2,1,0:T(8,128)(2,1)} %get-tuple-element.480) | data formatting | bytes 33554432 | tf_op jit(solution)/shard_map/while/body/eval_jaxpr/cond
  946.6 14.1 %conditional.2 = (bf16[8,64,64,256]{3,2,1,0:T(8,128)(2,1)}, s32[]{:T(128)}, s32[]{:T(128)}) conditional(s32[]{:T(128)} %bitcast.80, (bf16[8,64,64,256]{3,2,1,0:T(8,128)(2,1)}, s32[]{:T(128)}) %tuple.122, (bf16[8,64,64,256]{3,2,1,0:T(8,128)(2,1)}, s32[]{:T(128)}) %tuple.123, (bf16[8,64,64,256]{3,2,1,0:T(8,128)(2,1)}, ...), branch_computations={%region_18.19_spmd, %region_19.20_spmd, %region_20.21_spmd, %regio... | conditional | bytes 33554464 | solution.py:150
  946.6 14.1 %copy.95 = bf16[8,64,64,256]{3,2,1,0:T(8,128)(2,1)} copy(bf16[8,64,64,256]{3,2,1,0:T(8,128)(2,1)} %get-tuple-element.480) | data formatting | bytes 33554432 | tf_op jit(solution)/shard_map/while/body/eval_jaxpr/cond
  967.6 14.1 %conditional.2 = (bf16[8,64,64,256]{3,2,1,0:T(8,128)(2,1)}, s32[]{:T(128)}, s32[]{:T(128)}) conditional(s32[]{:T(128)} %bitcast.80, (bf16[8,64,64,256]{3,2,1,0:T(8,128)(2,1)}, s32[]{:T(128)}) %tuple.122, (bf16[8,64,64,256]{3,2,1,0:T(8,128)(2,1)}, s32[]{:T(128)}) %tuple.123, (bf16[8,64,64,256]{3,2,1,0:T(8,128)(2,1)}, ...), branch_computations={%region_18.19_spmd, %region_19.20_spmd, %region_20.21_spmd, %regio... | conditional | bytes 33554464 | solution.py:150
  967.6 14.1 %copy.97 = bf16[8,64,64,256]{3,2,1,0:T(8,128)(2,1)} copy(bf16[8,64,64,256]{3,2,1,0:T(8,128)(2,1)} %get-tuple-element.483) | data formatting | bytes 33554432 | tf_op jit(solution)/shard_map/while/body/eval_jaxpr/cond
  988.7 14.1 %conditional.2 = (bf16[8,64,64,256]{3,2,1,0:T(8,128)(2,1)}, s32[]{:T(128)}, s32[]{:T(128)}) conditional(s32[]{:T(128)} %bitcast.80, (bf16[8,64,64,256]{3,2,1,0:T(8,128)(2,1)}, s32[]{:T(128)}) %tuple.122, (bf16[8,64,64,256]{3,2,1,0:T(8,128)(2,1)}, s32[]{:T(128)}) %tuple.123, (bf16[8,64,64,256]{3,2,1,0:T(8,128)(2,1)}, ...), branch_computations={%region_18.19_spmd, %region_19.20_spmd, %region_20.21_spmd, %regio... | conditional | bytes 33554464 | solution.py:150
  988.7 14.1 %copy.97 = bf16[8,64,64,256]{3,2,1,0:T(8,128)(2,1)} copy(bf16[8,64,64,256]{3,2,1,0:T(8,128)(2,1)} %get-tuple-element.483) | data formatting | bytes 33554432 | tf_op jit(solution)/shard_map/while/body/eval_jaxpr/cond
  1009.7 14.1 %conditional.2 = (bf16[8,64,64,256]{3,2,1,0:T(8,128)(2,1)}, s32[]{:T(128)}, s32[]{:T(128)}) conditional(s32[]{:T(128)} %bitcast.80, (bf16[8,64,64,256]{3,2,1,0:T(8,128)(2,1)}, s32[]{:T(128)}) %tuple.122, (bf16[8,64,64,256]{3,2,1,0:T(8,128)(2,1)}, s32[]{:T(128)}) %tuple.123, (bf16[8,64,64,256]{3,2,1,0:T(8,128)(2,1)}, ...), branch_computations={%region_18.19_spmd, %region_19.20_spmd, %region_20.21_spmd, %regio... | conditional | bytes 33554464 | solution.py:150
  1009.7 14.1 %copy.97 = bf16[8,64,64,256]{3,2,1,0:T(8,128)(2,1)} copy(bf16[8,64,64,256]{3,2,1,0:T(8,128)(2,1)} %get-tuple-element.483) | data formatting | bytes 33554432 | tf_op jit(solution)/shard_map/while/body/eval_jaxpr/cond
  1030.8 14.1 %conditional.2 = (bf16[8,64,64,256]{3,2,1,0:T(8,128)(2,1)}, s32[]{:T(128)}, s32[]{:T(128)}) conditional(s32[]{:T(128)} %bitcast.80, (bf16[8,64,64,256]{3,2,1,0:T(8,128)(2,1)}, s32[]{:T(128)}) %tuple.122, (bf16[8,64,64,256]{3,2,1,0:T(8,128)(2,1)}, s32[]{:T(128)}) %tuple.123, (bf16[8,64,64,256]{3,2,1,0:T(8,128)(2,1)}, ...), branch_computations={%region_18.19_spmd, %region_19.20_spmd, %region_20.21_spmd, %regio... | conditional | bytes 33554464 | solution.py:150
  1030.8 14.1 %copy.97 = bf16[8,64,64,256]{3,2,1,0:T(8,128)(2,1)} copy(bf16[8,64,64,256]{3,2,1,0:T(8,128)(2,1)} %get-tuple-element.483) | data formatting | bytes 33554432 | tf_op jit(solution)/shard_map/while/body/eval_jaxpr/cond
  1051.8 14.1 %conditional.2 = (bf16[8,64,64,256]{3,2,1,0:T(8,128)(2,1)}, s32[]{:T(128)}, s32[]{:T(128)}) conditional(s32[]{:T(128)} %bitcast.80, (bf16[8,64,64,256]{3,2,1,0:T(8,128)(2,1)}, s32[]{:T(128)}) %tuple.122, (bf16[8,64,64,256]{3,2,1,0:T(8,128)(2,1)}, s32[]{:T(128)}) %tuple.123, (bf16[8,64,64,256]{3,2,1,0:T(8,128)(2,1)}, ...), branch_computations={%region_18.19_spmd, %region_19.20_spmd, %region_20.21_spmd, %regio... | conditional | bytes 33554464 | solution.py:150
  1051.8 14.1 %copy.97 = bf16[8,64,64,256]{3,2,1,0:T(8,128)(2,1)} copy(bf16[8,64,64,256]{3,2,1,0:T(8,128)(2,1)} %get-tuple-element.483) | data formatting | bytes 33554432 | tf_op jit(solution)/shard_map/while/body/eval_jaxpr/cond
  1072.8 14.1 %conditional.2 = (bf16[8,64,64,256]{3,2,1,0:T(8,128)(2,1)}, s32[]{:T(128)}, s32[]{:T(128)}) conditional(s32[]{:T(128)} %bitcast.80, (bf16[8,64,64,256]{3,2,1,0:T(8,128)(2,1)}, s32[]{:T(128)}) %tuple.122, (bf16[8,64,64,256]{3,2,1,0:T(8,128)(2,1)}, s32[]{:T(128)}) %tuple.123, (bf16[8,64,64,256]{3,2,1,0:T(8,128)(2,1)}, ...), branch_computations={%region_18.19_spmd, %region_19.20_spmd, %region_20.21_spmd, %regio... | conditional | bytes 33554464 | solution.py:150
  1072.8 14.1 %copy.97 = bf16[8,64,64,256]{3,2,1,0:T(8,128)(2,1)} copy(bf16[8,64,64,256]{3,2,1,0:T(8,128)(2,1)} %get-tuple-element.483) | data formatting | bytes 33554432 | tf_op jit(solution)/shard_map/while/body/eval_jaxpr/cond
  1093.9 14.1 %conditional.2 = (bf16[8,64,64,256]{3,2,1,0:T(8,128)(2,1)}, s32[]{:T(128)}, s32[]{:T(128)}) conditional(s32[]{:T(128)} %bitcast.80, (bf16[8,64,64,256]{3,2,1,0:T(8,128)(2,1)}, s32[]{:T(128)}) %tuple.122, (bf16[8,64,64,256]{3,2,1,0:T(8,128)(2,1)}, s32[]{:T(128)}) %tuple.123, (bf16[8,64,64,256]{3,2,1,0:T(8,128)(2,1)}, ...), branch_computations={%region_18.19_spmd, %region_19.20_spmd, %region_20.21_spmd, %regio... | conditional | bytes 33554464 | solution.py:150
  1093.9 14.1 %copy.97 = bf16[8,64,64,256]{3,2,1,0:T(8,128)(2,1)} copy(bf16[8,64,64,256]{3,2,1,0:T(8,128)(2,1)} %get-tuple-element.483) | data formatting | bytes 33554432 | tf_op jit(solution)/shard_map/while/body/eval_jaxpr/cond
  1114.9 14.1 %conditional.2 = (bf16[8,64,64,256]{3,2,1,0:T(8,128)(2,1)}, s32[]{:T(128)}, s32[]{:T(128)}) conditional(s32[]{:T(128)} %bitcast.80, (bf16[8,64,64,256]{3,2,1,0:T(8,128)(2,1)}, s32[]{:T(128)}) %tuple.122, (bf16[8,64,64,256]{3,2,1,0:T(8,128)(2,1)}, s32[]{:T(128)}) %tuple.123, (bf16[8,64,64,256]{3,2,1,0:T(8,128)(2,1)}, ...), branch_computations={%region_18.19_spmd, %region_19.20_spmd, %region_20.21_spmd, %regio... | conditional | bytes 33554464 | solution.py:150
  1114.9 14.1 %copy.97 = bf16[8,64,64,256]{3,2,1,0:T(8,128)(2,1)} copy(bf16[8,64,64,256]{3,2,1,0:T(8,128)(2,1)} %get-tuple-element.483) | data formatting | bytes 33554432 | tf_op jit(solution)/shard_map/while/body/eval_jaxpr/cond
  1136.0 14.1 %conditional.2 = (bf16[8,64,64,256]{3,2,1,0:T(8,128)(2,1)}, s32[]{:T(128)}, s32[]{:T(128)}) conditional(s32[]{:T(128)} %bitcast.80, (bf16[8,64,64,256]{3,2,1,0:T(8,128)(2,1)}, s32[]{:T(128)}) %tuple.122, (bf16[8,64,64,256]{3,2,1,0:T(8,128)(2,1)}, s32[]{:T(128)}) %tuple.123, (bf16[8,64,64,256]{3,2,1,0:T(8,128)(2,1)}, ...), branch_computations={%region_18.19_spmd, %region_19.20_spmd, %region_20.21_spmd, %regio... | conditional | bytes 33554464 | solution.py:150
  1136.0 14.1 %copy.99 = bf16[8,64,64,256]{3,2,1,0:T(8,128)(2,1)} copy(bf16[8,64,64,256]{3,2,1,0:T(8,128)(2,1)} %get-tuple-element.486) | data formatting | bytes 33554432 | tf_op jit(solution)/shard_map/while/body/eval_jaxpr/cond
  1157.0 14.1 %conditional.2 = (bf16[8,64,64,256]{3,2,1,0:T(8,128)(2,1)}, s32[]{:T(128)}, s32[]{:T(128)}) conditional(s32[]{:T(128)} %bitcast.80, (bf16[8,64,64,256]{3,2,1,0:T(8,128)(2,1)}, s32[]{:T(128)}) %tuple.122, (bf16[8,64,64,256]{3,2,1,0:T(8,128)(2,1)}, s32[]{:T(128)}) %tuple.123, (bf16[8,64,64,256]{3,2,1,0:T(8,128)(2,1)}, ...), branch_computations={%region_18.19_spmd, %region_19.20_spmd, %region_20.21_spmd, %regio... | conditional | bytes 33554464 | solution.py:150
  1157.0 14.1 %copy.99 = bf16[8,64,64,256]{3,2,1,0:T(8,128)(2,1)} copy(bf16[8,64,64,256]{3,2,1,0:T(8,128)(2,1)} %get-tuple-element.486) | data formatting | bytes 33554432 | tf_op jit(solution)/shard_map/while/body/eval_jaxpr/cond
  1178.0 14.1 %conditional.2 = (bf16[8,64,64,256]{3,2,1,0:T(8,128)(2,1)}, s32[]{:T(128)}, s32[]{:T(128)}) conditional(s32[]{:T(128)} %bitcast.80, (bf16[8,64,64,256]{3,2,1,0:T(8,128)(2,1)}, s32[]{:T(128)}) %tuple.122, (bf16[8,64,64,256]{3,2,1,0:T(8,128)(2,1)}, s32[]{:T(128)}) %tuple.123, (bf16[8,64,64,256]{3,2,1,0:T(8,128)(2,1)}, ...), branch_computations={%region_18.19_spmd, %region_19.20_spmd, %region_20.21_spmd, %regio... | conditional | bytes 33554464 | solution.py:150
  1178.0 14.1 %copy.99 = bf16[8,64,64,256]{3,2,1,0:T(8,128)(2,1)} copy(bf16[8,64,64,256]{3,2,1,0:T(8,128)(2,1)} %get-tuple-element.486) | data formatting | bytes 33554432 | tf_op jit(solution)/shard_map/while/body/eval_jaxpr/cond
  1199.1 14.1 %conditional.2 = (bf16[8,64,64,256]{3,2,1,0:T(8,128)(2,1)}, s32[]{:T(128)}, s32[]{:T(128)}) conditional(s32[]{:T(128)} %bitcast.80, (bf16[8,64,64,256]{3,2,1,0:T(8,128)(2,1)}, s32[]{:T(128)}) %tuple.122, (bf16[8,64,64,256]{3,2,1,0:T(8,128)(2,1)}, s32[]{:T(128)}) %tuple.123, (bf16[8,64,64,256]{3,2,1,0:T(8,128)(2,1)}, ...), branch_computations={%region_18.19_spmd, %region_19.20_spmd, %region_20.21_spmd, %regio... | conditional | bytes 33554464 | solution.py:150
  1199.1 14.1 %copy.101 = bf16[8,64,64,256]{3,2,1,0:T(8,128)(2,1)} copy(bf16[8,64,64,256]{3,2,1,0:T(8,128)(2,1)} %get-tuple-element.489) | data formatting | bytes 33554432 | tf_op jit(solution)/shard_map/while/body/eval_jaxpr/cond
  1220.1 14.1 %conditional.2 = (bf16[8,64,64,256]{3,2,1,0:T(8,128)(2,1)}, s32[]{:T(128)}, s32[]{:T(128)}) conditional(s32[]{:T(128)} %bitcast.80, (bf16[8,64,64,256]{3,2,1,0:T(8,128)(2,1)}, s32[]{:T(128)}) %tuple.122, (bf16[8,64,64,256]{3,2,1,0:T(8,128)(2,1)}, s32[]{:T(128)}) %tuple.123, (bf16[8,64,64,256]{3,2,1,0:T(8,128)(2,1)}, ...), branch_computations={%region_18.19_spmd, %region_19.20_spmd, %region_20.21_spmd, %regio... | conditional | bytes 33554464 | solution.py:150
  1220.1 14.1 %copy.101 = bf16[8,64,64,256]{3,2,1,0:T(8,128)(2,1)} copy(bf16[8,64,64,256]{3,2,1,0:T(8,128)(2,1)} %get-tuple-element.489) | data formatting | bytes 33554432 | tf_op jit(solution)/shard_map/while/body/eval_jaxpr/cond
  1241.2 14.1 %conditional.2 = (bf16[8,64,64,256]{3,2,1,0:T(8,128)(2,1)}, s32[]{:T(128)}, s32[]{:T(128)}) conditional(s32[]{:T(128)} %bitcast.80, (bf16[8,64,64,256]{3,2,1,0:T(8,128)(2,1)}, s32[]{:T(128)}) %tuple.122, (bf16[8,64,64,256]{3,2,1,0:T(8,128)(2,1)}, s32[]{:T(128)}) %tuple.123, (bf16[8,64,64,256]{3,2,1,0:T(8,128)(2,1)}, ...), branch_computations={%region_18.19_spmd, %region_19.20_spmd, %region_20.21_spmd, %regio... | conditional | bytes 33554464 | solution.py:150
  1241.2 14.1 %copy.101 = bf16[8,64,64,256]{3,2,1,0:T(8,128)(2,1)} copy(bf16[8,64,64,256]{3,2,1,0:T(8,128)(2,1)} %get-tuple-element.489) | data formatting | bytes 33554432 | tf_op jit(solution)/shard_map/while/body/eval_jaxpr/cond
  (223 shorter events, 197.2 us)
Async XLA Ops:
  7.2 639.7 %reduce-scatter.2.cloned.1.call-start = ((), (), s32[]{:S(2)}) async-start(), calls=%async_computation.1 | async-start | bytes 5242880 | tf_op jit(solution)/shard_map/reduce_scatter | solution.py:219
  10.1 0.6 copy-start.20
  12.1 3.0 copy-start.26
  12.9 9.3 copy-start.16
  12.9 9.3 copy-start.18
  13.9 8.3 copy-start.13
  18.5 6.2 copy-start.6
  20.1 2.2 copy-start.4
  23.6 1.5 copy-start.8
  23.6 2.1 copy-start.14
  30.1 4.3 copy-start.3
  143.9 25.2 %copy-start = (bf16[16,64,64,256]{3,2,1,0:T(8,128)(2,1)S(1)}, bf16[16,64,64,256]{3,2,1,0:T(8,128)(2,1)}, u32[]{:S(2)}) copy-start(bf16[16,64,64,256]{3,2,1,0:T(8,128)(2,1)} %add_convert_fusion) | copy-start | bytes 100663296
  217.8 705.8 %collective-permute-start.2 = (bf16[8,64,64,256]{3,2,1,0:T(8,128)(2,1)}, bf16[8,64,64,256]{3,2,1,0:T(8,128)(2,1)}, u32[]{:S(2)}, u32[]{:S(2)}) collective-permute-start(bf16[8,64,64,256]{3,2,1,0:T(8,128)(2,1)} %pad_maximum_fusion.1), channel_id=1, source_target_pairs={{0,1},{1,0},{2,3},{3,2},{4,5},{5,4},{6,7},{7,6},{8,9},{9,8},{10,11... | collective-permute-start | bytes 50331656 | tf_op jit(solution)/shard_map/ppermute | solution.py:196
  219.9 21.3 %copy-start.1 = (f32[16,8,64,64]{3,2,1,0:T(8,128)S(1)}, f32[16,8,64,64]{3,2,1,0:T(8,128)}, u32[]{:S(2)}) copy-start(f32[16,8,64,64]{3,2,1,0:T(8,128)} %reshape.352) | copy-start | bytes 6291460
  241.2 7.6 copy-start.22
  277.9 3.6 copy-start.2
  294.2 4.8 copy-start.12
  325.6 2.6 copy-start.15
  325.6 2.7 copy-start.7
  325.6 2.7 copy-start.9
  325.6 4.5 copy-start.24
  325.7 305.2 %collective-permute-start.4 = (bf16[3,64,64,256]{3,2,1,0:T(8,128)(2,1)}, bf16[3,64,64,256]{3,2,1,0:T(8,128)(2,1)}, u32[]{:S(2)}, u32[]{:S(2)}) collective-permute-start(bf16[3,64,64,256]{3,2,1,0:T(8,128)(2,1)} %constant_dynamic-update-slice_fusion.4), channel_id=1, source_target_pairs={{0,3},{1,2},{2,1},{3,0},{4,7},{5,6},{6,5},{7,4},{8,11},{9,10},{10,... | collective-permute-start | bytes 18874376 | tf_op jit(solution)/shard_map/ppermute | solution.py:179
  328.2 310.6 %collective-permute-start.3 = (bf16[3,64,64,256]{3,2,1,0:T(8,128)(2,1)}, bf16[3,64,64,256]{3,2,1,0:T(8,128)(2,1)}, u32[]{:S(2)}, u32[]{:S(2)}) collective-permute-start(bf16[3,64,64,256]{3,2,1,0:T(8,128)(2,1)} %constant_dynamic-update-slice_fusion.2), channel_id=1, source_target_pairs={{0,2},{1,3},{2,0},{3,1},{4,6},{5,7},{6,4},{7,5},{8,10},{9,11},{10,... | collective-permute-start | bytes 18874376 | tf_op jit(solution)/shard_map/ppermute | solution.py:179
  329.9 44.4 %collective-permute-start.5 = (bf16[8,3,4096]{2,1,0:T(4,128)(2,1)S(1)}, bf16[8,3,4096]{2,1,0:T(4,128)(2,1)S(1)}, u32[]{:S(2)}, u32[]{:S(2)}) collective-permute-start(bf16[8,3,4096]{2,1,0:T(4,128)(2,1)S(1)} %gather_fusion.3), channel_id=1, source_target_pairs={{0,1},{1,0},{2,3},{3,2},{4,5},{5,4},{6,7},{7,6},{8,9},{9,8},{10,11... | collective-permute-start | bytes 589832 | tf_op jit(solution)/shard_map/ppermute | solution.py:142
  341.3 10.7 copy-start.23
  341.3 10.7 copy-start.21
  341.3 13.5 %copy-start.17 = (s32[8]{0:T(128)S(1)}, s32[8]{0:T(128)}, u32[]{:S(2)}) copy-start(s32[8]{0:T(128)} %copy-done.16) | copy-start | bytes 100
  341.3 14.3 %copy-start.5 = (bf16[16,3,4096]{2,1,0:T(4,128)(2,1)S(1)}, bf16[16,3,4096]{2,1,0:T(4,128)(2,1)}, u32[]{:S(2)}) copy-start(bf16[16,3,4096]{2,1,0:T(4,128)(2,1)} %copy-done.4) | copy-start | bytes 1179652
  341.3 14.3 %copy-start.10 = (bf16[16,8,4096]{2,1,0:T(8,128)(2,1)S(1)}, bf16[16,8,4096]{2,1,0:T(8,128)(2,1)}, u32[]{:S(2)}) copy-start(bf16[16,8,4096]{2,1,0:T(8,128)(2,1)} %param.32) | copy-start | bytes 3145732
  356.4 16.2 %copy-start.19 = (s32[8]{0:T(128)S(1)}, s32[8]{0:T(128)}, u32[]{:S(2)}) copy-start(s32[8]{0:T(128)} %copy-done.18) | copy-start | bytes 100
  356.4 17.7 %copy-start.25 = (s32[64]{0:T(128)S(1)}, s32[64]{0:T(128)}, u32[]{:S(2)}) copy-start(s32[64]{0:T(128)} %get-tuple-element.293) | copy-start | bytes 772
  356.5 17.7 %copy-start.27 = (s32[64]{0:T(128)S(1)}, s32[64]{0:T(128)}, u32[]{:S(2)}) copy-start(s32[64]{0:T(128)} %copy-done.26) | copy-start | bytes 772
  370.7 234.4 %collective-permute-start.6 = (bf16[8,3,4096]{2,1,0:T(4,128)(2,1)S(1)}, bf16[8,3,4096]{2,1,0:T(4,128)(2,1)S(1)}, u32[]{:S(2)}, u32[]{:S(2)}) collective-permute-start(bf16[8,3,4096]{2,1,0:T(4,128)(2,1)S(1)} %gather_fusion.4), channel_id=1, source_target_pairs={{0,2},{1,3},{2,0},{3,1},{4,6},{5,7},{6,4},{7,5},{8,10},{9,11},{10,... | collective-permute-start | bytes 589832 | tf_op jit(solution)/shard_map/ppermute | solution.py:142
  374.3 240.5 %collective-permute-start.7 = (bf16[8,3,4096]{2,1,0:T(4,128)(2,1)S(1)}, bf16[8,3,4096]{2,1,0:T(4,128)(2,1)}, u32[]{:S(2)}, u32[]{:S(2)}) collective-permute-start(bf16[8,3,4096]{2,1,0:T(4,128)(2,1)S(1)} %gather_fusion.5), channel_id=1, source_target_pairs={{0,3},{1,2},{2,1},{3,0},{4,7},{5,6},{6,5},{7,4},{8,11},{9,10},{10,... | collective-permute-start | bytes 589832 | tf_op jit(solution)/shard_map/ppermute | solution.py:142
  605.1 5.2 copy-start.11
  605.1 11.8 collective-permute-start.8
  614.8 9.3 collective-permute-start.9
  617.0 11.1 collective-permute-start.10
  654.7 47.8 %collective-permute-start.1 = (bf16[1,64,64,256]{3,2,1,0:T(8,128)(2,1)}, bf16[1,64,64,256]{3,2,1,0:T(8,128)(2,1)S(1)}, u32[]{:S(2)}, u32[]{:S(2)}) collective-permute-start(bf16[1,64,64,256]{3,2,1,0:T(8,128)(2,1)} %constant_dynamic-slice_fusion.9), channel_id=1, source_target_pairs={{0,3},{1,2},{2,1},{3,0},{4,7},{5,6},{6,5},{7,4},{8,11},{9,10},{10,... | collective-permute-start | bytes 6291464 | tf_op jit(solution)/shard_map/while/body/ppermute | solution.py:188
  709.6 47.7 %collective-permute-start.1 = (bf16[1,64,64,256]{3,2,1,0:T(8,128)(2,1)}, bf16[1,64,64,256]{3,2,1,0:T(8,128)(2,1)S(1)}, u32[]{:S(2)}, u32[]{:S(2)}) collective-permute-start(bf16[1,64,64,256]{3,2,1,0:T(8,128)(2,1)} %constant_dynamic-slice_fusion.9), channel_id=1, source_target_pairs={{0,3},{1,2},{2,1},{3,0},{4,7},{5,6},{6,5},{7,4},{8,11},{9,10},{10,... | collective-permute-start | bytes 6291464 | tf_op jit(solution)/shard_map/while/body/ppermute | solution.py:188
  764.4 47.8 %collective-permute-start.1 = (bf16[1,64,64,256]{3,2,1,0:T(8,128)(2,1)}, bf16[1,64,64,256]{3,2,1,0:T(8,128)(2,1)S(1)}, u32[]{:S(2)}, u32[]{:S(2)}) collective-permute-start(bf16[1,64,64,256]{3,2,1,0:T(8,128)(2,1)} %constant_dynamic-slice_fusion.9), channel_id=1, source_target_pairs={{0,3},{1,2},{2,1},{3,0},{4,7},{5,6},{6,5},{7,4},{8,11},{9,10},{10,... | collective-permute-start | bytes 6291464 | tf_op jit(solution)/shard_map/while/body/ppermute | solution.py:188
  819.3 47.9 %collective-permute-start.1 = (bf16[1,64,64,256]{3,2,1,0:T(8,128)(2,1)}, bf16[1,64,64,256]{3,2,1,0:T(8,128)(2,1)S(1)}, u32[]{:S(2)}, u32[]{:S(2)}) collective-permute-start(bf16[1,64,64,256]{3,2,1,0:T(8,128)(2,1)} %constant_dynamic-slice_fusion.9), channel_id=1, source_target_pairs={{0,3},{1,2},{2,1},{3,0},{4,7},{5,6},{6,5},{7,4},{8,11},{9,10},{10,... | collective-permute-start | bytes 6291464 | tf_op jit(solution)/shard_map/while/body/ppermute | solution.py:188
  874.3 47.8 %collective-permute-start.1 = (bf16[1,64,64,256]{3,2,1,0:T(8,128)(2,1)}, bf16[1,64,64,256]{3,2,1,0:T(8,128)(2,1)S(1)}, u32[]{:S(2)}, u32[]{:S(2)}) collective-permute-start(bf16[1,64,64,256]{3,2,1,0:T(8,128)(2,1)} %constant_dynamic-slice_fusion.9), channel_id=1, source_target_pairs={{0,3},{1,2},{2,1},{3,0},{4,7},{5,6},{6,5},{7,4},{8,11},{9,10},{10,... | collective-permute-start | bytes 6291464 | tf_op jit(solution)/shard_map/while/body/ppermute | solution.py:188
Sparse Core Ops, SparseCore 0:
  325.8 78.8 reduce-scatter.1

commit v5 on v3

--- a/solution.py
+++ b/solution.py
@@ -177,14 +177,19 @@
     )
     first_slots = min(3, cap)
     state_pieces = [jnp.take(retained, own_index, axis=0, mode="clip")]
+    first_index = send_index.reshape(owners, cap)[:, :first_slots].reshape(-1)
+    first_arrivals = lax.all_to_all(
+        jnp.take(retained, first_index, axis=0, mode="clip"), "req", 0, 0, tiled=True
+    )
     for bits, index in zip(partner_bits, pair_index):
         pairs = [(i, i ^ bits) for i in range(owners)]
         if bits == 1:
             outgoing = jnp.take(retained, index, axis=0, mode="clip")
             state_pieces.append(lax.ppermute(outgoing, "req", pairs))
             continue
-        outgoing = jnp.take(retained, index[:first_slots], axis=0, mode="clip")
-        arrived = lax.ppermute(outgoing, "req", pairs)
+        arrived = lax.dynamic_slice_in_dim(
+            first_arrivals, (req_index ^ bits) * first_slots, first_slots, 0
+        )
         buffer = jnp.concatenate(
             [arrived, jnp.zeros((cap - first_slots,) + arrived.shape[1:], arrived.dtype)], axis=0
         )

time: 1040 us -> 911 us (0.88)
  waiting for transfers between devices: 479 us -> 323 us
  other arithmetic: 121 us -> 139 us
    ppermute x6, waiting for transfers between devices: 246 us -> 91 us  [send_pieces(): pieces.append(lax.ppermute(outgoing, 'req', pairs))]
    unnamed x3 -> x2, other arithmetic: 26.3 us -> 43.8 us
    dynamic_slice x0 -> x1, local copies, waits for them, and re-layouts: none -> 11.8 us  [on_device(): lax.dynamic_slice_in_dim(first_arrivals, (req_index ^ bits) * first_slots...]
    gather x4 -> x2, local copies, waits for them, and re-layouts: 31.7 us -> 23.4 us  [on_device(): jnp.take(retained, first_index, axis=0, mode='clip')]
  transfers between devices with their start and end apart: 15 -> 14, of which waited for: 8 -> 9; matrix products, arithmetic and copies ran while one was open for 23% -> 25% of each run, Pallas kernels for 0% -> 0%
where the time goes in v5:
time: 911 us; the launch traced here: 899 us
  waiting for transfers between devices  323 us (35%)
  local copies, waits for them, and re-layouts  253 us (28%)
  matrix products  140 us (15%)
  other arithmetic  139 us (15%)
  between operations  16.1 us (2%)
  starting transfers between devices  15.2 us (2%)
    ppermute x5, waiting for transfers between devices, one_slot(): got = lax.ppermute(row, 'req', pairs)  232 us
    ppermute x6, waiting for transfers between devices, send_pieces(): pieces.append(lax.ppermute(outgoing, 'req', pairs))  91 us
    gather x3, local copies, waits for them, and re-layouts, on_device(): jnp.take(jnp.concatenate(state_pieces, axis=0), gather_index, axis=0, mod...  67 us
    gather x3, local copies, waits for them, and re-layouts, on_device(): state_pieces = [jnp.take(retained, own_index, axis=0, mode='clip')]  46.2 us
    dot_general x1, matrix products, on_device(): jnp.einsum('rshp,rshn->rhpn', weighted_x, b_heads, precision=highest)  45 us
    concatenate x1, other arithmetic, on_device(): jnp.concatenate(state_pieces, axis=0)  44.4 us
    unnamed x2, other arithmetic  43.8 us
    dot_general x1, matrix products, on_device(): jnp.dot(normed.reshape(local_requests * L, local_heads * P_SIZE), out_wei...  26.8 us
  transfers between devices with their start and end apart: 14, of which 9 were waited for; matrix products, arithmetic and copies ran while one was open for 25% of the time, Pallas kernels for 0%

profile of v5, /device:TPU:0, one launch (start us, length us, event | category | flops | bytes accessed | tf_op | source)
XLA Modules:
  0.0 899.3 jit_solution(6803595443513854326)
XLA Ops:
  10.1 1.4 convert_reduce_fusion
  17.4 1.5 copy.48
  19.0 2.1 fusion.35
  25.9 3.0 reshape.351
  28.9 4.1 broadcast_multiply_fusion
  33.1 5.7 convolution_bitcast_fusion
  38.7 45.0 %add_convert_fusion = bf16[16,64,64,256]{3,2,1,0:T(8,128)(2,1)} fusion(bf16[16,64,64,256]{3,2,1,0:T(8,128)(2,1)} %param.30, f32[16,64]{1,0:T(8,128)S(1)} %exp.40, f32[16,8,64,256]{3,2,1,0:T(8,128)} %convolution_bitcast_fusion, f32[16,8,64,64]{3,2,1,0:T(8,128)} %broadcast_multiply_fusion), kind=kOutput, calls=%fused_computation.25 | convolution fusion | flops 872415232 | bytes 77598720 | tf_op jit(solution)/shard_map/rshp,rshn->rhpn/dot_general | solution.py:95
  83.7 25.1 %fusion.78 = (bf16[16,64,64,128]{3,2,1,0:T(8,128)(2,1)}, bf16[16,64,64,128]{3,2,1,0:T(8,128)(2,1)}) fusion(bf16[16,64,64,256]{3,2,1,0:T(8,128)(2,1)} %add_convert_fusion), kind=kLoop, calls=%fused_computation.177 | loop fusion | bytes 67108864 | tf_op jit(solution)/shard_map/jit(_take)/gather | solution.py:179
  108.8 11.7 %gather_fusion.16 = bf16[12,64,64,128]{3,2,1,0:T(8,128)(2,1)} fusion(bf16[16,64,64,128]{3,2,1,0:T(8,128)(2,1)} %get-tuple-element.114, s32[1024]{0:T(1024)S(1)} %pad_clamp_fusion.3), kind=kCustom, calls=%fused_computation.16 | custom fusion | bytes 25165872 | tf_op jit(solution)/shard_map/jit(_take)/gather | solution.py:182
  120.5 11.7 %gather_fusion.17 = bf16[12,64,64,128]{3,2,1,0:T(8,128)(2,1)} fusion(bf16[16,64,64,128]{3,2,1,0:T(8,128)(2,1)} %get-tuple-element.115, s32[1024]{0:T(1024)S(1)} %pad_clamp_fusion.3), kind=kCustom, calls=%fused_computation.17 | custom fusion | bytes 25165872 | tf_op jit(solution)/shard_map/jit(_take)/gather | solution.py:182
  132.2 21.1 %pad_maximum_fusion.2 = bf16[12,64,64,256]{3,2,1,0:T(8,128)(2,1)} fusion(bf16[12,64,64,128]{3,2,1,0:T(8,128)(2,1)} %gather_fusion.17, bf16[12,64,64,128]{3,2,1,0:T(8,128)(2,1)} %gather_fusion.16), kind=kLoop, calls=%fused_computation.27 | loop fusion | flops 50331648 | bytes 50331648
  153.4 8.4 all-to-all-start
  161.9 10.5 %gather_fusion.14 = bf16[8,64,64,128]{3,2,1,0:T(8,128)(2,1)} fusion(bf16[16,64,64,128]{3,2,1,0:T(8,128)(2,1)} %get-tuple-element.114, s32[1024]{0:T(1024)S(1)} %pad_clamp_fusion.4), kind=kCustom, calls=%fused_computation.14 | custom fusion | bytes 16777248 | tf_op jit(solution)/shard_map/jit(_take)/gather | solution.py:187
  172.4 10.4 %gather_fusion.15 = bf16[8,64,64,128]{3,2,1,0:T(8,128)(2,1)} fusion(bf16[16,64,64,128]{3,2,1,0:T(8,128)(2,1)} %get-tuple-element.115, s32[1024]{0:T(1024)S(1)} %pad_clamp_fusion.4), kind=kCustom, calls=%fused_computation.15 | custom fusion | bytes 16777248 | tf_op jit(solution)/shard_map/jit(_take)/gather | solution.py:187
  182.7 22.7 %pad_maximum_fusion.3 = bf16[8,64,64,256]{3,2,1,0:T(8,128)(2,1)} fusion(bf16[8,64,64,128]{3,2,1,0:T(8,128)(2,1)} %gather_fusion.15, bf16[8,64,64,128]{3,2,1,0:T(8,128)(2,1)} %gather_fusion.14), kind=kLoop, calls=%fused_computation.28 | loop fusion | flops 33554432 | bytes 33554432
  206.3 3.6 convolution_bitcast_fusion.1
  209.9 21.8 %fusion.1 = f32[16,64,8,8]{3,2,1,0:T(8,128)} fusion(f32[16,8,64,256]{3,2,1,0:T(8,128)} %convolution_bitcast_fusion, f32[16,8,64,256]{3,2,1,0:T(8,128)S(1)} %convolution_bitcast_fusion.1), kind=kOutput, calls=%fused_computation.30 | convolution fusion | flops 100663296 | bytes 17039360 | tf_op jit(solution)/shard_map/rthn,rshn->rhts/dot_general | solution.py:80
  231.7 10.3 %fusion.9 = f32[16,64,64,8]{2,3,1,0:T(8,128)} fusion(f32[16,64,8,8]{3,2,1,0:T(8,128)} %fusion.1, f32[16,8,64,64]{3,2,1,0:T(8,128)} %reshape.351, f32[16,64,8]{2,1,0:T(8,128)S(1)} %copy.53, f32[16,64,8]{2,1,0:T(8,128)S(1)} %copy.51, pred[8,8]{1,0:T(8,128)(4,1)S(1)} %iota_compare_fusion.8), kind=kOutput, calls=%fused_computation.41 | convolution fusion | flops 25427968 | bytes 4522048 | tf_op jit(solution)/shard_map/rhts,rshp->rthp/dot_general | solution.py:82
  242.2 23.6 %fusion.7 = f32[16,8,64,64]{3,1,2,0:T(8,128)S(1)} fusion(f32[16,64,64,8]{2,3,1,0:T(8,128)} %fusion.9, f32[16,8,64,64]{3,2,1,0:T(8,128)} %reshape.351, bf16[16,64,64,256]{3,2,1,0:T(8,128)(2,1)} %param.30, f32[16,8,64,256]{3,2,1,0:T(8,128)} %copy-done, f32[64]{0:T(128)S(1)} %copy-done.15, f32[16,8,64]{1,2,0:T(8,128)S(1)} %copy.55), kind=kOutput, calls=%fused_computation.39 | convolution fusion | flops 807403520 | bytes 48267520 | tf_op jit(solution)/shard_map/rhpn,rthn->rthp/dot_general | solution.py:83
  265.8 2.7 copy.58
  268.5 3.6 reshape.354
  272.1 1.9 fusion.76
  274.0 4.6 mul.235
  278.7 3.3 reduce_sum.63
  282.0 2.6 mul.236
  284.6 4.8 mul.237
  289.4 26.8 %fusion.38 = f32[128,8192]{1,0:T(8,128)} fusion(bf16[4096,8192]{1,0:T(8,128)(2,1)} %param.41, f32[16,8,4096]{2,1,0:T(8,128)} %mul.237, f32[4096]{0:T(1024)S(1)} %copy-done.9, f32[16,8,4096]{2,1,0:T(8,128)S(1)} %reshape.354, bf16[16,8,4096]{2,1,0:T(8,128)(2,1)S(1)} %copy-done.2), kind=kOutput, calls=%fused_computation.86 | convolution fusion | flops 8594653184 | bytes 76562432 | tf_op jit(solution)/shard_map/dot_general | solution.py:108
  320.3 2.9 collective-permute-start.4
  326.9 4.9 all-reduce.3
  331.8 2.0 convolution_convert_fusion
  337.9 10.8 %gather_fusion.12 = bf16[8,64,64,128]{3,2,1,0:T(8,128)(2,1)} fusion(bf16[16,64,64,128]{3,2,1,0:T(8,128)(2,1)} %get-tuple-element.114, s32[1024]{0:T(1024)S(1)} %pad_clamp_fusion.5), kind=kCustom, calls=%fused_computation.12 | custom fusion | bytes 16777248 | tf_op jit(solution)/shard_map/jit(_take)/gather | solution.py:179
  348.6 10.4 %gather_fusion.13 = bf16[8,64,64,128]{3,2,1,0:T(8,128)(2,1)} fusion(bf16[16,64,64,128]{3,2,1,0:T(8,128)(2,1)} %get-tuple-element.115, s32[1024]{0:T(1024)S(1)} %pad_clamp_fusion.5), kind=kCustom, calls=%fused_computation.13 | custom fusion | bytes 16777248 | tf_op jit(solution)/shard_map/jit(_take)/gather | solution.py:179
  360.4 1.5 collective-permute-start.7
  361.9 79.8 %collective-permute-done.4 = bf16[8,3,4096]{2,1,0:T(4,128)(2,1)} collective-permute-done((bf16[8,3,4096]{2,1,0:T(4,128)(2,1)S(1)}, bf16[8,3,4096]{2,1,0:T(4,128)(2,1)}, u32[]{:S(2)}, u32[]{:S(2)}) %collective-permute-start.4) | collective-permute-done | bytes 196640 | tf_op jit(solution)/shard_map/ppermute | solution.py:163
  441.7 4.0 collective-permute-done.5
  445.7 1.9 pad_maximum_fusion.8
  449.6 3.3 collective-permute-done.7
  452.8 4.0 collective-permute-done.8
  456.8 1.7 pad_maximum_fusion.9
  460.6 2.1 convert_bitcast_fusion
  462.6 11.8 %constant_dynamic-slice_fusion.6 = (bf16[3,64,64,256]{3,2,1,0:T(8,128)(2,1)}, bf16[3,64,64,256]{3,2,1,0:T(8,128)(2,1)}) fusion(bf16[12,64,64,256]{3,2,1,0:T(8,128)(2,1)} %all-to-all-done, s32[]{:T(128)S(6)} %select_n.116, s32[]{:T(128)S(6)} %select_n.118), kind=kLoop, calls=%fused_computation.142 | loop fusion | bytes 25165832 | tf_op jit(solution)/shard_map/dynamic_slice | solution.py:190
  474.5 9.4 %concatenate.33 = bf16[8,64,64,256]{3,2,1,0:T(8,128)(2,1)} pad(bf16[3,64,64,256]{3,2,1,0:T(8,128)(2,1)} %get-tuple-element.116, bf16[]{:T(256)} %constant.119.clone.1), padding=0_5x0_0x0_0x0_0 | pad | bytes 23068674 | tf_op jit(solution)/shard_map/concatenate | solution.py:193
  484.3 6.0 concatenate.35
  490.2 267.7 %while.21 = (s32[]{:T(128)}, bf16[8,64,64,256]{3,2,1,0:T(8,128)(2,1)}, s32[]{:T(128)}, s32[8]{0:T(128)S(1)}, bf16[16,64,64,256]{3,2,1,0:T(8,128)(2,1)}, /*index=5*/s32[]{:T(128)}, s32[]{:T(128)}, s32[]{:T(128)}, s32[]{:T(128)}) while((s32[]{:T(128)}, bf16[8,64,64,256]{3,2,1,0:T(8,128)(2,1)}, s32[]{:T(128)}, s32[8]{0:T(128)S(1)}, ...), condition=%wide.region_9.11_spmd, body=%wide.region_8.10_spmd.sunk | while | flops 8 | bytes 16777436 | solution.py:204
  492.5 3.2 constant_dynamic-slice_fusion.10
  496.1 48.0 %collective-permute-done = bf16[1,64,64,256]{3,2,1,0:T(8,128)(2,1)S(1)} collective-permute-done((bf16[1,64,64,256]{3,2,1,0:T(8,128)(2,1)}, bf16[1,64,64,256]{3,2,1,0:T(8,128)(2,1)S(1)}, u32[]{:S(2)}, u32[]{:S(2)}) %collective-permute-start) | collective-permute-done | bytes 2097184 | tf_op jit(solution)/shard_map/while/body/ppermute | solution.py:201
  544.1 1.5 constant_dynamic-update-slice_fusion.4
  547.8 3.2 constant_dynamic-slice_fusion.10
  551.3 47.3 %collective-permute-done = bf16[1,64,64,256]{3,2,1,0:T(8,128)(2,1)S(1)} collective-permute-done((bf16[1,64,64,256]{3,2,1,0:T(8,128)(2,1)}, bf16[1,64,64,256]{3,2,1,0:T(8,128)(2,1)S(1)}, u32[]{:S(2)}, u32[]{:S(2)}) %collective-permute-start) | collective-permute-done | bytes 2097184 | tf_op jit(solution)/shard_map/while/body/ppermute | solution.py:201
  598.6 1.5 constant_dynamic-update-slice_fusion.4
  602.3 3.2 constant_dynamic-slice_fusion.10
  605.8 46.4 %collective-permute-done = bf16[1,64,64,256]{3,2,1,0:T(8,128)(2,1)S(1)} collective-permute-done((bf16[1,64,64,256]{3,2,1,0:T(8,128)(2,1)}, bf16[1,64,64,256]{3,2,1,0:T(8,128)(2,1)S(1)}, u32[]{:S(2)}, u32[]{:S(2)}) %collective-permute-start) | collective-permute-done | bytes 2097184 | tf_op jit(solution)/shard_map/while/body/ppermute | solution.py:201
  652.2 1.5 constant_dynamic-update-slice_fusion.4
  655.9 3.2 constant_dynamic-slice_fusion.10
  659.3 45.5 %collective-permute-done = bf16[1,64,64,256]{3,2,1,0:T(8,128)(2,1)S(1)} collective-permute-done((bf16[1,64,64,256]{3,2,1,0:T(8,128)(2,1)}, bf16[1,64,64,256]{3,2,1,0:T(8,128)(2,1)S(1)}, u32[]{:S(2)}, u32[]{:S(2)}) %collective-permute-start) | collective-permute-done | bytes 2097184 | tf_op jit(solution)/shard_map/while/body/ppermute | solution.py:201
  704.8 1.5 constant_dynamic-update-slice_fusion.4
  708.6 3.2 constant_dynamic-slice_fusion.10
  712.0 44.5 %collective-permute-done = bf16[1,64,64,256]{3,2,1,0:T(8,128)(2,1)S(1)} collective-permute-done((bf16[1,64,64,256]{3,2,1,0:T(8,128)(2,1)}, bf16[1,64,64,256]{3,2,1,0:T(8,128)(2,1)S(1)}, u32[]{:S(2)}, u32[]{:S(2)}) %collective-permute-start) | collective-permute-done | bytes 2097184 | tf_op jit(solution)/shard_map/while/body/ppermute | solution.py:201
  756.5 1.4 constant_dynamic-update-slice_fusion.4
  758.0 44.4 %pad_maximum_fusion = bf16[32,64,64,256]{3,2,1,0:T(8,128)(2,1)} fusion(bf16[8,64,64,256]{3,2,1,0:T(8,128)(2,1)} %get-tuple-element.62, bf16[8,64,64,256]{3,2,1,0:T(8,128)(2,1)} %get-tuple-element.61, bf16[8,64,64,256]{3,2,1,0:T(8,128)(2,1)} %collective-permute-done.2, bf16[8,64,64,128]{3,2,1,0:T(8,128)(2,1)} %gather_fusion.13, ...), kind=kLoop, calls=%fused_computation.24 | loop fusion | flops 335544320 | bytes 134217728 | tf_op jit(solution)/shard_map/concatenate | solution.py:206
  802.3 43.4 %fusion.77 = (bf16[32,64,64,128]{3,2,1,0:T(8,128)(2,1)}, bf16[32,64,64,128]{3,2,1,0:T(8,128)(2,1)}) fusion(bf16[32,64,64,256]{3,2,1,0:T(8,128)(2,1)} %pad_maximum_fusion), kind=kLoop, calls=%fused_computation.176 | loop fusion | bytes 134217728 | tf_op jit(solution)/shard_map/jit(_take)/gather | solution.py:205
  845.8 11.8 %gather_fusion.18 = bf16[16,64,64,128]{3,2,1,0:T(8,128)(2,1)} fusion(bf16[32,64,64,128]{3,2,1,0:T(8,128)(2,1)} %get-tuple-element.112, s32[1024]{0:T(1024)S(1)} %pad_clamp_fusion.2), kind=kCustom, calls=%fused_computation.18 | custom fusion | bytes 33554496 | tf_op jit(solution)/shard_map/jit(_take)/gather | solution.py:205
  857.6 11.8 %gather_fusion.19 = bf16[16,64,64,128]{3,2,1,0:T(8,128)(2,1)} fusion(bf16[32,64,64,128]{3,2,1,0:T(8,128)(2,1)} %get-tuple-element.113, s32[1024]{0:T(1024)S(1)} %pad_clamp_fusion.2), kind=kCustom, calls=%fused_computation.19 | custom fusion | bytes 33554496 | tf_op jit(solution)/shard_map/jit(_take)/gather | solution.py:205
  869.4 22.9 %pad_maximum_fusion.1 = bf16[16,64,64,256]{3,2,1,0:T(8,128)(2,1)} fusion(bf16[16,64,64,128]{3,2,1,0:T(8,128)(2,1)} %gather_fusion.19, bf16[16,64,64,128]{3,2,1,0:T(8,128)(2,1)} %gather_fusion.18), kind=kLoop, calls=%fused_computation.26 | loop fusion | flops 67108864 | bytes 67108864 | tf_op jit(solution)/shard_map
  (122 shorter events, 35.0 us)
Async XLA Ops:
  10.0 1.5 copy-start.13
  11.5 2.6 copy-start.18
  12.8 8.3 copy-start.10
  17.4 6.2 copy-start.5
  19.0 2.1 copy-start.3
  22.4 1.5 copy-start.7
  22.4 2.1 copy-start.11
  153.4 309.3 %all-to-all-start = ((bf16[12,64,64,256]{3,2,1,0:T(8,128)(2,1)}), bf16[12,64,64,256]{3,2,1,0:T(8,128)(2,1)}, u32[]{:S(2)}, u32[]{:S(2)}) async-start(bf16[12,64,64,256]{3,2,1,0:T(8,128)(2,1)} %pad_maximum_fusion.2), calls=%async_computation.1 | async-start | bytes 50331648 | tf_op jit(solution)/shard_map/all_to_all | solution.py:181
  161.8 298.8 %reduce-scatter.2.cloned.1.call-start = ((), (), s32[]{:S(2)}) async-start(), calls=%async_computation.2 | async-start | bytes 5242880 | tf_op jit(solution)/shard_map/reduce_scatter | solution.py:114
  205.5 284.8 %collective-permute-start.2 = (bf16[8,64,64,256]{3,2,1,0:T(8,128)(2,1)}, bf16[8,64,64,256]{3,2,1,0:T(8,128)(2,1)}, u32[]{:S(2)}, u32[]{:S(2)}) collective-permute-start(bf16[8,64,64,256]{3,2,1,0:T(8,128)(2,1)} %pad_maximum_fusion.3), channel_id=1, source_target_pairs={{0,1},{1,0},{2,3},{3,2},{4,5},{5,4},{6,7},{7,6},{8,9},{9,8},{10,11... | collective-permute-start | bytes 50331656 | tf_op jit(solution)/shard_map/ppermute | solution.py:188
  209.9 21.8 %copy-start = (f32[16,8,64,256]{3,2,1,0:T(8,128)}, f32[16,8,64,256]{3,2,1,0:T(8,128)S(1)}, u32[]{:S(2)}) copy-start(f32[16,8,64,256]{3,2,1,0:T(8,128)S(1)} %convolution_bitcast_fusion.1) | copy-start | bytes 25165828
  231.7 10.5 %copy-start.15 = (f32[64]{0:T(128)S(1)}, f32[64]{0:T(128)}, u32[]{:S(2)}) copy-start(f32[64]{0:T(128)} %param.39) | copy-start | bytes 772
  268.5 3.6 copy-start.2
  284.6 4.8 copy-start.9
  316.2 0.7 copy-start.12
  316.2 1.1 copy-start.6
  316.2 1.4 copy-start.8
  316.2 7.0 copy-start.16
  316.3 7.0 copy-start.14
  316.3 15.5 %copy-start.4 = (bf16[16,3,4096]{2,1,0:T(4,128)(2,1)S(1)}, bf16[16,3,4096]{2,1,0:T(4,128)(2,1)}, u32[]{:S(2)}) copy-start(bf16[16,3,4096]{2,1,0:T(4,128)(2,1)} %copy-done.3) | copy-start | bytes 1179652
  318.4 17.7 %copy-start.17 = (s32[64]{0:T(128)S(1)}, s32[64]{0:T(128)}, u32[]{:S(2)}) copy-start(s32[64]{0:T(128)} %get-tuple-element.88) | copy-start | bytes 772
  318.5 17.7 %copy-start.19 = (s32[64]{0:T(128)S(1)}, s32[64]{0:T(128)}, u32[]{:S(2)}) copy-start(s32[64]{0:T(128)} %copy-done.18) | copy-start | bytes 772
  319.2 41.2 %collective-permute-start.3 = (bf16[8,3,4096]{2,1,0:T(4,128)(2,1)S(1)}, bf16[8,3,4096]{2,1,0:T(4,128)(2,1)}, u32[]{:S(2)}, u32[]{:S(2)}) collective-permute-start(bf16[8,3,4096]{2,1,0:T(4,128)(2,1)S(1)} %gather_fusion.3), channel_id=1, source_target_pairs={{0,1},{1,0},{2,3},{3,2},{4,5},{5,4},{6,7},{7,6},{8,9},{9,8},{10,11... | collective-permute-start | bytes 589832 | tf_op jit(solution)/shard_map/ppermute | solution.py:163
  320.3 121.4 %collective-permute-start.4 = (bf16[8,3,4096]{2,1,0:T(4,128)(2,1)S(1)}, bf16[8,3,4096]{2,1,0:T(4,128)(2,1)}, u32[]{:S(2)}, u32[]{:S(2)}) collective-permute-start(bf16[8,3,4096]{2,1,0:T(4,128)(2,1)S(1)} %gather_fusion.4), channel_id=1, source_target_pairs={{0,2},{1,3},{2,0},{3,1},{4,6},{5,7},{6,4},{7,5},{8,10},{9,11},{10,... | collective-permute-start | bytes 589832 | tf_op jit(solution)/shard_map/ppermute | solution.py:163
  326.8 118.9 %collective-permute-start.5 = (bf16[8,3,4096]{2,1,0:T(4,128)(2,1)S(1)}, bf16[8,3,4096]{2,1,0:T(4,128)(2,1)}, u32[]{:S(2)}, u32[]{:S(2)}) collective-permute-start(bf16[8,3,4096]{2,1,0:T(4,128)(2,1)S(1)} %gather_fusion.5), channel_id=1, source_target_pairs={{0,3},{1,2},{2,1},{3,0},{4,7},{5,6},{6,5},{7,4},{8,11},{9,10},{10,... | collective-permute-start | bytes 589832 | tf_op jit(solution)/shard_map/ppermute | solution.py:163
  360.3 89.2 %collective-permute-start.6 = (bf16[8,3,4096]{2,1,0:T(4,128)(2,1)S(1)}, bf16[8,3,4096]{2,1,0:T(4,128)(2,1)}, u32[]{:S(2)}, u32[]{:S(2)}) collective-permute-start(bf16[8,3,4096]{2,1,0:T(4,128)(2,1)S(1)} %gather_fusion.8), channel_id=1, source_target_pairs={{0,1},{1,0},{2,3},{3,2},{4,5},{5,4},{6,7},{7,6},{8,9},{9,8},{10,11... | collective-permute-start | bytes 589832 | tf_op jit(solution)/shard_map/ppermute | solution.py:163
  360.4 92.4 %collective-permute-start.7 = (bf16[8,3,4096]{2,1,0:T(4,128)(2,1)S(1)}, bf16[8,3,4096]{2,1,0:T(4,128)(2,1)S(1)}, u32[]{:S(2)}, u32[]{:S(2)}) collective-permute-start(bf16[8,3,4096]{2,1,0:T(4,128)(2,1)S(1)} %gather_fusion.9), channel_id=1, source_target_pairs={{0,2},{1,3},{2,0},{3,1},{4,6},{5,7},{6,4},{7,5},{8,10},{9,11},{10,... | collective-permute-start | bytes 589832 | tf_op jit(solution)/shard_map/ppermute | solution.py:163
  441.7 15.1 %collective-permute-start.8 = (bf16[8,3,4096]{2,1,0:T(4,128)(2,1)S(1)}, bf16[8,3,4096]{2,1,0:T(4,128)(2,1)S(1)}, u32[]{:S(2)}, u32[]{:S(2)}) collective-permute-start(bf16[8,3,4096]{2,1,0:T(4,128)(2,1)S(1)} %gather_fusion.10), channel_id=1, source_target_pairs={{0,3},{1,2},{2,1},{3,0},{4,7},{5,6},{6,5},{7,4},{8,11},{9,10},{10,... | collective-permute-start | bytes 589832 | tf_op jit(solution)/shard_map/ppermute | solution.py:163
  474.5 9.8 %copy-start.1 = (bf16[3,64,64,256]{3,2,1,0:T(8,128)(2,1)S(1)}, bf16[3,64,64,256]{3,2,1,0:T(8,128)(2,1)}, u32[]{:S(2)}) copy-start(bf16[3,64,64,256]{3,2,1,0:T(8,128)(2,1)} %get-tuple-element.117) | copy-start | bytes 18874372
  495.7 48.4 %collective-permute-start = (bf16[1,64,64,256]{3,2,1,0:T(8,128)(2,1)}, bf16[1,64,64,256]{3,2,1,0:T(8,128)(2,1)S(1)}, u32[]{:S(2)}, u32[]{:S(2)}) collective-permute-start(bf16[1,64,64,256]{3,2,1,0:T(8,128)(2,1)} %constant_dynamic-slice_fusion.10), channel_id=1, source_target_pairs={{0,2},{1,3},{2,0},{3,1},{4,6},{5,7},{6,4},{7,5},{8,10},{9,11},{10,... | collective-permute-start | bytes 6291464 | tf_op jit(solution)/shard_map/while/body/ppermute | solution.py:201
  551.0 47.5 %collective-permute-start = (bf16[1,64,64,256]{3,2,1,0:T(8,128)(2,1)}, bf16[1,64,64,256]{3,2,1,0:T(8,128)(2,1)S(1)}, u32[]{:S(2)}, u32[]{:S(2)}) collective-permute-start(bf16[1,64,64,256]{3,2,1,0:T(8,128)(2,1)} %constant_dynamic-slice_fusion.10), channel_id=1, source_target_pairs={{0,2},{1,3},{2,0},{3,1},{4,6},{5,7},{6,4},{7,5},{8,10},{9,11},{10,... | collective-permute-start | bytes 6291464 | tf_op jit(solution)/shard_map/while/body/ppermute | solution.py:201
  605.5 46.7 %collective-permute-start = (bf16[1,64,64,256]{3,2,1,0:T(8,128)(2,1)}, bf16[1,64,64,256]{3,2,1,0:T(8,128)(2,1)S(1)}, u32[]{:S(2)}, u32[]{:S(2)}) collective-permute-start(bf16[1,64,64,256]{3,2,1,0:T(8,128)(2,1)} %constant_dynamic-slice_fusion.10), channel_id=1, source_target_pairs={{0,2},{1,3},{2,0},{3,1},{4,6},{5,7},{6,4},{7,5},{8,10},{9,11},{10,... | collective-permute-start | bytes 6291464 | tf_op jit(solution)/shard_map/while/body/ppermute | solution.py:201
  659.0 45.7 %collective-permute-start = (bf16[1,64,64,256]{3,2,1,0:T(8,128)(2,1)}, bf16[1,64,64,256]{3,2,1,0:T(8,128)(2,1)S(1)}, u32[]{:S(2)}, u32[]{:S(2)}) collective-permute-start(bf16[1,64,64,256]{3,2,1,0:T(8,128)(2,1)} %constant_dynamic-slice_fusion.10), channel_id=1, source_target_pairs={{0,2},{1,3},{2,0},{3,1},{4,6},{5,7},{6,4},{7,5},{8,10},{9,11},{10,... | collective-permute-start | bytes 6291464 | tf_op jit(solution)/shard_map/while/body/ppermute | solution.py:201
  711.7 44.8 %collective-permute-start = (bf16[1,64,64,256]{3,2,1,0:T(8,128)(2,1)}, bf16[1,64,64,256]{3,2,1,0:T(8,128)(2,1)S(1)}, u32[]{:S(2)}, u32[]{:S(2)}) collective-permute-start(bf16[1,64,64,256]{3,2,1,0:T(8,128)(2,1)} %constant_dynamic-slice_fusion.10), channel_id=1, source_target_pairs={{0,2},{1,3},{2,0},{3,1},{4,6},{5,7},{6,4},{7,5},{8,10},{9,11},{10,... | collective-permute-start | bytes 6291464 | tf_op jit(solution)/shard_map/while/body/ppermute | solution.py:201
Sparse Core Ops, SparseCore 0:
  316.4 79.7 reduce-scatter.1

commit v6 on v5

--- a/solution.py
+++ b/solution.py
@@ -202,8 +202,19 @@
             return lax.dynamic_update_index_in_dim(held, got, slot, 0)
 
         state_pieces.append(lax.fori_loop(first_slots, needed, one_slot, buffer))
-    new_ssm_state = jnp.take(
-        jnp.concatenate(state_pieces, axis=0), gather_index, axis=0, mode="clip"
+    piece_of = jnp.clip(arriving_source ^ req_index, 0, owners - 1)
+    slot_of = jnp.clip(arriving_rank, 0, cap - 1)
+
+    def place(row, held):
+        slot = slot_of[row]
+        chosen = lax.dynamic_index_in_dim(state_pieces[0], slot, 0, keepdims=True)
+        for which in range(1, len(state_pieces)):
+            candidate = lax.dynamic_index_in_dim(state_pieces[which], slot, 0, keepdims=True)
+            chosen = jnp.where(piece_of[row] == which, candidate, chosen)
+        return lax.dynamic_update_index_in_dim(held, chosen, row, 0)
+
+    new_ssm_state = lax.fori_loop(
+        0, local_requests, place, jnp.zeros_like(retained)
     )
     new_conv_x_state = hand_over(kept_x)
     new_conv_bc_state = hand_over(kept_bc)

time: 911 us -> 977 us (1.072)
  loops' own time: 8.55 us -> 75.5 us
  other arithmetic: 139 us -> 194 us
  local copies, waits for them, and re-layouts: 253 us -> 208 us
  waiting for transfers between devices: 323 us -> 309 us
    dynamic_update_slice x0 -> x16, other arithmetic: none -> 107 us  [place(): return lax.dynamic_update_index_in_dim(held, chosen, row, 0)]
    gather x3 -> x0, local copies, waits for them, and re-layouts: 67 us -> none  [on_device(): jnp.take(jnp.concatenate(state_pieces, axis=0), gather_index, axis=0, mod...]
    another operation x0 -> x1, loops' own time: none -> 65.3 us  [on_device(): lax.fori_loop(0, local_requests, place, jnp.zeros_like(retained))]
    concatenate x1 -> x0, other arithmetic: 44.4 us -> none  [on_device(): jnp.concatenate(state_pieces, axis=0)]
    gather x2 -> x3, local copies, waits for them, and re-layouts: 23.4 us -> 48.4 us  [on_device(): jnp.take(retained, first_index, axis=0, mode='clip')]
    gather x3 -> x2, local copies, waits for them, and re-layouts: 46.2 us -> 21.9 us  [on_device(): state_pieces = [jnp.take(retained, own_index, axis=0, mode='clip')]]
    another operation x1 -> x0, other arithmetic: 22.9 us -> none
    dynamic_slice x0 -> x32, local copies, waits for them, and re-layouts: none -> 20.8 us  [the longest x16 10.5 us: place(): chosen = jnp.where(piece_of[row] == which, candidate, chosen)]
where the time goes in v6:
time: 977 us; the launch traced here: 966 us
  waiting for transfers between devices  309 us (32%)
  local copies, waits for them, and re-layouts  208 us (21%)
  other arithmetic  194 us (20%)
  matrix products  139 us (14%)
  loops' own time  75.5 us (8%)
  starting transfers between devices  20.1 us (2%)
  between operations  16.1 us (2%)
    ppermute x5, waiting for transfers between devices, one_slot(): got = lax.ppermute(row, 'req', pairs)  232 us
    dynamic_update_slice x16, other arithmetic, place(): return lax.dynamic_update_index_in_dim(held, chosen, row, 0)  107 us
    ppermute x6, waiting for transfers between devices, send_pieces(): pieces.append(lax.ppermute(outgoing, 'req', pairs))  76.8 us
    another operation x1, loops' own time, on_device(): lax.fori_loop(0, local_requests, place, jnp.zeros_like(retained))  65.3 us
    unnamed x3, other arithmetic  58.1 us
    gather x3, local copies, waits for them, and re-layouts, on_device(): jnp.take(retained, first_index, axis=0, mode='clip')  48.4 us
    dot_general x1, matrix products, on_device(): jnp.einsum('rshp,rshn->rhpn', weighted_x, b_heads, precision=highest)  44.8 us
    dot_general x1, matrix products, on_device(): jnp.dot(normed.reshape(local_requests * L, local_heads * P_SIZE), out_wei...  26.8 us
  transfers between devices with their start and end apart: 14, of which 9 were waited for; matrix products, arithmetic and copies ran while one was open for 25% of the time, Pallas kernels for 0%

profile of v6, /device:TPU:0, one launch (start us, length us, event | category | flops | bytes accessed | tf_op | source)
XLA Modules:
  0.0 966.3 jit_solution(17803541348975412937)
XLA Ops:
  14.7 2.1 fusion.36
  18.2 3.0 reshape.357
  31.4 2.6 broadcast_multiply_fusion
  34.0 5.6 convolution_bitcast_fusion
  39.7 44.8 %add_convert_fusion = bf16[16,64,64,256]{3,2,1,0:T(8,128)(2,1)} fusion(bf16[16,64,64,256]{3,2,1,0:T(8,128)(2,1)} %param.32, f32[16,64]{1,0:T(8,128)S(1)} %exp.40, f32[16,8,64,256]{3,2,1,0:T(8,128)} %convolution_bitcast_fusion, f32[16,8,64,64]{3,2,1,0:T(8,128)} %broadcast_multiply_fusion), kind=kOutput, calls=%fused_computation.23 | convolution fusion | flops 872415232 | bytes 77598720 | tf_op jit(solution)/shard_map/rshp,rshn->rhpn/dot_general | solution.py:95
  84.5 25.0 %fusion.77 = (bf16[16,64,64,128]{3,2,1,0:T(8,128)(2,1)}, bf16[16,64,64,128]{3,2,1,0:T(8,128)(2,1)}) fusion(bf16[16,64,64,256]{3,2,1,0:T(8,128)(2,1)} %add_convert_fusion), kind=kLoop, calls=%fused_computation.176 | loop fusion | bytes 67108864 | tf_op jit(solution)/shard_map/jit(_take)/gather | solution.py:182
  109.5 11.7 %gather_fusion.12 = bf16[12,64,64,128]{3,2,1,0:T(8,128)(2,1)} fusion(bf16[16,64,64,128]{3,2,1,0:T(8,128)(2,1)} %get-tuple-element.268, s32[1024]{0:T(1024)S(1)} %pad_clamp_fusion.5), kind=kCustom, calls=%fused_computation.12 | custom fusion | bytes 25165872 | tf_op jit(solution)/shard_map/jit(_take)/gather | solution.py:182
  121.2 11.7 %gather_fusion.13 = bf16[12,64,64,128]{3,2,1,0:T(8,128)(2,1)} fusion(bf16[16,64,64,128]{3,2,1,0:T(8,128)(2,1)} %get-tuple-element.269, s32[1024]{0:T(1024)S(1)} %pad_clamp_fusion.5), kind=kCustom, calls=%fused_computation.13 | custom fusion | bytes 25165872 | tf_op jit(solution)/shard_map/jit(_take)/gather | solution.py:182
  132.9 21.2 %pad_maximum_fusion = bf16[12,64,64,256]{3,2,1,0:T(8,128)(2,1)} fusion(bf16[12,64,64,128]{3,2,1,0:T(8,128)(2,1)} %gather_fusion.13, bf16[12,64,64,128]{3,2,1,0:T(8,128)(2,1)} %gather_fusion.12), kind=kLoop, calls=%fused_computation.24 | loop fusion | flops 50331648 | bytes 50331648
  154.1 8.4 all-to-all-start
  162.6 10.4 %gather_fusion.14 = bf16[8,64,64,128]{3,2,1,0:T(8,128)(2,1)} fusion(bf16[16,64,64,128]{3,2,1,0:T(8,128)(2,1)} %get-tuple-element.268, s32[1024]{0:T(1024)S(1)} %pad_clamp_fusion.4), kind=kCustom, calls=%fused_computation.14 | custom fusion | bytes 16777248 | tf_op jit(solution)/shard_map/jit(_take)/gather | solution.py:187
  173.0 10.3 %gather_fusion.15 = bf16[8,64,64,128]{3,2,1,0:T(8,128)(2,1)} fusion(bf16[16,64,64,128]{3,2,1,0:T(8,128)(2,1)} %get-tuple-element.269, s32[1024]{0:T(1024)S(1)} %pad_clamp_fusion.4), kind=kCustom, calls=%fused_computation.15 | custom fusion | bytes 16777248 | tf_op jit(solution)/shard_map/jit(_take)/gather | solution.py:187
  183.3 22.7 %pad_maximum_fusion.1 = bf16[8,64,64,256]{3,2,1,0:T(8,128)(2,1)} fusion(bf16[8,64,64,128]{3,2,1,0:T(8,128)(2,1)} %gather_fusion.15, bf16[8,64,64,128]{3,2,1,0:T(8,128)(2,1)} %gather_fusion.14), kind=kLoop, calls=%fused_computation.25 | loop fusion | flops 33554432 | bytes 33554432
  207.2 3.6 convolution_bitcast_fusion.1
  210.8 21.8 %fusion.1 = f32[16,64,8,8]{3,2,1,0:T(8,128)} fusion(f32[16,8,64,256]{3,2,1,0:T(8,128)} %convolution_bitcast_fusion, f32[16,8,64,256]{3,2,1,0:T(8,128)S(1)} %convolution_bitcast_fusion.1), kind=kOutput, calls=%fused_computation.28 | convolution fusion | flops 100663296 | bytes 17039360 | tf_op jit(solution)/shard_map/rthn,rshn->rhts/dot_general | solution.py:80
  232.6 10.3 %fusion.9 = f32[16,64,64,8]{2,3,1,0:T(8,128)} fusion(f32[16,64,8,8]{3,2,1,0:T(8,128)} %fusion.1, f32[16,8,64,64]{3,2,1,0:T(8,128)} %reshape.357, f32[16,64,8]{2,1,0:T(8,128)S(1)} %copy.53, f32[16,64,8]{2,1,0:T(8,128)S(1)} %copy.51, pred[8,8]{1,0:T(8,128)(4,1)S(1)} %iota_compare_fusion.8), kind=kOutput, calls=%fused_computation.39 | convolution fusion | flops 25427968 | bytes 4522048 | tf_op jit(solution)/shard_map/rhts,rshp->rthp/dot_general | solution.py:82
  243.2 23.6 %fusion.7 = f32[16,8,64,64]{3,1,2,0:T(8,128)S(1)} fusion(f32[16,64,64,8]{2,3,1,0:T(8,128)} %fusion.9, f32[16,8,64,64]{3,2,1,0:T(8,128)} %reshape.357, bf16[16,64,64,256]{3,2,1,0:T(8,128)(2,1)} %param.32, f32[16,8,64,256]{3,2,1,0:T(8,128)} %copy-done, f32[64]{0:T(128)S(1)} %copy-done.19, f32[16,8,64]{1,2,0:T(8,128)S(1)} %copy.55), kind=kOutput, calls=%fused_computation.37 | convolution fusion | flops 807403520 | bytes 48267520 | tf_op jit(solution)/shard_map/rhpn,rthn->rthp/dot_general | solution.py:83
  266.8 2.7 copy.58
  269.5 3.6 reshape.360
  275.0 4.6 mul.235
  279.6 3.3 reduce_sum.63
  283.0 2.6 mul.236
  285.6 4.8 mul.237
  290.4 26.8 %fusion.38 = f32[128,8192]{1,0:T(8,128)} fusion(bf16[4096,8192]{1,0:T(8,128)(2,1)} %param.43, f32[16,8,4096]{2,1,0:T(8,128)} %mul.237, f32[4096]{0:T(1024)S(1)} %copy-done.13, f32[16,8,4096]{2,1,0:T(8,128)S(1)} %reshape.360, bf16[16,8,4096]{2,1,0:T(8,128)(2,1)S(1)} %copy-done.3), kind=kOutput, calls=%fused_computation.84 | convolution fusion | flops 8594653184 | bytes 76562432 | tf_op jit(solution)/shard_map/dot_general | solution.py:108
  321.0 2.9 collective-permute-start.4
  324.8 11.2 %gather_fusion.16 = bf16[8,64,64,128]{3,2,1,0:T(8,128)(2,1)} fusion(bf16[16,64,64,128]{3,2,1,0:T(8,128)(2,1)} %get-tuple-element.268, s32[1024]{0:T(1024)S(1)} %pad_clamp_fusion.3), kind=kCustom, calls=%fused_computation.16 | custom fusion | bytes 16777248 | tf_op jit(solution)/shard_map/jit(_take)/gather | solution.py:179
  336.1 10.7 %gather_fusion.17 = bf16[8,64,64,128]{3,2,1,0:T(8,128)(2,1)} fusion(bf16[16,64,64,128]{3,2,1,0:T(8,128)(2,1)} %get-tuple-element.269, s32[1024]{0:T(1024)S(1)} %pad_clamp_fusion.3), kind=kCustom, calls=%fused_computation.17 | custom fusion | bytes 16777248 | tf_op jit(solution)/shard_map/jit(_take)/gather | solution.py:179
  350.4 14.2 %pad_maximum_fusion.2 = bf16[8,64,64,256]{3,2,1,0:T(8,128)(2,1)} fusion(bf16[8,64,64,128]{3,2,1,0:T(8,128)(2,1)} %gather_fusion.17, bf16[8,64,64,128]{3,2,1,0:T(8,128)(2,1)} %gather_fusion.16), kind=kLoop, calls=%fused_computation.26 | loop fusion | flops 33554432 | bytes 33554432
  364.7 5.2 all-reduce.3
  376.8 65.7 %collective-permute-done.4 = bf16[8,3,4096]{2,1,0:T(4,128)(2,1)} collective-permute-done((bf16[8,3,4096]{2,1,0:T(4,128)(2,1)S(1)}, bf16[8,3,4096]{2,1,0:T(4,128)(2,1)}, u32[]{:S(2)}, u32[]{:S(2)}) %collective-permute-start.4) | collective-permute-done | bytes 196640 | tf_op jit(solution)/shard_map/ppermute | solution.py:163
  442.4 3.9 collective-permute-done.5
  450.3 3.3 collective-permute-done.7
  453.6 3.9 collective-permute-done.8
  463.3 11.8 %constant_dynamic-slice_fusion.5 = (bf16[3,64,64,256]{3,2,1,0:T(8,128)(2,1)}, bf16[3,64,64,256]{3,2,1,0:T(8,128)(2,1)}) fusion(bf16[12,64,64,256]{3,2,1,0:T(8,128)(2,1)} %all-to-all-done, s32[]{:T(128)S(6)} %select_n.185, s32[]{:T(128)S(6)} %select_n.183), kind=kLoop, calls=%fused_computation.139 | loop fusion | bytes 25165832 | tf_op jit(solution)/shard_map/dynamic_slice | solution.py:190
  475.2 9.4 concatenate.32
  485.0 6.0 concatenate.30
  491.0 274.6 %while.34 = (s32[]{:T(128)}, bf16[8,64,64,256]{3,2,1,0:T(8,128)(2,1)}, s32[]{:T(128)}, s32[8]{0:T(128)S(1)}, bf16[16,64,64,256]{3,2,1,0:T(8,128)(2,1)}, /*index=5*/s32[]{:T(128)}, s32[]{:T(128)}, s32[]{:T(128)}, s32[]{:T(128)}) while((s32[]{:T(128)}, bf16[8,64,64,256]{3,2,1,0:T(8,128)(2,1)}, s32[]{:T(128)}, s32[8]{0:T(128)S(1)}, ...), condition=%wide.region_16.18_spmd, body=%wide.region_15.17_spmd.sunk | while | flops 8 | bytes 16777436 | solution.py:204
  493.7 3.2 constant_dynamic-slice_fusion.10
  497.0 47.2 %collective-permute-done = bf16[1,64,64,256]{3,2,1,0:T(8,128)(2,1)S(1)} collective-permute-done((bf16[1,64,64,256]{3,2,1,0:T(8,128)(2,1)}, bf16[1,64,64,256]{3,2,1,0:T(8,128)(2,1)S(1)}, u32[]{:S(2)}, u32[]{:S(2)}) %collective-permute-start) | collective-permute-done | bytes 2097184 | tf_op jit(solution)/shard_map/while/body/ppermute | solution.py:201
  548.3 3.2 constant_dynamic-slice_fusion.10
  552.5 46.4 %collective-permute-done = bf16[1,64,64,256]{3,2,1,0:T(8,128)(2,1)S(1)} collective-permute-done((bf16[1,64,64,256]{3,2,1,0:T(8,128)(2,1)}, bf16[1,64,64,256]{3,2,1,0:T(8,128)(2,1)S(1)}, u32[]{:S(2)}, u32[]{:S(2)}) %collective-permute-start) | collective-permute-done | bytes 2097184 | tf_op jit(solution)/shard_map/while/body/ppermute | solution.py:201
  603.1 3.2 constant_dynamic-slice_fusion.10
  607.7 46.0 %collective-permute-done = bf16[1,64,64,256]{3,2,1,0:T(8,128)(2,1)S(1)} collective-permute-done((bf16[1,64,64,256]{3,2,1,0:T(8,128)(2,1)}, bf16[1,64,64,256]{3,2,1,0:T(8,128)(2,1)S(1)}, u32[]{:S(2)}, u32[]{:S(2)}) %collective-permute-start) | collective-permute-done | bytes 2097184 | tf_op jit(solution)/shard_map/while/body/ppermute | solution.py:201
  657.9 3.2 constant_dynamic-slice_fusion.10
  662.9 46.0 %collective-permute-done = bf16[1,64,64,256]{3,2,1,0:T(8,128)(2,1)S(1)} collective-permute-done((bf16[1,64,64,256]{3,2,1,0:T(8,128)(2,1)}, bf16[1,64,64,256]{3,2,1,0:T(8,128)(2,1)S(1)}, u32[]{:S(2)}, u32[]{:S(2)}) %collective-permute-start) | collective-permute-done | bytes 2097184 | tf_op jit(solution)/shard_map/while/body/ppermute | solution.py:201
  713.1 3.2 constant_dynamic-slice_fusion.10
  718.1 46.0 %collective-permute-done = bf16[1,64,64,256]{3,2,1,0:T(8,128)(2,1)S(1)} collective-permute-done((bf16[1,64,64,256]{3,2,1,0:T(8,128)(2,1)}, bf16[1,64,64,256]{3,2,1,0:T(8,128)(2,1)S(1)}, u32[]{:S(2)}, u32[]{:S(2)}) %collective-permute-start) | collective-permute-done | bytes 2097184 | tf_op jit(solution)/shard_map/while/body/ppermute | solution.py:201
  765.6 193.6 %while.36 = (s32[]{:T(128)}, bf16[16,64,64,256]{3,2,1,0:T(8,128)(2,1)}, s32[16]{0:T(128)S(1)}, s32[16]{0:T(128)S(1)}, bf16[8,64,64,256]{3,2,1,0:T(8,128)(2,1)}, ...) while((s32[]{:T(128)}, ...), condition=%wide.region_18.20_spmd, body=%wide.region_17.19_spmd.sunk | while | flops 3145736 | bytes 10488030 | solution.py:216
  771.0 6.7 select_dynamic-update-slice_fusion.2
  783.1 6.7 select_dynamic-update-slice_fusion.2
  795.2 6.7 select_dynamic-update-slice_fusion.2
  807.3 6.7 select_dynamic-update-slice_fusion.2
  819.4 6.7 select_dynamic-update-slice_fusion.2
  831.5 6.7 select_dynamic-update-slice_fusion.2
  843.6 6.7 select_dynamic-update-slice_fusion.2
  855.7 6.7 select_dynamic-update-slice_fusion.2
  867.8 6.7 select_dynamic-update-slice_fusion.2
  879.9 6.7 select_dynamic-update-slice_fusion.2
  892.0 6.7 select_dynamic-update-slice_fusion.2
  904.1 6.7 select_dynamic-update-slice_fusion.2
  916.2 6.7 select_dynamic-update-slice_fusion.2
  928.3 6.7 select_dynamic-update-slice_fusion.2
  940.4 6.7 select_dynamic-update-slice_fusion.2
  952.5 6.7 select_dynamic-update-slice_fusion.2
  (180 shorter events, 83.9 us)
Async XLA Ops:
  7.2 9.7 %copy-start.14 = (f32[4096]{0:T(1024)S(1)}, f32[4096]{0:T(1024)}, u32[]{:S(2)}) copy-start(f32[4096]{0:T(1024)} %param.36) | copy-start | bytes 49156
  9.7 7.1 copy-start.17
  11.2 1.0 copy-start.23
  14.7 2.1 copy-start.6
  18.2 3.7 copy-start.20
  18.2 8.1 copy-start.11
  18.2 8.5 copy-start.9
  21.2 6.3 copy-start.15
  26.7 0.8 copy-start.4
  28.8 2.6 copy-start.1
  31.4 2.6 copy-start.21
  154.1 309.3 %all-to-all-start = ((bf16[12,64,64,256]{3,2,1,0:T(8,128)(2,1)}), bf16[12,64,64,256]{3,2,1,0:T(8,128)(2,1)}, u32[]{:S(2)}, u32[]{:S(2)}) async-start(bf16[12,64,64,256]{3,2,1,0:T(8,128)(2,1)} %pad_maximum_fusion), calls=%async_computation.1 | async-start | bytes 50331648 | tf_op jit(solution)/shard_map/all_to_all | solution.py:181
  162.5 298.8 %reduce-scatter.2.cloned.1.call-start = ((), (), s32[]{:S(2)}) async-start(), calls=%async_computation.2 | async-start | bytes 5242880 | tf_op jit(solution)/shard_map/reduce_scatter | solution.py:114
  206.0 285.0 %collective-permute-start.2 = (bf16[8,64,64,256]{3,2,1,0:T(8,128)(2,1)}, bf16[8,64,64,256]{3,2,1,0:T(8,128)(2,1)}, u32[]{:S(2)}, u32[]{:S(2)}) collective-permute-start(bf16[8,64,64,256]{3,2,1,0:T(8,128)(2,1)} %pad_maximum_fusion.1), channel_id=1, source_target_pairs={{0,1},{1,0},{2,3},{3,2},{4,5},{5,4},{6,7},{7,6},{8,9},{9,8},{10,11... | collective-permute-start | bytes 50331656 | tf_op jit(solution)/shard_map/ppermute | solution.py:188
  210.8 21.8 %copy-start = (f32[16,8,64,256]{3,2,1,0:T(8,128)}, f32[16,8,64,256]{3,2,1,0:T(8,128)S(1)}, u32[]{:S(2)}) copy-start(f32[16,8,64,256]{3,2,1,0:T(8,128)S(1)} %convolution_bitcast_fusion.1) | copy-start | bytes 25165828
  232.6 10.3 %copy-start.12 = (f32[16,8,64]{2,1,0:T(8,128)S(1)}, f32[16,8,64]{2,1,0:T(8,128)}, u32[]{:S(2)}) copy-start(f32[16,8,64]{2,1,0:T(8,128)} %get-tuple-element.276) | copy-start | bytes 98308
  232.6 10.5 %copy-start.19 = (f32[64]{0:T(128)S(1)}, f32[64]{0:T(128)}, u32[]{:S(2)}) copy-start(f32[64]{0:T(128)} %param.41) | copy-start | bytes 772
  269.5 3.6 copy-start.3
  285.6 4.8 copy-start.13
  317.2 0.7 copy-start.16
  317.2 1.1 copy-start.7
  317.2 1.4 copy-start.8
  320.1 55.0 %collective-permute-start.3 = (bf16[8,3,4096]{2,1,0:T(4,128)(2,1)S(1)}, bf16[8,3,4096]{2,1,0:T(4,128)(2,1)}, u32[]{:S(2)}, u32[]{:S(2)}) collective-permute-start(bf16[8,3,4096]{2,1,0:T(4,128)(2,1)S(1)} %gather_fusion.3), channel_id=1, source_target_pairs={{0,1},{1,0},{2,3},{3,2},{4,5},{5,4},{6,7},{7,6},{8,9},{9,8},{10,11... | collective-permute-start | bytes 589832 | tf_op jit(solution)/shard_map/ppermute | solution.py:163
  321.0 121.4 %collective-permute-start.4 = (bf16[8,3,4096]{2,1,0:T(4,128)(2,1)S(1)}, bf16[8,3,4096]{2,1,0:T(4,128)(2,1)}, u32[]{:S(2)}, u32[]{:S(2)}) collective-permute-start(bf16[8,3,4096]{2,1,0:T(4,128)(2,1)S(1)} %gather_fusion.4), channel_id=1, source_target_pairs={{0,2},{1,3},{2,0},{3,1},{4,6},{5,7},{6,4},{7,5},{8,10},{9,11},{10,... | collective-permute-start | bytes 589832 | tf_op jit(solution)/shard_map/ppermute | solution.py:163
  324.7 121.6 %collective-permute-start.5 = (bf16[8,3,4096]{2,1,0:T(4,128)(2,1)S(1)}, bf16[8,3,4096]{2,1,0:T(4,128)(2,1)}, u32[]{:S(2)}, u32[]{:S(2)}) collective-permute-start(bf16[8,3,4096]{2,1,0:T(4,128)(2,1)S(1)} %gather_fusion.5), channel_id=1, source_target_pairs={{0,3},{1,2},{2,1},{3,0},{4,7},{5,6},{6,5},{7,4},{8,11},{9,10},{10,... | collective-permute-start | bytes 589832 | tf_op jit(solution)/shard_map/ppermute | solution.py:163
  336.0 10.7 %copy-start.18 = (s32[64]{0:T(128)S(1)}, s32[64]{0:T(128)}, u32[]{:S(2)}) copy-start(s32[64]{0:T(128)} %copy-done.17) | copy-start | bytes 772
  336.0 10.7 %copy-start.22 = (s32[64]{0:T(128)S(1)}, s32[64]{0:T(128)}, u32[]{:S(2)}) copy-start(s32[64]{0:T(128)} %param.34) | copy-start | bytes 772
  336.0 13.5 %copy-start.24 = (s32[64]{0:T(128)S(1)}, s32[64]{0:T(128)}, u32[]{:S(2)}) copy-start(s32[64]{0:T(128)} %copy-done.23) | copy-start | bytes 772
  336.0 13.5 %copy-start.25 = (s32[64]{0:T(128)S(1)}, s32[64]{0:T(128)}, u32[]{:S(2)}) copy-start(s32[64]{0:T(128)} %get-tuple-element.229) | copy-start | bytes 772
  336.0 13.6 %copy-start.5 = (bf16[16,3,4096]{2,1,0:T(4,128)(2,1)S(1)}, bf16[16,3,4096]{2,1,0:T(4,128)(2,1)}, u32[]{:S(2)}) copy-start(bf16[16,3,4096]{2,1,0:T(4,128)(2,1)} %copy-done.4) | copy-start | bytes 1179652
  336.0 13.6 %copy-start.10 = (bf16[16,8,4096]{2,1,0:T(8,128)(2,1)S(1)}, bf16[16,8,4096]{2,1,0:T(8,128)(2,1)}, u32[]{:S(2)}) copy-start(bf16[16,8,4096]{2,1,0:T(8,128)(2,1)} %param.28) | copy-start | bytes 3145732
  375.1 75.2 %collective-permute-start.6 = (bf16[8,3,4096]{2,1,0:T(4,128)(2,1)S(1)}, bf16[8,3,4096]{2,1,0:T(4,128)(2,1)}, u32[]{:S(2)}, u32[]{:S(2)}) collective-permute-start(bf16[8,3,4096]{2,1,0:T(4,128)(2,1)S(1)} %gather_fusion.8), channel_id=1, source_target_pairs={{0,1},{1,0},{2,3},{3,2},{4,5},{5,4},{6,7},{7,6},{8,9},{9,8},{10,11... | collective-permute-start | bytes 589832 | tf_op jit(solution)/shard_map/ppermute | solution.py:163
  375.2 78.4 %collective-permute-start.7 = (bf16[8,3,4096]{2,1,0:T(4,128)(2,1)S(1)}, bf16[8,3,4096]{2,1,0:T(4,128)(2,1)S(1)}, u32[]{:S(2)}, u32[]{:S(2)}) collective-permute-start(bf16[8,3,4096]{2,1,0:T(4,128)(2,1)S(1)} %gather_fusion.9), channel_id=1, source_target_pairs={{0,2},{1,3},{2,0},{3,1},{4,6},{5,7},{6,4},{7,5},{8,10},{9,11},{10,... | collective-permute-start | bytes 589832 | tf_op jit(solution)/shard_map/ppermute | solution.py:163
  442.4 15.1 %collective-permute-start.8 = (bf16[8,3,4096]{2,1,0:T(4,128)(2,1)S(1)}, bf16[8,3,4096]{2,1,0:T(4,128)(2,1)S(1)}, u32[]{:S(2)}, u32[]{:S(2)}) collective-permute-start(bf16[8,3,4096]{2,1,0:T(4,128)(2,1)S(1)} %gather_fusion.10), channel_id=1, source_target_pairs={{0,3},{1,2},{2,1},{3,0},{4,7},{5,6},{6,5},{7,4},{8,11},{9,10},{10,... | collective-permute-start | bytes 589832 | tf_op jit(solution)/shard_map/ppermute | solution.py:163
  475.2 9.8 %copy-start.2 = (bf16[3,64,64,256]{3,2,1,0:T(8,128)(2,1)S(1)}, bf16[3,64,64,256]{3,2,1,0:T(8,128)(2,1)}, u32[]{:S(2)}) copy-start(bf16[3,64,64,256]{3,2,1,0:T(8,128)(2,1)} %get-tuple-element.271) | copy-start | bytes 18874372
  496.8 47.3 %collective-permute-start = (bf16[1,64,64,256]{3,2,1,0:T(8,128)(2,1)}, bf16[1,64,64,256]{3,2,1,0:T(8,128)(2,1)S(1)}, u32[]{:S(2)}, u32[]{:S(2)}) collective-permute-start(bf16[1,64,64,256]{3,2,1,0:T(8,128)(2,1)} %constant_dynamic-slice_fusion.10), channel_id=1, source_target_pairs={{0,3},{1,2},{2,1},{3,0},{4,7},{5,6},{6,5},{7,4},{8,11},{9,10},{10,... | collective-permute-start | bytes 6291464 | tf_op jit(solution)/shard_map/while/body/ppermute | solution.py:201
  551.5 47.3 %collective-permute-start = (bf16[1,64,64,256]{3,2,1,0:T(8,128)(2,1)}, bf16[1,64,64,256]{3,2,1,0:T(8,128)(2,1)S(1)}, u32[]{:S(2)}, u32[]{:S(2)}) collective-permute-start(bf16[1,64,64,256]{3,2,1,0:T(8,128)(2,1)} %constant_dynamic-slice_fusion.10), channel_id=1, source_target_pairs={{0,3},{1,2},{2,1},{3,0},{4,7},{5,6},{6,5},{7,4},{8,11},{9,10},{10,... | collective-permute-start | bytes 6291464 | tf_op jit(solution)/shard_map/while/body/ppermute | solution.py:201
  606.3 47.5 %collective-permute-start = (bf16[1,64,64,256]{3,2,1,0:T(8,128)(2,1)}, bf16[1,64,64,256]{3,2,1,0:T(8,128)(2,1)S(1)}, u32[]{:S(2)}, u32[]{:S(2)}) collective-permute-start(bf16[1,64,64,256]{3,2,1,0:T(8,128)(2,1)} %constant_dynamic-slice_fusion.10), channel_id=1, source_target_pairs={{0,3},{1,2},{2,1},{3,0},{4,7},{5,6},{6,5},{7,4},{8,11},{9,10},{10,... | collective-permute-start | bytes 6291464 | tf_op jit(solution)/shard_map/while/body/ppermute | solution.py:201
  661.1 47.8 %collective-permute-start = (bf16[1,64,64,256]{3,2,1,0:T(8,128)(2,1)}, bf16[1,64,64,256]{3,2,1,0:T(8,128)(2,1)S(1)}, u32[]{:S(2)}, u32[]{:S(2)}) collective-permute-start(bf16[1,64,64,256]{3,2,1,0:T(8,128)(2,1)} %constant_dynamic-slice_fusion.10), channel_id=1, source_target_pairs={{0,3},{1,2},{2,1},{3,0},{4,7},{5,6},{6,5},{7,4},{8,11},{9,10},{10,... | collective-permute-start | bytes 6291464 | tf_op jit(solution)/shard_map/while/body/ppermute | solution.py:201
  716.3 47.8 %collective-permute-start = (bf16[1,64,64,256]{3,2,1,0:T(8,128)(2,1)}, bf16[1,64,64,256]{3,2,1,0:T(8,128)(2,1)S(1)}, u32[]{:S(2)}, u32[]{:S(2)}) collective-permute-start(bf16[1,64,64,256]{3,2,1,0:T(8,128)(2,1)} %constant_dynamic-slice_fusion.10), channel_id=1, source_target_pairs={{0,3},{1,2},{2,1},{3,0},{4,7},{5,6},{6,5},{7,4},{8,11},{9,10},{10,... | collective-permute-start | bytes 6291464 | tf_op jit(solution)/shard_map/while/body/ppermute | solution.py:201
Sparse Core Ops, SparseCore 0:
  317.3 79.6 reduce-scatter.1
